TPU v7x, 512 devices: a whole 4x4x16 slice. The times are simulated.
512 devices in a mesh: tm: 64 (over x, z), wafer: 8 (over y, core).
Axes of the slice: x: 4, y: 4, z: 16, core: 2. Of those that a mesh axis runs over, the one named last changes fastest.
Arguments:
- timestream: float32 [64, 64, 1024], P('tm', 'wafer'), may hold values from -6 to 6
- noise_weight: float32 [64, 64], P('tm', 'wafer'), may hold values from 0.3 to 5.4, as said below
- hit_slot: int32 [64, 64, 1024], P('tm', 'wafer'), may hold values from 0 to 3
- tile_pixel: int32 [64, 64, 1024], P('tm', 'wafer'), may hold values from 0 to 16368
- pol_angle: float32 [64, 64, 1024], P('tm', 'wafer'), may hold values from -3.140625 to 3.140625
- hit_tiles: int32 [64, 4], P('tm'), may hold values from 0 to 127, as said below
- sky_map: float32 [128, 3, 16384], P('tm'), may hold values from -6 to 6
- precond: float32 [128, 6, 16384], P('tm'), may hold values from -0.45 to 8, as said below
Outputs:
- new_map: float32 [128, 3, 16384], P('tm')
- new_residual: float32 [64, 64, 1024], P('tm', 'wafer')
Inputs may be any that keep to these rules, and one draw needn't show every extreme that they name: `hit_tiles`: the tiles of block c are distinct and lie among the 6 tiles (c - 1) * 2 to (c + 2) * 2 - 1, taken modulo 128; the first lies among the lower 2 of them, the second among the upper 2. `noise_weight`: Positive. `precond`: at every pixel each diagonal entry exceeds the sum of the magnitudes of the off-diagonal entries of its row. `tile_pixel`: the last 15 pixels of every tile are never hit.
All inputs are finite; a program needn't handle non-finite values.
Results may differ from a plain program's by a relative error of at most 0.0003.
Values sent between devices are 32-bit elements; how exact they have to be, the bound alone decides.
No kernel may reach another device: no remote copies, remote signals or barrier semaphores. Data moves between devices by JAX's collectives and lax.ppermute only.
A program may use at most 64 MiB of HBM per device.

v0:
```python
import functools

import jax
import jax.numpy as jnp
from jax import lax
from jax.sharding import Mesh
from jax.sharding import PartitionSpec as P

TM = ("tm_0", "tm_1")
WAFER = ("wafer_0", "wafer_1")
TM_WAFER = ("tm_0", "tm_1", "wafer_0", "wafer_1")


def with_halo(block, sides, width):
    for axis, dim in sides:
        count = lax.axis_size(axis)
        forward = [(i, i + 1) for i in range(count - 1)]
        forward.append((count - 1, 0))
        backward = [(target, source) for source, target in forward]
        low = lax.ppermute(
            lax.slice_in_dim(block, block.shape[dim] - width, None, axis=dim), axis, forward
        )
        high = lax.ppermute(lax.slice_in_dim(block, 0, width, axis=dim), axis, backward)
        block = jnp.concatenate([low, block, high], axis=dim)
    return block


def passed_along(value, axis, by):
    count = lax.axis_size(axis)
    return lax.ppermute(value, axis, [(i, (i + by) % count) for i in range(count)])


def in_blocks(value, dim, count):
    shape = value.shape
    parts = value.reshape(*shape[:dim], count, shape[dim] // count, *shape[dim + 1 :])
    return jnp.moveaxis(parts, dim, 0)


def sum_at_owner(value, axis, dim):
    count = lax.axis_size(axis)
    parts = lax.all_to_all(in_blocks(value, dim, count), axis, 0, 0, tiled=True)
    return jnp.sum(parts, axis=0)


def laid_out(parts, dim):
    shape = list(parts.shape[1:])
    shape[dim] *= parts.shape[0]
    return jnp.moveaxis(parts, 0, dim).reshape(shape)


def copy_for_each(value, axis):
    copies = jnp.broadcast_to(value, (lax.axis_size(axis), *value.shape))
    return lax.all_to_all(copies, axis, split_axis=0, concat_axis=0, tiled=True)


def collect(value, axis, dim):
    return laid_out(copy_for_each(value, axis), dim)


def by_axis(value, axes):
    return functools.reduce(lax.psum, axes, value)


def precondition(gradient, inverse):
    g_i = gradient[:, 0]
    g_q = gradient[:, 1]
    g_u = gradient[:, 2]
    out_i = inverse[:, 0] * g_i + inverse[:, 3] * g_q + inverse[:, 4] * g_u
    out_q = inverse[:, 3] * g_i + inverse[:, 1] * g_q + inverse[:, 5] * g_u
    out_u = inverse[:, 4] * g_i + inverse[:, 5] * g_q + inverse[:, 2] * g_u
    return jnp.stack([out_i, out_q, out_u], axis=1)


def rescan(window, local_ids, base_index, cos_two, sin_two):
    pixels = window.shape[2]
    hit_table = jnp.take(window, local_ids, axis=0).reshape(-1)
    first = jnp.take(hit_table, base_index)
    second = jnp.take(hit_table, base_index + pixels)
    third = jnp.take(hit_table, base_index + 2 * pixels)
    return first + cos_two * second + sin_two * third


def local(timestream, noise_weight, hit_slot, tile_pixel, pol_angle, hit_tiles, sky_map, precond):
    tiles_dev = sky_map.shape[0]
    pixels = sky_map.shape[2]
    hit_count = hit_tiles.shape[1]
    all_tiles = tiles_dev * lax.axis_size(TM)
    position = lax.axis_index(TM)
    local_ids = jnp.mod(hit_tiles[0] - (position - 1) * tiles_dev, all_tiles)
    base_index = hit_slot[0] * (3 * pixels) + tile_pixel[0]
    doubled = 2.0 * pol_angle[0]
    cos_two = jnp.cos(doubled)
    sin_two = jnp.sin(doubled)
    weights_col = noise_weight[0][:, None]
    window = with_halo(sky_map, ((TM, 0),), tiles_dev)
    resid = timestream[0] - rescan(window, local_ids, base_index, cos_two, sin_two)
    weighted = weights_col * resid
    flat_base = base_index.reshape(-1)
    all_index = jnp.concatenate([flat_base, flat_base + pixels, flat_base + 2 * pixels])
    all_terms = jnp.concatenate(
        [weighted.reshape(-1), (weighted * cos_two).reshape(-1), (weighted * sin_two).reshape(-1)]
    )
    partial_flat = jnp.zeros((hit_count * 3 * pixels,), jnp.float32).at[all_index].add(all_terms)
    partial_tiles = partial_flat.reshape(hit_count, 3, pixels)
    near_tiles = jnp.zeros((3 * tiles_dev, 3, pixels), jnp.float32).at[local_ids].add(partial_tiles)
    from_upper = passed_along(near_tiles[:tiles_dev], TM, -1)
    from_lower = passed_along(near_tiles[2 * tiles_dev :], TM, 1)
    owned_tiles = near_tiles[tiles_dev : 2 * tiles_dev] + from_upper + from_lower
    grad_share = sum_at_owner(owned_tiles, WAFER, 2)
    share_width = grad_share.shape[2]
    inverse_share = lax.dynamic_slice_in_dim(
        precond, lax.axis_index(WAFER) * share_width, share_width, 2
    )
    dir_share = precondition(grad_share, inverse_share)
    slope_part = jnp.sum(grad_share * dir_share)
    direction = collect(dir_share, WAFER, 2)
    slope = by_axis(slope_part, TM_WAFER)
    dir_window = with_halo(direction, ((TM, 0),), tiles_dev)
    rescanned = rescan(dir_window, local_ids, base_index, cos_two, sin_two)
    curve_part = jnp.sum(weights_col * rescanned * rescanned)
    curvature = by_axis(curve_part, TM_WAFER)
    step_size = slope / curvature
    new_map = sky_map + step_size * direction
    new_residual = (resid - step_size * rescanned)[None]
    return (new_map, new_residual)


def solution(mesh):
    split = Mesh(mesh.devices.reshape(4, 16, 4, 2), ("tm_0", "tm_1", "wafer_0", "wafer_1"))
    in_specs = (
        P(TM, WAFER, None),
        P(TM, WAFER),
        P(TM, WAFER, None),
        P(TM, WAFER, None),
        P(TM, WAFER, None),
        P(TM, None),
        P(TM, None, None),
        P(TM, None, None),
    )
    out_specs = (P(TM, None, None), P(TM, WAFER, None))
    return jax.shard_map(local, mesh=split, in_specs=in_specs, out_specs=out_specs, check_vma=False)
```

profile of v0, /device:TPU:1, one launch (start us, length us, event | category | flops | bytes accessed | tf_op | source)
XLA Modules:
  0.0 573.9 jit_solution(13763982510204243038)
XLA Ops:
  0.6 0.0 copy-start.4
  0.6 1.3 copy.23
  1.9 4.4 collective-permute-start
  6.3 11.7 %collective-permute-start.1 = (f32[2,3,16384]{2,1,0:T(4,128)S(1)}, f32[2,3,16384]{2,1,0:T(4,128)S(1)}, u32[]{:S(2)}, u32[]{:S(2)}) collective-permute-start(f32[2,3,16384]{2,1,0:T(4,128)S(1)} %copy.23), channel_id=1, source_target_pairs={{8,0},{16,8},{24,16},{32,24},{40,32},{48,40},{56,48},{64,56},{72,6... | collective-permute-start | bytes 1179656 | tf_op jit(solution)/shard_map/ppermute | solution.py:23
  18.0 0.8 fusion.11
  19.0 0.1 compare_select_fusion
  19.1 0.0 copy-done.4
  19.2 8.4 %collective-permute-done = f32[2,3,16384]{2,1,0:T(4,128)S(1)} collective-permute-done((f32[2,3,16384]{2,1,0:T(4,128)S(1)}, f32[2,3,16384]{2,1,0:T(4,128)S(1)}, u32[]{:S(2)}, u32[]{:S(2)}) %collective-permute-start) | collective-permute-done | bytes 393248 | tf_op jit(solution)/shard_map/ppermute | solution.py:20
  27.7 0.9 collective-permute-done.1
  28.6 0.4 pad_maximum_fusion
  28.9 1.2 gather_fusion
  30.1 0.3 broadcast_select_fusion.1
  30.4 0.6 reshape.253
  31.0 45.5 %gather_fusion.2 = f32[8192]{0:T(1024)S(1)} fusion(f32[196608]{0:T(1024)S(1)} %reshape.253, s32[8192]{0:T(1024)S(1)} %get-tuple-element.39), kind=kCustom, calls=%fused_computation.3.clone | custom fusion | bytes 98304 | tf_op jit(solution)/shard_map/jit(_take)/gather | solution.py:78
  76.6 45.5 %gather_fusion.3 = f32[8192]{0:T(1024)S(1)} fusion(f32[196608]{0:T(1024)S(1)} %reshape.253, s32[8192]{0:T(1024)S(1)} %get-tuple-element.38), kind=kCustom, calls=%fused_computation.4.clone | custom fusion | bytes 98304 | tf_op jit(solution)/shard_map/jit(_take)/gather | solution.py:79
  122.1 0.0 copy-start.1
  122.2 0.0 copy-start.2
  122.2 0.0 copy-start.3
  122.2 45.5 %gather_fusion.1 = f32[8192]{0:T(1024)S(1)} fusion(f32[196608]{0:T(1024)S(1)} %reshape.253, s32[8192]{0:T(1024)S(1)} %bitcast_clamp_fusion.2), kind=kCustom, calls=%fused_computation.1.clone | custom fusion | bytes 98304 | tf_op jit(solution)/shard_map/jit(_take)/gather | solution.py:77
  167.7 0.0 copy-done.1
  167.7 0.0 copy-done.2
  167.8 0.0 copy-done.3
  167.8 0.2 multiply_bitcast_fusion
  167.9 0.1 fusion.9
  168.2 128.6 %scatter_custom_fusion = f32[196608]{0:T(1024)S(1)} fusion(s32[24576]{0:T(1024)S(1)} %bitcast.123, f32[24576]{0:T(1024)S(1)} %pad_maximum_fusion.2, f32[]{:T(128)} %constant.34.clone.1), kind=kCustom, calls=%fused_computation.18 | custom fusion | flops 24576 | bytes 786436 | tf_op jit(solution)/shard_map/scatter-add | solution.py:103
  296.7 0.4 reshape.337
  297.1 0.2 broadcast_in_dim.29
  297.3 1.6 scatter_fusion
  298.9 0.2 fusion.24
  299.1 7.4 %collective-permute-start.2 = (f32[2,3,16384]{2,1,0:T(4,128)S(1)}, f32[2,3,16384]{2,1,0:T(4,128)S(1)}, u32[]{:S(2)}, u32[]{:S(2)}) collective-permute-start(f32[2,3,16384]{2,1,0:T(4,128)S(1)} %get-tuple-element.27), channel_id=1, source_target_pairs={{0,504},{8,0},{16,8},{24,16},{32,24},{40,32},{48,40},{56,48},{64,5... | collective-permute-start | bytes 1179656 | tf_op jit(solution)/shard_map/ppermute | solution.py:30
  306.6 1.9 collective-permute-start.3
  308.5 7.8 %collective-permute-done.2 = f32[2,3,16384]{2,1,0:T(4,128)S(1)} collective-permute-done((f32[2,3,16384]{2,1,0:T(4,128)S(1)}, f32[2,3,16384]{2,1,0:T(4,128)S(1)}, u32[]{:S(2)}, u32[]{:S(2)}) %collective-permute-start.2) | collective-permute-done | bytes 393248 | tf_op jit(solution)/shard_map/ppermute | solution.py:30
  316.3 7.2 %collective-permute-done.3 = f32[2,3,16384]{2,1,0:T(4,128)S(1)} collective-permute-done((f32[2,3,16384]{2,1,0:T(4,128)S(1)}, f32[2,3,16384]{2,1,0:T(4,128)S(1)}, u32[]{:S(2)}, u32[]{:S(2)}) %collective-permute-start.3) | collective-permute-done | bytes 393248 | tf_op jit(solution)/shard_map/ppermute | solution.py:30
  323.5 0.2 fusion
  323.6 0.3 reshape.383
  323.9 1.1 copy.27
  325.0 7.1 %all-to-all-start = ((f32[8,2,3,2048]{3,1,2,0:T(2,128)}), f32[8,2,3,2048]{3,1,2,0:T(2,128)S(1)}, u32[]{:S(2)}, u32[]{:S(2)}) async-start(f32[8,2,3,2048]{3,1,2,0:T(2,128)} %copy.27), calls=%async_computation | async-start | bytes 786432 | tf_op jit(solution)/shard_map/all_to_all | solution.py:41
  332.1 7.7 %all-to-all-done = f32[8,2,3,2048]{3,1,2,0:T(2,128)S(1)} async-done(((f32[8,2,3,2048]{3,1,2,0:T(2,128)}), f32[8,2,3,2048]{3,1,2,0:T(2,128)S(1)}, u32[]{:S(2)}, u32[]{:S(2)}) %all-to-all-start) | async-done | bytes 393248 | tf_op jit(solution)/shard_map/all_to_all | solution.py:41
  339.8 0.1 reduce_sum.27
  340.0 0.9 fusion.18
  340.8 0.7 multiply_reduce_fusion
  341.5 0.2 broadcast_in_dim.31
  341.7 11.7 %all_to_all.10 = f32[8,2,3,2048]{3,1,2,0:T(2,128)S(1)} all-to-all(f32[8,2,3,2048]{3,1,2,0:T(2,128)S(1)} %broadcast_in_dim.31), channel_id=1, replica_groups=mesh['tm_0'=4,'tm_1'=16,'wafer_0'=4,'wafer_1'=2] {'wafer_0','wafer_1'}, dimensions={0} | all-to-all | bytes 786432 | tf_op jit(solution)/shard_map/all_to_all | solution.py:53
  353.3 0.3 copy.29
  353.6 1.9 collective-permute-start.4
  355.5 6.9 %collective-permute-start.5 = (f32[2,3,16384]{2,1,0:T(4,128)S(1)}, f32[2,3,16384]{2,1,0:T(4,128)S(1)}, u32[]{:S(2)}, u32[]{:S(2)}) collective-permute-start(f32[2,3,16384]{2,1,0:T(4,128)S(1)} %copy.29), channel_id=1, source_target_pairs={{8,0},{16,8},{24,16},{32,24},{40,32},{48,40},{56,48},{64,56},{72,6... | collective-permute-start | bytes 1179656 | tf_op jit(solution)/shard_map/ppermute | solution.py:23
  362.4 9.0 %collective-permute-done.4 = f32[2,3,16384]{2,1,0:T(4,128)S(1)} collective-permute-done((f32[2,3,16384]{2,1,0:T(4,128)S(1)}, f32[2,3,16384]{2,1,0:T(4,128)S(1)}, u32[]{:S(2)}, u32[]{:S(2)}) %collective-permute-start.4) | collective-permute-done | bytes 393248 | tf_op jit(solution)/shard_map/ppermute | solution.py:20
  371.4 0.9 collective-permute-done.5
  372.3 0.4 pad_maximum_fusion.1
  372.7 1.2 gather_fusion.4
  373.9 1.3 broadcast_select_fusion
  375.2 1.8 reshape.260
  376.9 45.5 %gather_fusion.5 = f32[8192]{0:T(1024)S(1)} fusion(f32[196608]{0:T(1024)S(1)} %reshape.260, s32[8192]{0:T(1024)S(1)} %bitcast_clamp_fusion.2), kind=kCustom, calls=%fused_computation.5.clone | custom fusion | bytes 98304 | tf_op jit(solution)/shard_map/jit(_take)/gather | solution.py:77
  422.5 45.5 %gather_fusion.6 = f32[8192]{0:T(1024)S(1)} fusion(f32[196608]{0:T(1024)S(1)} %reshape.260, s32[8192]{0:T(1024)S(1)} %get-tuple-element.39), kind=kCustom, calls=%fused_computation.6.clone | custom fusion | bytes 98304 | tf_op jit(solution)/shard_map/jit(_take)/gather | solution.py:78
  468.0 0.0 copy-start
  468.0 45.5 %gather_fusion.7 = f32[8192]{0:T(1024)S(1)} fusion(f32[196608]{0:T(1024)S(1)} %reshape.260, s32[8192]{0:T(1024)S(1)} %get-tuple-element.38), kind=kCustom, calls=%fused_computation.7.clone | custom fusion | bytes 98304 | tf_op jit(solution)/shard_map/jit(_take)/gather | solution.py:79
  513.6 0.8 fusion.3
  514.4 6.6 %all-reduce.2 = (f32[]{:T(128)}, f32[]{:T(128)}) all-reduce(f32[]{:T(128)} %get-tuple-element.16, f32[]{:T(128)} %get-tuple-element.14), channel_id=1, replica_groups=mesh['tm_0'=4,'tm_1'=16,'wafer_0'=4,'wafer_1'=2] {'tm_0'}, use_global_device_ids=true, to_apply=%region_4.7 | all-reduce | flops 2 | bytes 16 | tf_op jit(solution)/shard_map/psum | solution.py:61
  521.0 26.6 %all-reduce = (f32[]{:T(128)}, f32[]{:T(128)}) all-reduce(f32[]{:T(128)} %get-tuple-element.10, f32[]{:T(128)} %get-tuple-element.11), channel_id=1, replica_groups=mesh['tm_0'=4,'tm_1'=16,'wafer_0'=4,'wafer_1'=2] {'tm_1'}, use_global_device_ids=true, to_apply=%region_5.8 | all-reduce | flops 2 | bytes 16 | tf_op jit(solution)/shard_map/psum | solution.py:61
  547.6 7.7 %all-reduce.1 = (f32[]{:T(128)}, f32[]{:T(128)}) all-reduce(f32[]{:T(128)} %get-tuple-element.6, f32[]{:T(128)} %get-tuple-element.7), channel_id=1, replica_groups=mesh['tm_0'=4,'tm_1'=16,'wafer_0'=4,'wafer_1'=2] {'wafer_0'}, use_global_device_ids=true, to_apply=%region_6.9 | all-reduce | flops 2 | bytes 16 | tf_op jit(solution)/shard_map/psum | solution.py:61
  555.3 15.7 %all-reduce.3 = (f32[]{:T(128)}, f32[]{:T(128)}) all-reduce(f32[]{:T(128)} %get-tuple-element.8, f32[]{:T(128)} %get-tuple-element.9), channel_id=1, replica_groups=mesh['tm_0'=4,'tm_1'=16,'wafer_0'=4,'wafer_1'=2] {'wafer_1'}, use_global_device_ids=true, to_apply=%region_7.10 | all-reduce | flops 2 | bytes 16 | tf_op jit(solution)/shard_map/psum | solution.py:61
  572.3 0.0 copy-done
  572.3 1.0 multiply_add_fusion
  573.3 0.6 subtract_bitcast_fusion
  (24 shorter events, 0.4 us)
Async XLA Ops:
  0.6 18.5 %copy-start.4 = (s32[1,4]{1,0:T(1,128)S(1)}, s32[1,4]{1,0:T(1,128)}, u32[]{:S(2)}) copy-start(s32[1,4]{1,0:T(1,128)} %param.17) | copy-start | bytes 52
  1.9 25.8 %collective-permute-start = (f32[2,3,16384]{2,1,0:T(4,128)S(1)}, f32[2,3,16384]{2,1,0:T(4,128)S(1)}, u32[]{:S(2)}, u32[]{:S(2)}) collective-permute-start(f32[2,3,16384]{2,1,0:T(4,128)S(1)} %copy.23), channel_id=1, source_target_pairs={{0,8},{8,16},{16,24},{24,32},{32,40},{40,48},{48,56},{56,64},{64,7... | collective-permute-start | bytes 1179656 | tf_op jit(solution)/shard_map/ppermute | solution.py:20
  6.3 22.3 %collective-permute-start.1 = (f32[2,3,16384]{2,1,0:T(4,128)S(1)}, f32[2,3,16384]{2,1,0:T(4,128)S(1)}, u32[]{:S(2)}, u32[]{:S(2)}) collective-permute-start(f32[2,3,16384]{2,1,0:T(4,128)S(1)} %copy.23), channel_id=1, source_target_pairs={{8,0},{16,8},{24,16},{32,24},{40,32},{48,40},{56,48},{64,56},{72,6... | collective-permute-start | bytes 1179656 | tf_op jit(solution)/shard_map/ppermute | solution.py:23
  122.1 45.6 %copy-start.1 = (f32[1,8,1024]{2,1,0:T(8,128)S(1)}, f32[1,8,1024]{2,1,0:T(8,128)}, u32[]{:S(2)}) copy-start(f32[1,8,1024]{2,1,0:T(8,128)} %param.16) | copy-start | bytes 98308
  122.2 45.6 %copy-start.2 = (f32[1,8,1024]{2,1,0:T(8,128)S(1)}, f32[1,8,1024]{2,1,0:T(8,128)}, u32[]{:S(2)}) copy-start(f32[1,8,1024]{2,1,0:T(8,128)} %param.12) | copy-start | bytes 98308
  122.2 45.6 %copy-start.3 = (f32[1,8]{1,0:T(1,128)S(1)}, f32[1,8]{1,0:T(1,128)}, u32[]{:S(2)}) copy-start(f32[1,8]{1,0:T(1,128)} %param.13) | copy-start | bytes 100
  299.1 17.2 %collective-permute-start.2 = (f32[2,3,16384]{2,1,0:T(4,128)S(1)}, f32[2,3,16384]{2,1,0:T(4,128)S(1)}, u32[]{:S(2)}, u32[]{:S(2)}) collective-permute-start(f32[2,3,16384]{2,1,0:T(4,128)S(1)} %get-tuple-element.27), channel_id=1, source_target_pairs={{0,504},{8,0},{16,8},{24,16},{32,24},{40,32},{48,40},{56,48},{64,5... | collective-permute-start | bytes 1179656 | tf_op jit(solution)/shard_map/ppermute | solution.py:30
  306.6 16.9 %collective-permute-start.3 = (f32[2,3,16384]{2,1,0:T(4,128)S(1)}, f32[2,3,16384]{2,1,0:T(4,128)S(1)}, u32[]{:S(2)}, u32[]{:S(2)}) collective-permute-start(f32[2,3,16384]{2,1,0:T(4,128)S(1)} %get-tuple-element.28), channel_id=1, source_target_pairs={{0,8},{8,16},{16,24},{24,32},{32,40},{40,48},{48,56},{56,64},{64,7... | collective-permute-start | bytes 1179656 | tf_op jit(solution)/shard_map/ppermute | solution.py:30
  325.0 14.8 %all-to-all-start = ((f32[8,2,3,2048]{3,1,2,0:T(2,128)}), f32[8,2,3,2048]{3,1,2,0:T(2,128)S(1)}, u32[]{:S(2)}, u32[]{:S(2)}) async-start(f32[8,2,3,2048]{3,1,2,0:T(2,128)} %copy.27), calls=%async_computation | async-start | bytes 786432 | tf_op jit(solution)/shard_map/all_to_all | solution.py:41
  353.6 17.8 %collective-permute-start.4 = (f32[2,3,16384]{2,1,0:T(4,128)S(1)}, f32[2,3,16384]{2,1,0:T(4,128)S(1)}, u32[]{:S(2)}, u32[]{:S(2)}) collective-permute-start(f32[2,3,16384]{2,1,0:T(4,128)S(1)} %copy.29), channel_id=1, source_target_pairs={{0,8},{8,16},{16,24},{24,32},{32,40},{40,48},{48,56},{56,64},{64,7... | collective-permute-start | bytes 1179656 | tf_op jit(solution)/shard_map/ppermute | solution.py:20
  355.5 16.8 %collective-permute-start.5 = (f32[2,3,16384]{2,1,0:T(4,128)S(1)}, f32[2,3,16384]{2,1,0:T(4,128)S(1)}, u32[]{:S(2)}, u32[]{:S(2)}) collective-permute-start(f32[2,3,16384]{2,1,0:T(4,128)S(1)} %copy.29), channel_id=1, source_target_pairs={{8,0},{16,8},{24,16},{32,24},{40,32},{48,40},{56,48},{64,56},{72,6... | collective-permute-start | bytes 1179656 | tf_op jit(solution)/shard_map/ppermute | solution.py:23
  468.0 104.3 %copy-start = (f32[2,3,16384]{2,0,1:T(2,128)S(1)}, f32[2,3,16384]{2,0,1:T(2,128)}, u32[]{:S(2)}) copy-start(f32[2,3,16384]{2,0,1:T(2,128)} %param.18) | copy-start | bytes 1179652
where the time goes:
time: 575 us; the launch traced here: 574 us
  local copies, waits for them, and re-layouts  282 us (49%)
  other arithmetic  138 us (24%)
  blocking collectives  68.2 us (12%)
  waiting for transfers between devices  41.9 us (7%)
  starting transfers between devices  41.3 us (7%)
    scatter-add x1, other arithmetic, local(): jnp.zeros((hit_count * 3 * pixels,), jnp.float32).at[all_index]  129 us
    gather x4, local copies, waits for them, and re-layouts, rescan(): first = jnp.take(hit_table, base_index)  91.1 us
    gather x4, local copies, waits for them, and re-layouts, rescan(): third = jnp.take(hit_table, base_index + 2 * pixels)  91.1 us
    gather x4, local copies, waits for them, and re-layouts, rescan(): second = jnp.take(hit_table, base_index + pixels)  91.1 us
    psum x4, blocking collectives, by_axis(): return functools.reduce(lax.psum, axes, value)  56.6 us
    ppermute x2, starting transfers between devices, with_halo(): lax.ppermute(lax.slice_in_dim(block, 0, width, axis=dim), axis, backward)  18.6 us
    ppermute x2, waiting for transfers between devices, with_halo(): lax.ppermute(lax.slice_in_dim(block, block.shape[dim] - width, None, axis...  17.5 us
    ppermute x2, waiting for transfers between devices, passed_along(): lax.ppermute(value, axis, [(i, (i + by) % count) for i in range(count)])  15 us
  transfers between devices with their start and end apart: 7, of which 7 were waited for; matrix products, arithmetic and copies ran while one was open for 0% of the time, Pallas kernels for 0%

commit v1 on v0

--- a/solution.py
+++ b/solution.py
@@ -3,6 +3,8 @@
 import jax
 import jax.numpy as jnp
 from jax import lax
+from jax.experimental import pallas as pl
+from jax.experimental.pallas import tpu as pltpu
 from jax.sharding import Mesh
 from jax.sharding import PartitionSpec as P
 
@@ -71,37 +73,153 @@
     return jnp.stack([out_i, out_q, out_u], axis=1)
 
 
-def rescan(window, local_ids, base_index, cos_two, sin_two):
-    pixels = window.shape[2]
-    hit_table = jnp.take(window, local_ids, axis=0).reshape(-1)
-    first = jnp.take(hit_table, base_index)
-    second = jnp.take(hit_table, base_index + pixels)
-    third = jnp.take(hit_table, base_index + 2 * pixels)
-    return first + cos_two * second + sin_two * third
+SIDE = 128
+
+
+def split3(value):
+    hi = value.astype(jnp.bfloat16)
+    rest = value - hi.astype(jnp.float32)
+    mid = rest.astype(jnp.bfloat16)
+    lo = (rest - mid.astype(jnp.float32)).astype(jnp.bfloat16)
+    return hi, mid, lo
+
+
+def row_onehot(slot, pix, rows):
+    row = slot * SIDE + jnp.right_shift(pix, 7)
+    ids = lax.broadcasted_iota(jnp.int32, (rows, pix.shape[1]), 0)
+    return (ids == row).astype(jnp.bfloat16)
+
+
+def col_mask(pix):
+    col = jnp.bitwise_and(pix, SIDE - 1)
+    ids = lax.broadcasted_iota(jnp.int32, (SIDE, pix.shape[1]), 0)
+    return ids == col
+
+
+def sample_map(pieces, at, mask, comp):
+    picked = None
+    for piece in pieces:
+        part = jnp.dot(piece[comp], at, preferred_element_type=jnp.float32)
+        picked = part if picked is None else picked + part
+    return jnp.sum(jnp.where(mask, picked, 0.0), axis=0, keepdims=True)
+
+
+def bin_kernel(w_ref, mt_ref, slot_ref, pix_ref, cos_ref, sin_ref, ts_ref, resid_ref, g_ref,
+               hi_ref, mid_ref, lo_ref, acc_ref):
+    hi, mid, lo = split3(mt_ref[...])
+    hi_ref[...] = hi
+    mid_ref[...] = mid
+    lo_ref[...] = lo
+    acc_ref[...] = jnp.zeros(acc_ref.shape, jnp.float32)
+    rows = mt_ref.shape[2]
+    nt = (((1,), (1,)), ((), ()))
+
+    def body(d, carry):
+        slot = slot_ref[pl.ds(d, 1), :]
+        pix = pix_ref[pl.ds(d, 1), :]
+        cs = cos_ref[pl.ds(d, 1), :]
+        sn = sin_ref[pl.ds(d, 1), :]
+        at = row_onehot(slot, pix, rows)
+        mask = col_mask(pix)
+        pieces = (hi_ref, mid_ref, lo_ref)
+        v0 = sample_map(pieces, at, mask, 0)
+        v1 = sample_map(pieces, at, mask, 1)
+        v2 = sample_map(pieces, at, mask, 2)
+        resid = ts_ref[pl.ds(d, 1), :] - (v0 + cs * v1 + sn * v2)
+        resid_ref[pl.ds(d, 1), :] = resid
+        weighted = w_ref[d] * resid
+        for comp, term in ((0, weighted), (1, weighted * cs), (2, weighted * sn)):
+            dt = jnp.where(mask, term, 0.0)
+            total = None
+            for piece in split3(dt):
+                part = lax.dot_general(at, piece, nt, preferred_element_type=jnp.float32)
+                total = part if total is None else total + part
+            acc_ref[comp] += total
+        return carry
+
+    lax.fori_loop(0, slot_ref.shape[0], body, 0)
+    for s in range(g_ref.shape[0]):
+        for comp in range(3):
+            g_ref[s, comp] = acc_ref[comp, s * SIDE:(s + 1) * SIDE, :]
+
+
+def scan_kernel(mt_ref, slot_ref, pix_ref, cos_ref, sin_ref, out_ref, hi_ref, mid_ref, lo_ref):
+    hi, mid, lo = split3(mt_ref[...])
+    hi_ref[...] = hi
+    mid_ref[...] = mid
+    lo_ref[...] = lo
+    rows = mt_ref.shape[2]
+
+    def body(d, carry):
+        slot = slot_ref[pl.ds(d, 1), :]
+        pix = pix_ref[pl.ds(d, 1), :]
+        at = row_onehot(slot, pix, rows)
+        mask = col_mask(pix)
+        pieces = (hi_ref, mid_ref, lo_ref)
+        v0 = sample_map(pieces, at, mask, 0)
+        v1 = sample_map(pieces, at, mask, 1)
+        v2 = sample_map(pieces, at, mask, 2)
+        out_ref[pl.ds(d, 1), :] = v0 + cos_ref[pl.ds(d, 1), :] * v1 + sin_ref[pl.ds(d, 1), :] * v2
+        return carry
+
+    lax.fori_loop(0, slot_ref.shape[0], body, 0)
+
+
+def transposed_window(window, local_ids):
+    hits = jnp.take(window, local_ids, axis=0)
+    count = hits.shape[0]
+    grid = hits.reshape(count, 3, SIDE, SIDE)
+    return jnp.transpose(grid, (1, 3, 0, 2)).reshape(3, SIDE, count * SIDE)
+
+
+VMEM = pltpu.MemorySpace.VMEM
+
+
+def bin_call(weights, mt, slot, pix, cos_two, sin_two, ts):
+    dets, samp = slot.shape
+    hits = mt.shape[2] // SIDE
+    smem = pl.BlockSpec(memory_space=pltpu.SMEM)
+    vmem = pl.BlockSpec(memory_space=VMEM)
+    return pl.pallas_call(
+        bin_kernel,
+        out_shape=(
+            jax.ShapeDtypeStruct((dets, samp), jnp.float32),
+            jax.ShapeDtypeStruct((hits, 3, SIDE, SIDE), jnp.float32),
+        ),
+        in_specs=[smem] + [vmem] * 6,
+        out_specs=(vmem, vmem),
+        scratch_shapes=[pltpu.VMEM(mt.shape, jnp.bfloat16)] * 3
+        + [pltpu.VMEM((3, hits * SIDE, SIDE), jnp.float32)],
+    )(weights, mt, slot, pix, cos_two, sin_two, ts)
+
+
+def scan_call(mt, slot, pix, cos_two, sin_two):
+    vmem = pl.BlockSpec(memory_space=VMEM)
+    return pl.pallas_call(
+        scan_kernel,
+        out_shape=jax.ShapeDtypeStruct(slot.shape, jnp.float32),
+        in_specs=[vmem] * 5,
+        out_specs=vmem,
+        scratch_shapes=[pltpu.VMEM(mt.shape, jnp.bfloat16)] * 3,
+    )(mt, slot, pix, cos_two, sin_two)
 
 
 def local(timestream, noise_weight, hit_slot, tile_pixel, pol_angle, hit_tiles, sky_map, precond):
     tiles_dev = sky_map.shape[0]
     pixels = sky_map.shape[2]
-    hit_count = hit_tiles.shape[1]
     all_tiles = tiles_dev * lax.axis_size(TM)
     position = lax.axis_index(TM)
     local_ids = jnp.mod(hit_tiles[0] - (position - 1) * tiles_dev, all_tiles)
-    base_index = hit_slot[0] * (3 * pixels) + tile_pixel[0]
     doubled = 2.0 * pol_angle[0]
     cos_two = jnp.cos(doubled)
     sin_two = jnp.sin(doubled)
-    weights_col = noise_weight[0][:, None]
+    weights = noise_weight[0]
+    slot = hit_slot[0]
+    pix = tile_pixel[0]
     window = with_halo(sky_map, ((TM, 0),), tiles_dev)
-    resid = timestream[0] - rescan(window, local_ids, base_index, cos_two, sin_two)
-    weighted = weights_col * resid
-    flat_base = base_index.reshape(-1)
-    all_index = jnp.concatenate([flat_base, flat_base + pixels, flat_base + 2 * pixels])
-    all_terms = jnp.concatenate(
-        [weighted.reshape(-1), (weighted * cos_two).reshape(-1), (weighted * sin_two).reshape(-1)]
-    )
-    partial_flat = jnp.zeros((hit_count * 3 * pixels,), jnp.float32).at[all_index].add(all_terms)
-    partial_tiles = partial_flat.reshape(hit_count, 3, pixels)
+    mt = transposed_window(window, local_ids)
+    resid, binned = bin_call(weights, mt, slot, pix, cos_two, sin_two, timestream[0])
+    partial_tiles = binned.reshape(binned.shape[0], 3, pixels)
     near_tiles = jnp.zeros((3 * tiles_dev, 3, pixels), jnp.float32).at[local_ids].add(partial_tiles)
     from_upper = passed_along(near_tiles[:tiles_dev], TM, -1)
     from_lower = passed_along(near_tiles[2 * tiles_dev :], TM, 1)
@@ -114,12 +232,12 @@
     dir_share = precondition(grad_share, inverse_share)
     slope_part = jnp.sum(grad_share * dir_share)
     direction = collect(dir_share, WAFER, 2)
-    slope = by_axis(slope_part, TM_WAFER)
     dir_window = with_halo(direction, ((TM, 0),), tiles_dev)
-    rescanned = rescan(dir_window, local_ids, base_index, cos_two, sin_two)
-    curve_part = jnp.sum(weights_col * rescanned * rescanned)
-    curvature = by_axis(curve_part, TM_WAFER)
-    step_size = slope / curvature
+    dir_mt = transposed_window(dir_window, local_ids)
+    rescanned = scan_call(dir_mt, slot, pix, cos_two, sin_two)
+    curve_part = jnp.sum(weights[:, None] * rescanned * rescanned)
+    totals = lax.psum(jnp.stack([slope_part, curve_part]), TM_WAFER)
+    step_size = totals[0] / totals[1]
     new_map = sky_map + step_size * direction
     new_residual = (resid - step_size * rescanned)[None]
     return (new_map, new_residual)

time: 575 us -> 275 us (0.48)
  local copies, waits for them, and re-layouts: 282 us -> 12.1 us
  other arithmetic: 138 us -> 12.8 us
  Pallas kernels: 0 us -> 50.5 us
  blocking collectives: 68.2 us -> 115 us
    gather x14 -> x2, local copies, waits for them, and re-layouts: 276 us -> 2.35 us  [transposed_window(): hits = jnp.take(window, local_ids, axis=0)]
    scatter-add x1 -> x0, other arithmetic: 129 us -> none  [local(): jnp.zeros((hit_count * 3 * pixels,), jnp.float32).at[all_index]]
    pallas_call x0 -> x2, Pallas kernels: none -> 50.5 us  [the longest x1 36.2 us: bin_call(): pl.pallas_call(bin_kernel, out_shape=(jax.ShapeDtypeStruct((dets, samp),...]
    psum x4 -> x1, blocking collectives: 56.6 us -> 103 us  [local(): totals = lax.psum(jnp.stack([slope_part, curve_part]), TM_WAFER)]
  transfers between devices with their start and end apart: 7 -> 7, of which waited for: 7 -> 7; matrix products, arithmetic and copies ran while one was open for 0% -> 1% of each run, Pallas kernels for 0% -> 0%
where the time goes in v1:
time: 275 us; the launch traced here: 274 us
  blocking collectives  115 us (42%)
  Pallas kernels  50.5 us (18%)
  starting transfers between devices  41.3 us (15%)
  waiting for transfers between devices  40.3 us (15%)
  other arithmetic  12.8 us (5%)
  local copies, waits for them, and re-layouts  12.1 us (4%)
    psum x1, blocking collectives, local(): totals = lax.psum(jnp.stack([slope_part, curve_part]), TM_WAFER)  103 us
    pallas_call x1, Pallas kernels, bin_call(): pl.pallas_call(bin_kernel, out_shape=(jax.ShapeDtypeStruct((dets, samp),...  36.2 us
    ppermute x2, starting transfers between devices, with_halo(): lax.ppermute(lax.slice_in_dim(block, 0, width, axis=dim), axis, backward)  18.6 us
    ppermute x2, waiting for transfers between devices, with_halo(): lax.ppermute(lax.slice_in_dim(block, block.shape[dim] - width, None, axis...  15.8 us
    ppermute x2, waiting for transfers between devices, passed_along(): lax.ppermute(value, axis, [(i, (i + by) % count) for i in range(count)])  15 us
    pallas_call x1, Pallas kernels, scan_call(): pl.pallas_call(scan_kernel, out_shape=jax.ShapeDtypeStruct(slot.shape, jn...  14.3 us
    all_to_all x1, blocking collectives, copy_for_each(): return lax.all_to_all(copies, axis, split_axis=0, concat_axis=0, tiled=True)  11.7 us
    ppermute x2, starting transfers between devices, passed_along(): lax.ppermute(value, axis, [(i, (i + by) % count) for i in range(count)])  9.35 us
  transfers between devices with their start and end apart: 7, of which 7 were waited for; matrix products, arithmetic and copies ran while one was open for 1% of the time, Pallas kernels for 0%

profile of v1, /device:TPU:1, one launch (start us, length us, event | category | flops | bytes accessed | tf_op | source)
XLA Modules:
  0.0 274.2 jit_solution(11348776889893631331)
XLA Ops:
  0.6 1.3 copy.34
  1.9 4.4 %collective-permute-start = (f32[2,3,16384]{2,1,0:T(4,128)S(1)}, f32[2,3,16384]{2,1,0:T(4,128)S(1)}, u32[]{:S(2)}, u32[]{:S(2)}) collective-permute-start(f32[2,3,16384]{2,1,0:T(4,128)S(1)} %copy.34), channel_id=1, source_target_pairs={{0,8},{8,16},{16,24},{24,32},{32,40},{40,48},{48,56},{56,64},{64,7... | collective-permute-start | bytes 1179656 | tf_op jit(solution)/shard_map/ppermute | solution.py:22
  6.3 11.7 %collective-permute-start.1 = (f32[2,3,16384]{2,1,0:T(4,128)S(1)}, f32[2,3,16384]{2,1,0:T(4,128)S(1)}, u32[]{:S(2)}, u32[]{:S(2)}) collective-permute-start(f32[2,3,16384]{2,1,0:T(4,128)S(1)} %copy.34), channel_id=1, source_target_pairs={{8,0},{16,8},{24,16},{32,24},{40,32},{48,40},{56,48},{64,56},{72,6... | collective-permute-start | bytes 1179656 | tf_op jit(solution)/shard_map/ppermute | solution.py:25
  18.0 0.7 compare_and_fusion
  18.7 0.7 fusion.9
  19.3 1.5 sine_bitcast_fusion
  20.8 6.8 %collective-permute-done = f32[2,3,16384]{2,1,0:T(4,128)S(1)} collective-permute-done((f32[2,3,16384]{2,1,0:T(4,128)S(1)}, f32[2,3,16384]{2,1,0:T(4,128)S(1)}, u32[]{:S(2)}, u32[]{:S(2)}) %collective-permute-start) | collective-permute-done | bytes 393248 | tf_op jit(solution)/shard_map/ppermute | solution.py:22
  27.7 0.9 collective-permute-done.1
  28.6 0.4 pad_maximum_fusion
  28.9 1.2 gather_fusion
  30.1 0.3 broadcast_select_fusion.1
  30.4 0.6 reshape.129
  31.0 0.3 copy.38
  31.3 1.2 reshape.93.mt_ref
  32.5 36.2 %shard_map.95 = (f32[8,1024]{1,0:T(8,128)}, f32[4,3,128,128]{3,2,1,0:T(8,128)}) custom-call(f32[8]{0:T(128)} %bitcast.42, f32[3,128,512]{2,1,0:T(8,128)} %reshape.93.mt_ref, s32[8,1024]{1,0:T(8,128)} %bitcast.37, s32[8,1024]{1,0:T(8,128)} %bitcast.39, f32[8,1024]{1,0:T(8,128)} %get-tuple-element.19.cos_ref, f32[8,1024]{1,0:T(8,128)} %get-tuple-element.18.sin_ref, ...), custom_call_target="tpu_custom_call" | custom-call | tf_op jit(solution)/shard_map/pallas_call | solution.py:183
  68.8 1.5 reshape.130
  70.2 0.2 broadcast_in_dim.19
  70.5 1.6 scatter_fusion
  72.1 0.2 fusion.10
  72.3 7.4 %collective-permute-start.2 = (f32[2,3,16384]{2,1,0:T(4,128)S(1)}, f32[2,3,16384]{2,1,0:T(4,128)S(1)}, u32[]{:S(2)}, u32[]{:S(2)}) collective-permute-start(f32[2,3,16384]{2,1,0:T(4,128)S(1)} %get-tuple-element.13), channel_id=1, source_target_pairs={{0,504},{8,0},{16,8},{24,16},{32,24},{40,32},{48,40},{56,48},{64,5... | collective-permute-start | bytes 1179656 | tf_op jit(solution)/shard_map/ppermute | solution.py:32
  79.7 1.9 collective-permute-start.3
  81.6 7.8 %collective-permute-done.2 = f32[2,3,16384]{2,1,0:T(4,128)S(1)} collective-permute-done((f32[2,3,16384]{2,1,0:T(4,128)S(1)}, f32[2,3,16384]{2,1,0:T(4,128)S(1)}, u32[]{:S(2)}, u32[]{:S(2)}) %collective-permute-start.2) | collective-permute-done | bytes 393248 | tf_op jit(solution)/shard_map/ppermute | solution.py:32
  89.4 7.2 %collective-permute-done.3 = f32[2,3,16384]{2,1,0:T(4,128)S(1)} collective-permute-done((f32[2,3,16384]{2,1,0:T(4,128)S(1)}, f32[2,3,16384]{2,1,0:T(4,128)S(1)}, u32[]{:S(2)}, u32[]{:S(2)}) %collective-permute-start.3) | collective-permute-done | bytes 393248 | tf_op jit(solution)/shard_map/ppermute | solution.py:32
  96.6 0.2 fusion
  96.8 0.3 reshape.131
  97.1 1.1 copy.42
  98.1 7.1 %all-to-all-start = ((f32[8,2,3,2048]{3,1,2,0:T(2,128)}), f32[8,2,3,2048]{3,1,2,0:T(2,128)S(1)}, u32[]{:S(2)}, u32[]{:S(2)}) async-start(f32[8,2,3,2048]{3,1,2,0:T(2,128)} %copy.42), calls=%async_computation | async-start | bytes 786432 | tf_op jit(solution)/shard_map/all_to_all | solution.py:43
  105.2 7.7 %all-to-all-done = f32[8,2,3,2048]{3,1,2,0:T(2,128)S(1)} async-done(((f32[8,2,3,2048]{3,1,2,0:T(2,128)}), f32[8,2,3,2048]{3,1,2,0:T(2,128)S(1)}, u32[]{:S(2)}, u32[]{:S(2)}) %all-to-all-start) | async-done | bytes 393248 | tf_op jit(solution)/shard_map/all_to_all | solution.py:43
  112.9 0.1 reduce_sum.27
  113.1 0.9 fusion.6
  113.9 0.7 multiply_reduce_fusion
  114.6 0.2 broadcast_in_dim.20
  114.8 11.7 %all_to_all.10 = f32[8,2,3,2048]{3,1,2,0:T(2,128)S(1)} all-to-all(f32[8,2,3,2048]{3,1,2,0:T(2,128)S(1)} %broadcast_in_dim.20), channel_id=1, replica_groups=mesh['tm_0'=4,'tm_1'=16,'wafer_0'=4,'wafer_1'=2] {'wafer_0','wafer_1'}, dimensions={0} | all-to-all | bytes 786432 | tf_op jit(solution)/shard_map/all_to_all | solution.py:55
  126.5 0.3 copy.44
  126.7 1.9 collective-permute-start.4
  128.7 6.9 %collective-permute-start.5 = (f32[2,3,16384]{2,1,0:T(4,128)S(1)}, f32[2,3,16384]{2,1,0:T(4,128)S(1)}, u32[]{:S(2)}, u32[]{:S(2)}) collective-permute-start(f32[2,3,16384]{2,1,0:T(4,128)S(1)} %copy.44), channel_id=1, source_target_pairs={{8,0},{16,8},{24,16},{32,24},{40,32},{48,40},{56,48},{64,56},{72,6... | collective-permute-start | bytes 1179656 | tf_op jit(solution)/shard_map/ppermute | solution.py:25
  135.5 9.0 %collective-permute-done.4 = f32[2,3,16384]{2,1,0:T(4,128)S(1)} collective-permute-done((f32[2,3,16384]{2,1,0:T(4,128)S(1)}, f32[2,3,16384]{2,1,0:T(4,128)S(1)}, u32[]{:S(2)}, u32[]{:S(2)}) %collective-permute-start.4) | collective-permute-done | bytes 393248 | tf_op jit(solution)/shard_map/ppermute | solution.py:22
  144.6 0.9 collective-permute-done.5
  145.5 0.4 pad_maximum_fusion.1
  145.8 1.2 gather_fusion.1
  147.0 0.3 broadcast_select_fusion
  147.3 0.6 reshape.132
  147.9 0.3 copy.48
  148.2 0.0 copy-start.2
  148.2 0.0 copy-start
  148.3 0.0 copy-start.1
  148.3 1.2 reshape.98.mt_ref
  149.5 14.3 %shard_map.96 = f32[8,1024]{1,0:T(8,128)} custom-call(f32[3,128,512]{2,1,0:T(8,128)} %reshape.98.mt_ref, s32[8,1024]{1,0:T(8,128)} %bitcast.38, s32[8,1024]{1,0:T(8,128)} %bitcast.40, f32[8,1024]{1,0:T(8,128)} %get-tuple-element.19.cos_ref, f32[8,1024]{1,0:T(8,128)} %get-tuple-element.18.sin_ref), custom_call_target="tpu_custom_call" | custom-call | tf_op jit(solution)/shard_map/pallas_call | solution.py:198
  163.7 0.0 copy-done.2
  163.7 1.4 fusion.1
  165.2 1.4 pad_maximum_fusion.3
  166.5 103.4 %psum.7 = f32[2]{0:T(128)S(1)} all-reduce(f32[2]{0:T(128)S(1)} %pad_maximum_fusion.3), channel_id=1, replica_groups=mesh['tm_0'=4,'tm_1'=16,'wafer_0'=4,'wafer_1'=2] {'tm_0','tm_1','wafer_0..., use_global_device_ids=true, to_apply=%region_4.6 | all-reduce | flops 2 | bytes 16 | tf_op jit(solution)/shard_map/psum | solution.py:239
  269.9 0.6 fusion.11
  271.8 0.0 copy-done
  271.8 1.0 multiply_add_fusion
  272.8 0.0 copy-done.1
  272.8 1.4 subtract_bitcast_fusion
  (2 shorter events, 0.0 us)
Async XLA Ops:
  1.9 25.8 %collective-permute-start = (f32[2,3,16384]{2,1,0:T(4,128)S(1)}, f32[2,3,16384]{2,1,0:T(4,128)S(1)}, u32[]{:S(2)}, u32[]{:S(2)}) collective-permute-start(f32[2,3,16384]{2,1,0:T(4,128)S(1)} %copy.34), channel_id=1, source_target_pairs={{0,8},{8,16},{16,24},{24,32},{32,40},{40,48},{48,56},{56,64},{64,7... | collective-permute-start | bytes 1179656 | tf_op jit(solution)/shard_map/ppermute | solution.py:22
  6.3 22.3 %collective-permute-start.1 = (f32[2,3,16384]{2,1,0:T(4,128)S(1)}, f32[2,3,16384]{2,1,0:T(4,128)S(1)}, u32[]{:S(2)}, u32[]{:S(2)}) collective-permute-start(f32[2,3,16384]{2,1,0:T(4,128)S(1)} %copy.34), channel_id=1, source_target_pairs={{8,0},{16,8},{24,16},{32,24},{40,32},{48,40},{56,48},{64,56},{72,6... | collective-permute-start | bytes 1179656 | tf_op jit(solution)/shard_map/ppermute | solution.py:25
  72.3 17.2 %collective-permute-start.2 = (f32[2,3,16384]{2,1,0:T(4,128)S(1)}, f32[2,3,16384]{2,1,0:T(4,128)S(1)}, u32[]{:S(2)}, u32[]{:S(2)}) collective-permute-start(f32[2,3,16384]{2,1,0:T(4,128)S(1)} %get-tuple-element.13), channel_id=1, source_target_pairs={{0,504},{8,0},{16,8},{24,16},{32,24},{40,32},{48,40},{56,48},{64,5... | collective-permute-start | bytes 1179656 | tf_op jit(solution)/shard_map/ppermute | solution.py:32
  79.7 16.9 %collective-permute-start.3 = (f32[2,3,16384]{2,1,0:T(4,128)S(1)}, f32[2,3,16384]{2,1,0:T(4,128)S(1)}, u32[]{:S(2)}, u32[]{:S(2)}) collective-permute-start(f32[2,3,16384]{2,1,0:T(4,128)S(1)} %get-tuple-element.14), channel_id=1, source_target_pairs={{0,8},{8,16},{16,24},{24,32},{32,40},{40,48},{48,56},{56,64},{64,7... | collective-permute-start | bytes 1179656 | tf_op jit(solution)/shard_map/ppermute | solution.py:32
  98.1 14.8 %all-to-all-start = ((f32[8,2,3,2048]{3,1,2,0:T(2,128)}), f32[8,2,3,2048]{3,1,2,0:T(2,128)S(1)}, u32[]{:S(2)}, u32[]{:S(2)}) async-start(f32[8,2,3,2048]{3,1,2,0:T(2,128)} %copy.42), calls=%async_computation | async-start | bytes 786432 | tf_op jit(solution)/shard_map/all_to_all | solution.py:43
  126.7 17.8 %collective-permute-start.4 = (f32[2,3,16384]{2,1,0:T(4,128)S(1)}, f32[2,3,16384]{2,1,0:T(4,128)S(1)}, u32[]{:S(2)}, u32[]{:S(2)}) collective-permute-start(f32[2,3,16384]{2,1,0:T(4,128)S(1)} %copy.44), channel_id=1, source_target_pairs={{0,8},{8,16},{16,24},{24,32},{32,40},{40,48},{48,56},{56,64},{64,7... | collective-permute-start | bytes 1179656 | tf_op jit(solution)/shard_map/ppermute | solution.py:22
  128.7 16.8 %collective-permute-start.5 = (f32[2,3,16384]{2,1,0:T(4,128)S(1)}, f32[2,3,16384]{2,1,0:T(4,128)S(1)}, u32[]{:S(2)}, u32[]{:S(2)}) collective-permute-start(f32[2,3,16384]{2,1,0:T(4,128)S(1)} %copy.44), channel_id=1, source_target_pairs={{8,0},{16,8},{24,16},{32,24},{40,32},{48,40},{56,48},{64,56},{72,6... | collective-permute-start | bytes 1179656 | tf_op jit(solution)/shard_map/ppermute | solution.py:25
  148.2 15.5 %copy-start.2 = (f32[1,8]{1,0:T(1,128)S(1)}, f32[1,8]{1,0:T(1,128)}, u32[]{:S(2)}) copy-start(f32[1,8]{1,0:T(1,128)} %param.11) | copy-start | bytes 100
  148.2 123.6 %copy-start = (f32[2,3,16384]{2,0,1:T(2,128)S(1)}, f32[2,3,16384]{2,0,1:T(2,128)}, u32[]{:S(2)}) copy-start(f32[2,3,16384]{2,0,1:T(2,128)} %param.16) | copy-start | bytes 1179652
  148.3 124.5 %copy-start.1 = (f32[8,1024]{1,0:T(8,128)S(1)}, f32[8,1024]{1,0:T(8,128)}, u32[]{:S(2)}) copy-start(f32[8,1024]{1,0:T(8,128)} %get-tuple-element.6) | copy-start | bytes 98308

commit v2 on v1

--- a/solution.py
+++ b/solution.py
@@ -236,7 +236,7 @@
     dir_mt = transposed_window(dir_window, local_ids)
     rescanned = scan_call(dir_mt, slot, pix, cos_two, sin_two)
     curve_part = jnp.sum(weights[:, None] * rescanned * rescanned)
-    totals = lax.psum(jnp.stack([slope_part, curve_part]), TM_WAFER)
+    totals = by_axis(jnp.stack([slope_part, curve_part]), ("wafer_1", "wafer_0", "tm_0", "tm_1"))
     step_size = totals[0] / totals[1]
     new_map = sky_map + step_size * direction
     new_residual = (resid - step_size * rescanned)[None]

time: 275 us -> 224 us (0.81)
  the two profiles are of different devices: /device:TPU:1 before, /device:TPU:8 now
where the time goes in v2:
time: 224 us; the launch traced here: 223 us
  blocking collectives  64 us (29%)
  Pallas kernels  50.5 us (23%)
  waiting for transfers between devices  42.1 us (19%)
  starting transfers between devices  39.4 us (18%)
  other arithmetic  12.8 us (6%)
  local copies, waits for them, and re-layouts  12.1 us (5%)
    psum x4, blocking collectives, by_axis(): return functools.reduce(lax.psum, axes, value)  52.7 us
    pallas_call x1, Pallas kernels, bin_call(): pl.pallas_call(bin_kernel, out_shape=(jax.ShapeDtypeStruct((dets, samp),...  36.2 us
    ppermute x2, starting transfers between devices, with_halo(): lax.ppermute(lax.slice_in_dim(block, 0, width, axis=dim), axis, backward)  19.1 us
    ppermute x2, waiting for transfers between devices, with_halo(): lax.ppermute(lax.slice_in_dim(block, block.shape[dim] - width, None, axis...  16.4 us
    ppermute x2, waiting for transfers between devices, passed_along(): lax.ppermute(value, axis, [(i, (i + by) % count) for i in range(count)])  15.8 us
    pallas_call x1, Pallas kernels, scan_call(): pl.pallas_call(scan_kernel, out_shape=jax.ShapeDtypeStruct(slot.shape, jn...  14.3 us
    all_to_all x1, blocking collectives, copy_for_each(): return lax.all_to_all(copies, axis, split_axis=0, concat_axis=0, tiled=True)  11.3 us
    ppermute x2, starting transfers between devices, passed_along(): lax.ppermute(value, axis, [(i, (i + by) % count) for i in range(count)])  9.63 us
  transfers between devices with their start and end apart: 7, of which 7 were waited for; matrix products, arithmetic and copies ran while one was open for 1% of the time, Pallas kernels for 0%

profile of v2, /device:TPU:8, one launch (start us, length us, event | category | flops | bytes accessed | tf_op | source)
XLA Modules:
  0.0 223.0 jit_solution(7780276345506690995)
XLA Ops:
  0.6 1.3 copy.34
  1.9 3.8 %collective-permute-start = (f32[2,3,16384]{2,1,0:T(4,128)S(1)}, f32[2,3,16384]{2,1,0:T(4,128)S(1)}, u32[]{:S(2)}, u32[]{:S(2)}) collective-permute-start(f32[2,3,16384]{2,1,0:T(4,128)S(1)} %copy.34), channel_id=1, source_target_pairs={{0,8},{8,16},{16,24},{24,32},{32,40},{40,48},{48,56},{56,64},{64,7... | collective-permute-start | bytes 1179656 | tf_op jit(solution)/shard_map/ppermute | solution.py:22
  5.7 11.7 %collective-permute-start.1 = (f32[2,3,16384]{2,1,0:T(4,128)S(1)}, f32[2,3,16384]{2,1,0:T(4,128)S(1)}, u32[]{:S(2)}, u32[]{:S(2)}) collective-permute-start(f32[2,3,16384]{2,1,0:T(4,128)S(1)} %copy.34), channel_id=1, source_target_pairs={{8,0},{16,8},{24,16},{32,24},{40,32},{48,40},{56,48},{64,56},{72,6... | collective-permute-start | bytes 1179656 | tf_op jit(solution)/shard_map/ppermute | solution.py:25
  17.4 0.7 compare_and_fusion
  18.1 0.7 fusion.9
  18.8 1.5 sine_bitcast_fusion
  20.3 7.1 %collective-permute-done = f32[2,3,16384]{2,1,0:T(4,128)S(1)} collective-permute-done((f32[2,3,16384]{2,1,0:T(4,128)S(1)}, f32[2,3,16384]{2,1,0:T(4,128)S(1)}, u32[]{:S(2)}, u32[]{:S(2)}) %collective-permute-start) | collective-permute-done | bytes 393248 | tf_op jit(solution)/shard_map/ppermute | solution.py:22
  27.4 1.2 collective-permute-done.1
  28.6 0.4 pad_maximum_fusion
  29.0 1.2 gather_fusion
  30.2 0.3 broadcast_select_fusion.1
  30.4 0.6 reshape.129
  31.0 0.3 copy.38
  31.4 1.2 reshape.93.mt_ref
  32.6 36.2 %shard_map.95 = (f32[8,1024]{1,0:T(8,128)}, f32[4,3,128,128]{3,2,1,0:T(8,128)}) custom-call(f32[8]{0:T(128)} %bitcast.42, f32[3,128,512]{2,1,0:T(8,128)} %reshape.93.mt_ref, s32[8,1024]{1,0:T(8,128)} %bitcast.37, s32[8,1024]{1,0:T(8,128)} %bitcast.39, f32[8,1024]{1,0:T(8,128)} %get-tuple-element.19.cos_ref, f32[8,1024]{1,0:T(8,128)} %get-tuple-element.18.sin_ref, ...), custom_call_target="tpu_custom_call" | custom-call | tf_op jit(solution)/shard_map/pallas_call | solution.py:183
  68.8 1.5 reshape.130
  70.3 0.2 broadcast_in_dim.19
  70.5 1.6 scatter_fusion
  72.1 0.2 fusion.10
  72.3 7.7 %collective-permute-start.2 = (f32[2,3,16384]{2,1,0:T(4,128)S(1)}, f32[2,3,16384]{2,1,0:T(4,128)S(1)}, u32[]{:S(2)}, u32[]{:S(2)}) collective-permute-start(f32[2,3,16384]{2,1,0:T(4,128)S(1)} %get-tuple-element.13), channel_id=1, source_target_pairs={{0,504},{8,0},{16,8},{24,16},{32,24},{40,32},{48,40},{56,48},{64,5... | collective-permute-start | bytes 1179656 | tf_op jit(solution)/shard_map/ppermute | solution.py:32
  80.0 1.9 collective-permute-start.3
  81.9 8.4 %collective-permute-done.2 = f32[2,3,16384]{2,1,0:T(4,128)S(1)} collective-permute-done((f32[2,3,16384]{2,1,0:T(4,128)S(1)}, f32[2,3,16384]{2,1,0:T(4,128)S(1)}, u32[]{:S(2)}, u32[]{:S(2)}) %collective-permute-start.2) | collective-permute-done | bytes 393248 | tf_op jit(solution)/shard_map/ppermute | solution.py:32
  90.3 7.4 %collective-permute-done.3 = f32[2,3,16384]{2,1,0:T(4,128)S(1)} collective-permute-done((f32[2,3,16384]{2,1,0:T(4,128)S(1)}, f32[2,3,16384]{2,1,0:T(4,128)S(1)}, u32[]{:S(2)}, u32[]{:S(2)}) %collective-permute-start.3) | collective-permute-done | bytes 393248 | tf_op jit(solution)/shard_map/ppermute | solution.py:32
  97.8 0.2 fusion
  97.9 0.3 reshape.131
  98.2 1.1 copy.42
  99.3 4.9 %all-to-all-start = ((f32[8,2,3,2048]{3,1,2,0:T(2,128)}), f32[8,2,3,2048]{3,1,2,0:T(2,128)S(1)}, u32[]{:S(2)}, u32[]{:S(2)}) async-start(f32[8,2,3,2048]{3,1,2,0:T(2,128)} %copy.42), calls=%async_computation | async-start | bytes 786432 | tf_op jit(solution)/shard_map/all_to_all | solution.py:43
  104.2 7.5 %all-to-all-done = f32[8,2,3,2048]{3,1,2,0:T(2,128)S(1)} async-done(((f32[8,2,3,2048]{3,1,2,0:T(2,128)}), f32[8,2,3,2048]{3,1,2,0:T(2,128)S(1)}, u32[]{:S(2)}, u32[]{:S(2)}) %all-to-all-start) | async-done | bytes 393248 | tf_op jit(solution)/shard_map/all_to_all | solution.py:43
  111.7 0.1 reduce_sum.27
  111.8 0.9 fusion.6
  112.7 0.7 multiply_reduce_fusion
  113.3 0.2 broadcast_in_dim.20
  113.5 11.3 %all_to_all.10 = f32[8,2,3,2048]{3,1,2,0:T(2,128)S(1)} all-to-all(f32[8,2,3,2048]{3,1,2,0:T(2,128)S(1)} %broadcast_in_dim.20), channel_id=1, replica_groups=mesh['tm_0'=4,'tm_1'=16,'wafer_0'=4,'wafer_1'=2] {'wafer_0','wafer_1'}, dimensions={0} | all-to-all | bytes 786432 | tf_op jit(solution)/shard_map/all_to_all | solution.py:55
  124.8 0.3 copy.44
  125.1 1.9 collective-permute-start.4
  127.0 7.4 %collective-permute-start.5 = (f32[2,3,16384]{2,1,0:T(4,128)S(1)}, f32[2,3,16384]{2,1,0:T(4,128)S(1)}, u32[]{:S(2)}, u32[]{:S(2)}) collective-permute-start(f32[2,3,16384]{2,1,0:T(4,128)S(1)} %copy.44), channel_id=1, source_target_pairs={{8,0},{16,8},{24,16},{32,24},{40,32},{48,40},{56,48},{64,56},{72,6... | collective-permute-start | bytes 1179656 | tf_op jit(solution)/shard_map/ppermute | solution.py:25
  134.5 9.3 %collective-permute-done.4 = f32[2,3,16384]{2,1,0:T(4,128)S(1)} collective-permute-done((f32[2,3,16384]{2,1,0:T(4,128)S(1)}, f32[2,3,16384]{2,1,0:T(4,128)S(1)}, u32[]{:S(2)}, u32[]{:S(2)}) %collective-permute-start.4) | collective-permute-done | bytes 393248 | tf_op jit(solution)/shard_map/ppermute | solution.py:22
  143.8 1.2 collective-permute-done.5
  145.0 0.4 pad_maximum_fusion.1
  145.4 1.2 gather_fusion.1
  146.5 0.3 broadcast_select_fusion
  146.8 0.6 reshape.132
  147.4 0.3 copy.48
  147.8 0.0 copy-start.2
  147.8 0.0 copy-start
  147.8 0.0 copy-start.1
  147.8 1.2 reshape.98.mt_ref
  149.0 14.3 %shard_map.96 = f32[8,1024]{1,0:T(8,128)} custom-call(f32[3,128,512]{2,1,0:T(8,128)} %reshape.98.mt_ref, s32[8,1024]{1,0:T(8,128)} %bitcast.38, s32[8,1024]{1,0:T(8,128)} %bitcast.40, f32[8,1024]{1,0:T(8,128)} %get-tuple-element.19.cos_ref, f32[8,1024]{1,0:T(8,128)} %get-tuple-element.18.sin_ref), custom_call_target="tpu_custom_call" | custom-call | tf_op jit(solution)/shard_map/pallas_call | solution.py:198
  163.2 0.0 copy-done.2
  163.2 1.4 fusion.1
  164.7 1.4 pad_maximum_fusion.3
  166.0 2.4 %psum.28 = f32[2]{0:T(128)S(1)} all-reduce(f32[2]{0:T(128)S(1)} %pad_maximum_fusion.3), channel_id=1, replica_groups=mesh['tm_0'=4,'tm_1'=16,'wafer_0'=4,'wafer_1'=2] {'wafer_1'}, use_global_device_ids=true, to_apply=%region_4.6 | all-reduce | flops 2 | bytes 16 | tf_op jit(solution)/shard_map/psum | solution.py:63
  168.5 9.2 %psum.29 = f32[2]{0:T(128)S(1)} all-reduce(f32[2]{0:T(128)S(1)} %psum.28), channel_id=1, replica_groups=mesh['tm_0'=4,'tm_1'=16,'wafer_0'=4,'wafer_1'=2] {'wafer_0'}, use_global_device_ids=true, to_apply=%region_5.7 | all-reduce | flops 2 | bytes 16 | tf_op jit(solution)/shard_map/psum | solution.py:63
  177.6 7.7 %psum.30 = f32[2]{0:T(128)S(1)} all-reduce(f32[2]{0:T(128)S(1)} %psum.29), channel_id=1, replica_groups=mesh['tm_0'=4,'tm_1'=16,'wafer_0'=4,'wafer_1'=2] {'tm_0'}, use_global_device_ids=true, to_apply=%region_6.8 | all-reduce | flops 2 | bytes 16 | tf_op jit(solution)/shard_map/psum | solution.py:63
  185.4 33.3 %psum.31 = f32[2]{0:T(128)S(1)} all-reduce(f32[2]{0:T(128)S(1)} %psum.30), channel_id=1, replica_groups=mesh['tm_0'=4,'tm_1'=16,'wafer_0'=4,'wafer_1'=2] {'tm_1'}, use_global_device_ids=true, to_apply=%region_7.9 | all-reduce | flops 2 | bytes 16 | tf_op jit(solution)/shard_map/psum | solution.py:63
  218.7 0.6 fusion.11
  220.6 0.0 copy-done
  220.7 1.0 multiply_add_fusion
  221.6 0.0 copy-done.1
  221.6 1.4 subtract_bitcast_fusion
  (2 shorter events, 0.0 us)
Async XLA Ops:
  1.9 25.5 %collective-permute-start = (f32[2,3,16384]{2,1,0:T(4,128)S(1)}, f32[2,3,16384]{2,1,0:T(4,128)S(1)}, u32[]{:S(2)}, u32[]{:S(2)}) collective-permute-start(f32[2,3,16384]{2,1,0:T(4,128)S(1)} %copy.34), channel_id=1, source_target_pairs={{0,8},{8,16},{16,24},{24,32},{32,40},{40,48},{48,56},{56,64},{64,7... | collective-permute-start | bytes 1179656 | tf_op jit(solution)/shard_map/ppermute | solution.py:22
  5.7 22.9 %collective-permute-start.1 = (f32[2,3,16384]{2,1,0:T(4,128)S(1)}, f32[2,3,16384]{2,1,0:T(4,128)S(1)}, u32[]{:S(2)}, u32[]{:S(2)}) collective-permute-start(f32[2,3,16384]{2,1,0:T(4,128)S(1)} %copy.34), channel_id=1, source_target_pairs={{8,0},{16,8},{24,16},{32,24},{40,32},{48,40},{56,48},{64,56},{72,6... | collective-permute-start | bytes 1179656 | tf_op jit(solution)/shard_map/ppermute | solution.py:25
  72.3 18.0 %collective-permute-start.2 = (f32[2,3,16384]{2,1,0:T(4,128)S(1)}, f32[2,3,16384]{2,1,0:T(4,128)S(1)}, u32[]{:S(2)}, u32[]{:S(2)}) collective-permute-start(f32[2,3,16384]{2,1,0:T(4,128)S(1)} %get-tuple-element.13), channel_id=1, source_target_pairs={{0,504},{8,0},{16,8},{24,16},{32,24},{40,32},{48,40},{56,48},{64,5... | collective-permute-start | bytes 1179656 | tf_op jit(solution)/shard_map/ppermute | solution.py:32
  80.0 17.7 %collective-permute-start.3 = (f32[2,3,16384]{2,1,0:T(4,128)S(1)}, f32[2,3,16384]{2,1,0:T(4,128)S(1)}, u32[]{:S(2)}, u32[]{:S(2)}) collective-permute-start(f32[2,3,16384]{2,1,0:T(4,128)S(1)} %get-tuple-element.14), channel_id=1, source_target_pairs={{0,8},{8,16},{16,24},{24,32},{32,40},{40,48},{48,56},{56,64},{64,7... | collective-permute-start | bytes 1179656 | tf_op jit(solution)/shard_map/ppermute | solution.py:32
  99.3 12.4 %all-to-all-start = ((f32[8,2,3,2048]{3,1,2,0:T(2,128)}), f32[8,2,3,2048]{3,1,2,0:T(2,128)S(1)}, u32[]{:S(2)}, u32[]{:S(2)}) async-start(f32[8,2,3,2048]{3,1,2,0:T(2,128)} %copy.42), calls=%async_computation | async-start | bytes 786432 | tf_op jit(solution)/shard_map/all_to_all | solution.py:43
  125.1 18.7 %collective-permute-start.4 = (f32[2,3,16384]{2,1,0:T(4,128)S(1)}, f32[2,3,16384]{2,1,0:T(4,128)S(1)}, u32[]{:S(2)}, u32[]{:S(2)}) collective-permute-start(f32[2,3,16384]{2,1,0:T(4,128)S(1)} %copy.44), channel_id=1, source_target_pairs={{0,8},{8,16},{16,24},{24,32},{32,40},{40,48},{48,56},{56,64},{64,7... | collective-permute-start | bytes 1179656 | tf_op jit(solution)/shard_map/ppermute | solution.py:22
  127.0 17.9 %collective-permute-start.5 = (f32[2,3,16384]{2,1,0:T(4,128)S(1)}, f32[2,3,16384]{2,1,0:T(4,128)S(1)}, u32[]{:S(2)}, u32[]{:S(2)}) collective-permute-start(f32[2,3,16384]{2,1,0:T(4,128)S(1)} %copy.44), channel_id=1, source_target_pairs={{8,0},{16,8},{24,16},{32,24},{40,32},{48,40},{56,48},{64,56},{72,6... | collective-permute-start | bytes 1179656 | tf_op jit(solution)/shard_map/ppermute | solution.py:25
  147.8 15.5 %copy-start.2 = (f32[1,8]{1,0:T(1,128)S(1)}, f32[1,8]{1,0:T(1,128)}, u32[]{:S(2)}) copy-start(f32[1,8]{1,0:T(1,128)} %param.11) | copy-start | bytes 100
  147.8 72.9 %copy-start = (f32[2,3,16384]{2,0,1:T(2,128)S(1)}, f32[2,3,16384]{2,0,1:T(2,128)}, u32[]{:S(2)}) copy-start(f32[2,3,16384]{2,0,1:T(2,128)} %param.16) | copy-start | bytes 1179652
  147.8 73.8 %copy-start.1 = (f32[8,1024]{1,0:T(8,128)S(1)}, f32[8,1024]{1,0:T(8,128)}, u32[]{:S(2)}) copy-start(f32[8,1024]{1,0:T(8,128)} %get-tuple-element.6) | copy-start | bytes 98308

commit v3 on v2

--- a/solution.py
+++ b/solution.py
@@ -8,9 +8,9 @@
 from jax.sharding import Mesh
 from jax.sharding import PartitionSpec as P
 
-TM = ("tm_0", "tm_1")
+TM = ("tm_0", "tm_hi", "tm_lo")
 WAFER = ("wafer_0", "wafer_1")
-TM_WAFER = ("tm_0", "tm_1", "wafer_0", "wafer_1")
+TM_WAFER = ("tm_0", "tm_hi", "tm_lo", "wafer_0", "wafer_1")
 
 
 def with_halo(block, sides, width):
@@ -76,12 +76,10 @@
 SIDE = 128
 
 
-def split3(value):
+def split2(value):
     hi = value.astype(jnp.bfloat16)
-    rest = value - hi.astype(jnp.float32)
-    mid = rest.astype(jnp.bfloat16)
-    lo = (rest - mid.astype(jnp.float32)).astype(jnp.bfloat16)
-    return hi, mid, lo
+    lo = (value - hi.astype(jnp.float32)).astype(jnp.bfloat16)
+    return hi, lo
 
 
 def row_onehot(slot, pix, rows):
@@ -96,20 +94,25 @@
     return ids == col
 
 
-def sample_map(pieces, at, mask, comp):
-    picked = None
-    for piece in pieces:
-        part = jnp.dot(piece[comp], at, preferred_element_type=jnp.float32)
-        picked = part if picked is None else picked + part
-    return jnp.sum(jnp.where(mask, picked, 0.0), axis=0, keepdims=True)
+def stacked_map(mt_ref, lhs_ref):
+    hi, lo = split2(mt_ref[...])
+    for comp in range(3):
+        lhs_ref[comp * SIDE:(comp + 1) * SIDE, :] = hi[comp]
+        lhs_ref[(3 + comp) * SIDE:(4 + comp) * SIDE, :] = lo[comp]
+
+
+def sampled(lhs_ref, at, mask):
+    both = jnp.dot(lhs_ref[...], at, preferred_element_type=jnp.float32)
+    values = []
+    for comp in range(3):
+        full = both[comp * SIDE:(comp + 1) * SIDE] + both[(3 + comp) * SIDE:(4 + comp) * SIDE]
+        values.append(jnp.sum(jnp.where(mask, full, 0.0), axis=0, keepdims=True))
+    return values
 
 
 def bin_kernel(w_ref, mt_ref, slot_ref, pix_ref, cos_ref, sin_ref, ts_ref, resid_ref, g_ref,
-               hi_ref, mid_ref, lo_ref, acc_ref):
-    hi, mid, lo = split3(mt_ref[...])
-    hi_ref[...] = hi
-    mid_ref[...] = mid
-    lo_ref[...] = lo
+               lhs_ref, rhs_ref, acc_ref):
+    stacked_map(mt_ref, lhs_ref)
     acc_ref[...] = jnp.zeros(acc_ref.shape, jnp.float32)
     rows = mt_ref.shape[2]
     nt = (((1,), (1,)), ((), ()))
@@ -121,33 +124,27 @@
         sn = sin_ref[pl.ds(d, 1), :]
         at = row_onehot(slot, pix, rows)
         mask = col_mask(pix)
-        pieces = (hi_ref, mid_ref, lo_ref)
-        v0 = sample_map(pieces, at, mask, 0)
-        v1 = sample_map(pieces, at, mask, 1)
-        v2 = sample_map(pieces, at, mask, 2)
+        v0, v1, v2 = sampled(lhs_ref, at, mask)
         resid = ts_ref[pl.ds(d, 1), :] - (v0 + cs * v1 + sn * v2)
         resid_ref[pl.ds(d, 1), :] = resid
         weighted = w_ref[d] * resid
         for comp, term in ((0, weighted), (1, weighted * cs), (2, weighted * sn)):
-            dt = jnp.where(mask, term, 0.0)
-            total = None
-            for piece in split3(dt):
-                part = lax.dot_general(at, piece, nt, preferred_element_type=jnp.float32)
-                total = part if total is None else total + part
-            acc_ref[comp] += total
+            hi, lo = split2(jnp.where(mask, term, 0.0))
+            rhs_ref[comp * SIDE:(comp + 1) * SIDE, :] = hi
+            rhs_ref[(3 + comp) * SIDE:(4 + comp) * SIDE, :] = lo
+        acc_ref[...] += lax.dot_general(at, rhs_ref[...], nt, preferred_element_type=jnp.float32)
         return carry
 
     lax.fori_loop(0, slot_ref.shape[0], body, 0)
     for s in range(g_ref.shape[0]):
         for comp in range(3):
-            g_ref[s, comp] = acc_ref[comp, s * SIDE:(s + 1) * SIDE, :]
-
-
-def scan_kernel(mt_ref, slot_ref, pix_ref, cos_ref, sin_ref, out_ref, hi_ref, mid_ref, lo_ref):
-    hi, mid, lo = split3(mt_ref[...])
-    hi_ref[...] = hi
-    mid_ref[...] = mid
-    lo_ref[...] = lo
+            rows_s = slice(s * SIDE, (s + 1) * SIDE)
+            g_ref[s, comp] = (acc_ref[rows_s, comp * SIDE:(comp + 1) * SIDE]
+                              + acc_ref[rows_s, (3 + comp) * SIDE:(4 + comp) * SIDE])
+
+
+def scan_kernel(mt_ref, slot_ref, pix_ref, cos_ref, sin_ref, out_ref, lhs_ref):
+    stacked_map(mt_ref, lhs_ref)
     rows = mt_ref.shape[2]
 
     def body(d, carry):
@@ -155,10 +152,7 @@
         pix = pix_ref[pl.ds(d, 1), :]
         at = row_onehot(slot, pix, rows)
         mask = col_mask(pix)
-        pieces = (hi_ref, mid_ref, lo_ref)
-        v0 = sample_map(pieces, at, mask, 0)
-        v1 = sample_map(pieces, at, mask, 1)
-        v2 = sample_map(pieces, at, mask, 2)
+        v0, v1, v2 = sampled(lhs_ref, at, mask)
         out_ref[pl.ds(d, 1), :] = v0 + cos_ref[pl.ds(d, 1), :] * v1 + sin_ref[pl.ds(d, 1), :] * v2
         return carry
 
@@ -188,8 +182,11 @@
         ),
         in_specs=[smem] + [vmem] * 6,
         out_specs=(vmem, vmem),
-        scratch_shapes=[pltpu.VMEM(mt.shape, jnp.bfloat16)] * 3
-        + [pltpu.VMEM((3, hits * SIDE, SIDE), jnp.float32)],
+        scratch_shapes=[
+            pltpu.VMEM((6 * SIDE, hits * SIDE), jnp.bfloat16),
+            pltpu.VMEM((6 * SIDE, samp), jnp.bfloat16),
+            pltpu.VMEM((hits * SIDE, 6 * SIDE), jnp.float32),
+        ],
     )(weights, mt, slot, pix, cos_two, sin_two, ts)
 
 
@@ -200,7 +197,7 @@
         out_shape=jax.ShapeDtypeStruct(slot.shape, jnp.float32),
         in_specs=[vmem] * 5,
         out_specs=vmem,
-        scratch_shapes=[pltpu.VMEM(mt.shape, jnp.bfloat16)] * 3,
+        scratch_shapes=[pltpu.VMEM((6 * SIDE, mt.shape[2]), jnp.bfloat16)],
     )(mt, slot, pix, cos_two, sin_two)
 
 
@@ -236,7 +233,7 @@
     dir_mt = transposed_window(dir_window, local_ids)
     rescanned = scan_call(dir_mt, slot, pix, cos_two, sin_two)
     curve_part = jnp.sum(weights[:, None] * rescanned * rescanned)
-    totals = by_axis(jnp.stack([slope_part, curve_part]), ("wafer_1", "wafer_0", "tm_0", "tm_1"))
+    totals = by_axis(jnp.stack([slope_part, curve_part]), ("wafer_1", "wafer_0", "tm_0", "tm_lo", "tm_hi"))
     step_size = totals[0] / totals[1]
     new_map = sky_map + step_size * direction
     new_residual = (resid - step_size * rescanned)[None]
@@ -244,7 +241,7 @@
 
 
 def solution(mesh):
-    split = Mesh(mesh.devices.reshape(4, 16, 4, 2), ("tm_0", "tm_1", "wafer_0", "wafer_1"))
+    split = Mesh(mesh.devices.reshape(4, 4, 4, 4, 2), TM_WAFER)
     in_specs = (
         P(TM, WAFER, None),
         P(TM, WAFER),

time: 224 us -> 202 us (0.902)
  Pallas kernels: 50.5 us -> 33.3 us
  blocking collectives: 64 us -> 59 us
    pallas_call x1, Pallas kernels: 36.2 us -> 23.1 us  [bin_call(): pl.pallas_call(bin_kernel, out_shape=(jax.ShapeDtypeStruct((dets, samp),...]
    psum x4 -> x5, blocking collectives: 52.7 us -> 47.7 us  [by_axis(): return functools.reduce(lax.psum, axes, value)]
    pallas_call x1, Pallas kernels: 14.3 us -> 10.2 us  [scan_call(): pl.pallas_call(scan_kernel, out_shape=jax.ShapeDtypeStruct(slot.shape, jn...]
where the time goes in v3:
time: 202 us; the launch traced here: 201 us
  blocking collectives  59 us (29%)
  waiting for transfers between devices  42.1 us (21%)
  starting transfers between devices  39.4 us (20%)
  Pallas kernels  33.3 us (16%)
  other arithmetic  12.8 us (6%)
  local copies, waits for them, and re-layouts  12.1 us (6%)
  between operations  2.21 us (1%)
    psum x5, blocking collectives, by_axis(): return functools.reduce(lax.psum, axes, value)  47.7 us
    pallas_call x1, Pallas kernels, bin_call(): pl.pallas_call(bin_kernel, out_shape=(jax.ShapeDtypeStruct((dets, samp),...  23.1 us
    ppermute x2, starting transfers between devices, with_halo(): lax.ppermute(lax.slice_in_dim(block, 0, width, axis=dim), axis, backward)  19.1 us
    ppermute x2, waiting for transfers between devices, with_halo(): lax.ppermute(lax.slice_in_dim(block, block.shape[dim] - width, None, axis...  16.4 us
    ppermute x2, waiting for transfers between devices, passed_along(): lax.ppermute(value, axis, [(i, (i + by) % count) for i in range(count)])  15.8 us
    all_to_all x1, blocking collectives, copy_for_each(): return lax.all_to_all(copies, axis, split_axis=0, concat_axis=0, tiled=True)  11.3 us
    pallas_call x1, Pallas kernels, scan_call(): pl.pallas_call(scan_kernel, out_shape=jax.ShapeDtypeStruct(slot.shape, jn...  10.2 us
    ppermute x2, starting transfers between devices, passed_along(): lax.ppermute(value, axis, [(i, (i + by) % count) for i in range(count)])  9.63 us
  transfers between devices with their start and end apart: 7, of which 7 were waited for; matrix products, arithmetic and copies ran while one was open for 1% of the time, Pallas kernels for 0%

profile of v3, /device:TPU:8, one launch (start us, length us, event | category | flops | bytes accessed | tf_op | source)
XLA Modules:
  0.0 200.9 jit_solution(17084360547980174407)
XLA Ops:
  0.6 1.3 copy.34
  1.9 3.8 %collective-permute-start = (f32[2,3,16384]{2,1,0:T(4,128)S(1)}, f32[2,3,16384]{2,1,0:T(4,128)S(1)}, u32[]{:S(2)}, u32[]{:S(2)}) collective-permute-start(f32[2,3,16384]{2,1,0:T(4,128)S(1)} %copy.34), channel_id=1, source_target_pairs={{0,8},{8,16},{16,24},{24,32},{32,40},{40,48},{48,56},{56,64},{64,7... | collective-permute-start | bytes 1179656 | tf_op jit(solution)/shard_map/ppermute | solution.py:22
  5.7 11.7 %collective-permute-start.1 = (f32[2,3,16384]{2,1,0:T(4,128)S(1)}, f32[2,3,16384]{2,1,0:T(4,128)S(1)}, u32[]{:S(2)}, u32[]{:S(2)}) collective-permute-start(f32[2,3,16384]{2,1,0:T(4,128)S(1)} %copy.34), channel_id=1, source_target_pairs={{8,0},{16,8},{24,16},{32,24},{40,32},{48,40},{56,48},{64,56},{72,6... | collective-permute-start | bytes 1179656 | tf_op jit(solution)/shard_map/ppermute | solution.py:25
  17.4 0.7 compare_and_fusion
  18.1 0.7 fusion.9
  18.8 1.5 sine_bitcast_fusion
  20.3 7.1 %collective-permute-done = f32[2,3,16384]{2,1,0:T(4,128)S(1)} collective-permute-done((f32[2,3,16384]{2,1,0:T(4,128)S(1)}, f32[2,3,16384]{2,1,0:T(4,128)S(1)}, u32[]{:S(2)}, u32[]{:S(2)}) %collective-permute-start) | collective-permute-done | bytes 393248 | tf_op jit(solution)/shard_map/ppermute | solution.py:22
  27.4 1.2 collective-permute-done.1
  28.6 0.4 pad_maximum_fusion
  29.0 1.2 gather_fusion
  30.2 0.3 broadcast_select_fusion.1
  30.4 0.6 reshape.129
  31.0 0.3 copy.38
  31.4 1.2 reshape.93.mt_ref
  32.6 23.1 %shard_map.95 = (f32[8,1024]{1,0:T(8,128)}, f32[4,3,128,128]{3,2,1,0:T(8,128)}) custom-call(f32[8]{0:T(128)} %bitcast.42, f32[3,128,512]{2,1,0:T(8,128)} %reshape.93.mt_ref, s32[8,1024]{1,0:T(8,128)} %bitcast.37, s32[8,1024]{1,0:T(8,128)} %bitcast.39, f32[8,1024]{1,0:T(8,128)} %get-tuple-element.19.cos_ref, f32[8,1024]{1,0:T(8,128)} %get-tuple-element.18.sin_ref, ...), custom_call_target="tpu_custom_call" | custom-call | tf_op jit(solution)/shard_map/pallas_call | solution.py:177
  55.7 1.5 reshape.130
  57.2 0.2 broadcast_in_dim.19
  57.4 1.6 scatter_fusion
  59.0 0.2 fusion.10
  59.2 7.7 %collective-permute-start.2 = (f32[2,3,16384]{2,1,0:T(4,128)S(1)}, f32[2,3,16384]{2,1,0:T(4,128)S(1)}, u32[]{:S(2)}, u32[]{:S(2)}) collective-permute-start(f32[2,3,16384]{2,1,0:T(4,128)S(1)} %get-tuple-element.13), channel_id=1, source_target_pairs={{0,504},{8,0},{16,8},{24,16},{32,24},{40,32},{48,40},{56,48},{64,5... | collective-permute-start | bytes 1179656 | tf_op jit(solution)/shard_map/ppermute | solution.py:32
  66.9 1.9 collective-permute-start.3
  68.8 8.4 %collective-permute-done.2 = f32[2,3,16384]{2,1,0:T(4,128)S(1)} collective-permute-done((f32[2,3,16384]{2,1,0:T(4,128)S(1)}, f32[2,3,16384]{2,1,0:T(4,128)S(1)}, u32[]{:S(2)}, u32[]{:S(2)}) %collective-permute-start.2) | collective-permute-done | bytes 393248 | tf_op jit(solution)/shard_map/ppermute | solution.py:32
  77.2 7.4 %collective-permute-done.3 = f32[2,3,16384]{2,1,0:T(4,128)S(1)} collective-permute-done((f32[2,3,16384]{2,1,0:T(4,128)S(1)}, f32[2,3,16384]{2,1,0:T(4,128)S(1)}, u32[]{:S(2)}, u32[]{:S(2)}) %collective-permute-start.3) | collective-permute-done | bytes 393248 | tf_op jit(solution)/shard_map/ppermute | solution.py:32
  84.7 0.2 fusion
  84.8 0.3 reshape.131
  85.1 1.1 copy.42
  86.2 4.9 %all-to-all-start = ((f32[8,2,3,2048]{3,1,2,0:T(2,128)}), f32[8,2,3,2048]{3,1,2,0:T(2,128)S(1)}, u32[]{:S(2)}, u32[]{:S(2)}) async-start(f32[8,2,3,2048]{3,1,2,0:T(2,128)} %copy.42), calls=%async_computation | async-start | bytes 786432 | tf_op jit(solution)/shard_map/all_to_all | solution.py:43
  91.1 7.5 %all-to-all-done = f32[8,2,3,2048]{3,1,2,0:T(2,128)S(1)} async-done(((f32[8,2,3,2048]{3,1,2,0:T(2,128)}), f32[8,2,3,2048]{3,1,2,0:T(2,128)S(1)}, u32[]{:S(2)}, u32[]{:S(2)}) %all-to-all-start) | async-done | bytes 393248 | tf_op jit(solution)/shard_map/all_to_all | solution.py:43
  98.6 0.1 reduce_sum.27
  98.7 0.9 fusion.6
  99.6 0.7 multiply_reduce_fusion
  100.2 0.2 broadcast_in_dim.20
  100.4 11.3 %all_to_all.10 = f32[8,2,3,2048]{3,1,2,0:T(2,128)S(1)} all-to-all(f32[8,2,3,2048]{3,1,2,0:T(2,128)S(1)} %broadcast_in_dim.20), channel_id=1, replica_groups=mesh['tm_0'=4,'tm_hi'=4,'tm_lo'=4,'wafer_0'=4,'wafer_1'=2] {'wafer_0','w..., dimensions={0} | all-to-all | bytes 786432 | tf_op jit(solution)/shard_map/all_to_all | solution.py:55
  111.7 0.3 copy.44
  112.0 1.9 collective-permute-start.4
  113.9 7.4 %collective-permute-start.5 = (f32[2,3,16384]{2,1,0:T(4,128)S(1)}, f32[2,3,16384]{2,1,0:T(4,128)S(1)}, u32[]{:S(2)}, u32[]{:S(2)}) collective-permute-start(f32[2,3,16384]{2,1,0:T(4,128)S(1)} %copy.44), channel_id=1, source_target_pairs={{8,0},{16,8},{24,16},{32,24},{40,32},{48,40},{56,48},{64,56},{72,6... | collective-permute-start | bytes 1179656 | tf_op jit(solution)/shard_map/ppermute | solution.py:25
  121.4 9.3 %collective-permute-done.4 = f32[2,3,16384]{2,1,0:T(4,128)S(1)} collective-permute-done((f32[2,3,16384]{2,1,0:T(4,128)S(1)}, f32[2,3,16384]{2,1,0:T(4,128)S(1)}, u32[]{:S(2)}, u32[]{:S(2)}) %collective-permute-start.4) | collective-permute-done | bytes 393248 | tf_op jit(solution)/shard_map/ppermute | solution.py:22
  130.7 1.2 collective-permute-done.5
  131.9 0.4 pad_maximum_fusion.1
  132.2 1.2 gather_fusion.1
  133.4 0.3 broadcast_select_fusion
  133.7 0.6 reshape.132
  134.3 0.3 copy.48
  134.6 0.0 copy-start.2
  134.7 0.0 copy-start
  134.7 0.0 copy-start.1
  134.7 1.2 reshape.98.mt_ref
  135.9 10.2 %shard_map.96 = f32[8,1024]{1,0:T(8,128)} custom-call(f32[3,128,512]{2,1,0:T(8,128)} %reshape.98.mt_ref, s32[8,1024]{1,0:T(8,128)} %bitcast.38, s32[8,1024]{1,0:T(8,128)} %bitcast.40, f32[8,1024]{1,0:T(8,128)} %get-tuple-element.19.cos_ref, f32[8,1024]{1,0:T(8,128)} %get-tuple-element.18.sin_ref), custom_call_target="tpu_custom_call" | custom-call | tf_op jit(solution)/shard_map/pallas_call | solution.py:195
  146.1 0.0 copy-done.2
  146.1 1.4 fusion.1
  147.5 1.4 pad_maximum_fusion.3
  148.9 2.4 %psum.35 = f32[2]{0:T(128)S(1)} all-reduce(f32[2]{0:T(128)S(1)} %pad_maximum_fusion.3), channel_id=1, replica_groups=mesh['tm_0'=4,'tm_hi'=4,'tm_lo'=4,'wafer_0'=4,'wafer_1'=2] {'wafer_1'}, use_global_device_ids=true, to_apply=%region_4.6 | all-reduce | flops 2 | bytes 16 | tf_op jit(solution)/shard_map/psum | solution.py:63
  151.3 9.1 %psum.36 = f32[2]{0:T(128)S(1)} all-reduce(f32[2]{0:T(128)S(1)} %psum.35), channel_id=1, replica_groups=mesh['tm_0'=4,'tm_hi'=4,'tm_lo'=4,'wafer_0'=4,'wafer_1'=2] {'wafer_0'}, use_global_device_ids=true, to_apply=%region_5.7 | all-reduce | flops 2 | bytes 16 | tf_op jit(solution)/shard_map/psum | solution.py:63
  160.5 7.7 %psum.37 = f32[2]{0:T(128)S(1)} all-reduce(f32[2]{0:T(128)S(1)} %psum.36), channel_id=1, replica_groups=mesh['tm_0'=4,'tm_hi'=4,'tm_lo'=4,'wafer_0'=4,'wafer_1'=2] {'tm_0'}, use_global_device_ids=true, to_apply=%region_6.8 | all-reduce | flops 2 | bytes 16 | tf_op jit(solution)/shard_map/psum | solution.py:63
  168.2 8.4 %psum.38 = f32[2]{0:T(128)S(1)} all-reduce(f32[2]{0:T(128)S(1)} %psum.37), channel_id=1, replica_groups=mesh['tm_0'=4,'tm_hi'=4,'tm_lo'=4,'wafer_0'=4,'wafer_1'=2] {'tm_lo'}, use_global_device_ids=true, to_apply=%region_7.9 | all-reduce | flops 2 | bytes 16 | tf_op jit(solution)/shard_map/psum | solution.py:63
  176.6 20.0 %psum.39 = f32[2]{0:T(128)S(1)} all-reduce(f32[2]{0:T(128)S(1)} %psum.38), channel_id=1, replica_groups=mesh['tm_0'=4,'tm_hi'=4,'tm_lo'=4,'wafer_0'=4,'wafer_1'=2] {'tm_hi'}, use_global_device_ids=true, to_apply=%region_8.10 | all-reduce | flops 2 | bytes 16 | tf_op jit(solution)/shard_map/psum | solution.py:63
  196.6 0.6 fusion.11
  198.5 0.0 copy-done
  198.5 1.0 multiply_add_fusion
  199.5 0.0 copy-done.1
  199.5 1.4 subtract_bitcast_fusion
  (2 shorter events, 0.0 us)
Async XLA Ops:
  1.9 25.5 %collective-permute-start = (f32[2,3,16384]{2,1,0:T(4,128)S(1)}, f32[2,3,16384]{2,1,0:T(4,128)S(1)}, u32[]{:S(2)}, u32[]{:S(2)}) collective-permute-start(f32[2,3,16384]{2,1,0:T(4,128)S(1)} %copy.34), channel_id=1, source_target_pairs={{0,8},{8,16},{16,24},{24,32},{32,40},{40,48},{48,56},{56,64},{64,7... | collective-permute-start | bytes 1179656 | tf_op jit(solution)/shard_map/ppermute | solution.py:22
  5.7 22.9 %collective-permute-start.1 = (f32[2,3,16384]{2,1,0:T(4,128)S(1)}, f32[2,3,16384]{2,1,0:T(4,128)S(1)}, u32[]{:S(2)}, u32[]{:S(2)}) collective-permute-start(f32[2,3,16384]{2,1,0:T(4,128)S(1)} %copy.34), channel_id=1, source_target_pairs={{8,0},{16,8},{24,16},{32,24},{40,32},{48,40},{56,48},{64,56},{72,6... | collective-permute-start | bytes 1179656 | tf_op jit(solution)/shard_map/ppermute | solution.py:25
  59.2 18.0 %collective-permute-start.2 = (f32[2,3,16384]{2,1,0:T(4,128)S(1)}, f32[2,3,16384]{2,1,0:T(4,128)S(1)}, u32[]{:S(2)}, u32[]{:S(2)}) collective-permute-start(f32[2,3,16384]{2,1,0:T(4,128)S(1)} %get-tuple-element.13), channel_id=1, source_target_pairs={{0,504},{8,0},{16,8},{24,16},{32,24},{40,32},{48,40},{56,48},{64,5... | collective-permute-start | bytes 1179656 | tf_op jit(solution)/shard_map/ppermute | solution.py:32
  66.9 17.7 %collective-permute-start.3 = (f32[2,3,16384]{2,1,0:T(4,128)S(1)}, f32[2,3,16384]{2,1,0:T(4,128)S(1)}, u32[]{:S(2)}, u32[]{:S(2)}) collective-permute-start(f32[2,3,16384]{2,1,0:T(4,128)S(1)} %get-tuple-element.14), channel_id=1, source_target_pairs={{0,8},{8,16},{16,24},{24,32},{32,40},{40,48},{48,56},{56,64},{64,7... | collective-permute-start | bytes 1179656 | tf_op jit(solution)/shard_map/ppermute | solution.py:32
  86.2 12.4 %all-to-all-start = ((f32[8,2,3,2048]{3,1,2,0:T(2,128)}), f32[8,2,3,2048]{3,1,2,0:T(2,128)S(1)}, u32[]{:S(2)}, u32[]{:S(2)}) async-start(f32[8,2,3,2048]{3,1,2,0:T(2,128)} %copy.42), calls=%async_computation | async-start | bytes 786432 | tf_op jit(solution)/shard_map/all_to_all | solution.py:43
  112.0 18.7 %collective-permute-start.4 = (f32[2,3,16384]{2,1,0:T(4,128)S(1)}, f32[2,3,16384]{2,1,0:T(4,128)S(1)}, u32[]{:S(2)}, u32[]{:S(2)}) collective-permute-start(f32[2,3,16384]{2,1,0:T(4,128)S(1)} %copy.44), channel_id=1, source_target_pairs={{0,8},{8,16},{16,24},{24,32},{32,40},{40,48},{48,56},{56,64},{64,7... | collective-permute-start | bytes 1179656 | tf_op jit(solution)/shard_map/ppermute | solution.py:22
  113.9 17.9 %collective-permute-start.5 = (f32[2,3,16384]{2,1,0:T(4,128)S(1)}, f32[2,3,16384]{2,1,0:T(4,128)S(1)}, u32[]{:S(2)}, u32[]{:S(2)}) collective-permute-start(f32[2,3,16384]{2,1,0:T(4,128)S(1)} %copy.44), channel_id=1, source_target_pairs={{8,0},{16,8},{24,16},{32,24},{40,32},{48,40},{56,48},{64,56},{72,6... | collective-permute-start | bytes 1179656 | tf_op jit(solution)/shard_map/ppermute | solution.py:25
  134.6 11.4 %copy-start.2 = (f32[1,8]{1,0:T(1,128)S(1)}, f32[1,8]{1,0:T(1,128)}, u32[]{:S(2)}) copy-start(f32[1,8]{1,0:T(1,128)} %param.11) | copy-start | bytes 100
  134.7 63.9 %copy-start = (f32[2,3,16384]{2,0,1:T(2,128)S(1)}, f32[2,3,16384]{2,0,1:T(2,128)}, u32[]{:S(2)}) copy-start(f32[2,3,16384]{2,0,1:T(2,128)} %param.16) | copy-start | bytes 1179652
  134.7 64.8 %copy-start.1 = (f32[8,1024]{1,0:T(8,128)S(1)}, f32[8,1024]{1,0:T(8,128)}, u32[]{:S(2)}) copy-start(f32[8,1024]{1,0:T(8,128)} %get-tuple-element.6) | copy-start | bytes 98308

commit v4 on v3

--- a/solution.py
+++ b/solution.py
@@ -213,29 +213,42 @@
     weights = noise_weight[0]
     slot = hit_slot[0]
     pix = tile_pixel[0]
+    wafers = lax.axis_size(WAFER)
+    share_width = pixels // wafers
+    own_pixels = lax.axis_index(WAFER) * share_width
+    precond_share = lax.dynamic_slice_in_dim(precond, own_pixels, share_width, 2)
+    precond_window = with_halo(precond_share, ((TM, 0),), tiles_dev)
     window = with_halo(sky_map, ((TM, 0),), tiles_dev)
     mt = transposed_window(window, local_ids)
     resid, binned = bin_call(weights, mt, slot, pix, cos_two, sin_two, timestream[0])
     partial_tiles = binned.reshape(binned.shape[0], 3, pixels)
     near_tiles = jnp.zeros((3 * tiles_dev, 3, pixels), jnp.float32).at[local_ids].add(partial_tiles)
-    from_upper = passed_along(near_tiles[:tiles_dev], TM, -1)
-    from_lower = passed_along(near_tiles[2 * tiles_dev :], TM, 1)
-    owned_tiles = near_tiles[tiles_dev : 2 * tiles_dev] + from_upper + from_lower
-    grad_share = sum_at_owner(owned_tiles, WAFER, 2)
-    share_width = grad_share.shape[2]
-    inverse_share = lax.dynamic_slice_in_dim(
-        precond, lax.axis_index(WAFER) * share_width, share_width, 2
+    near_share = sum_at_owner(near_tiles, WAFER, 2)
+    lower = near_share[:tiles_dev]
+    middle = near_share[tiles_dev : 2 * tiles_dev]
+    upper = near_share[2 * tiles_dev :]
+    from_below = passed_along(near_share[tiles_dev:], TM, 1)
+    from_above = passed_along(near_share[: 2 * tiles_dev], TM, -1)
+    from_two_below = passed_along(upper, TM, 2)
+    from_two_above = passed_along(lower, TM, -2)
+    grad_window = jnp.concatenate(
+        [
+            lower + from_below[:tiles_dev] + from_two_below,
+            middle + from_below[tiles_dev:] + from_above[:tiles_dev],
+            upper + from_above[tiles_dev:] + from_two_above,
+        ],
+        axis=0,
     )
-    dir_share = precondition(grad_share, inverse_share)
-    slope_part = jnp.sum(grad_share * dir_share)
-    direction = collect(dir_share, WAFER, 2)
-    dir_window = with_halo(direction, ((TM, 0),), tiles_dev)
+    dir_window_share = precondition(grad_window, precond_window)
+    own = slice(tiles_dev, 2 * tiles_dev)
+    slope_part = jnp.sum(grad_window[own] * dir_window_share[own])
+    dir_window = collect(dir_window_share, WAFER, 2)
     dir_mt = transposed_window(dir_window, local_ids)
     rescanned = scan_call(dir_mt, slot, pix, cos_two, sin_two)
     curve_part = jnp.sum(weights[:, None] * rescanned * rescanned)
     totals = by_axis(jnp.stack([slope_part, curve_part]), ("wafer_1", "wafer_0", "tm_0", "tm_lo", "tm_hi"))
     step_size = totals[0] / totals[1]
-    new_map = sky_map + step_size * direction
+    new_map = sky_map + step_size * dir_window[own]
     new_residual = (resid - step_size * rescanned)[None]
     return (new_map, new_residual)
 

time: 202 us -> 212 us (1.050)
  the two profiles are of different devices: /device:TPU:8 before, /device:TPU:32 now
where the time goes in v4:
time: 212 us; the launch traced here: 211 us
  starting transfers between devices  51.2 us (24%)
  blocking collectives  49.6 us (23%)
  waiting for transfers between devices  39.9 us (19%)
  Pallas kernels  33.4 us (16%)
  local copies, waits for them, and re-layouts  19.7 us (9%)
  other arithmetic  14.5 us (7%)
  between operations  2.31 us (1%)
    psum x5, blocking collectives, by_axis(): return functools.reduce(lax.psum, axes, value)  49.6 us
    pallas_call x1, Pallas kernels, bin_call(): pl.pallas_call(bin_kernel, out_shape=(jax.ShapeDtypeStruct((dets, samp),...  23.1 us
    ppermute x4, starting transfers between devices, passed_along(): lax.ppermute(value, axis, [(i, (i + by) % count) for i in range(count)])  22.4 us
    all_to_all x1, waiting for transfers between devices, copy_for_each(): return lax.all_to_all(copies, axis, split_axis=0, concat_axis=0, tiled=True)  20.6 us
    ppermute x2, starting transfers between devices, with_halo(): lax.ppermute(lax.slice_in_dim(block, 0, width, axis=dim), axis, backward)  11.6 us
    pallas_call x1, Pallas kernels, scan_call(): pl.pallas_call(scan_kernel, out_shape=jax.ShapeDtypeStruct(slot.shape, jn...  10.3 us
    ppermute x2, starting transfers between devices, with_halo(): lax.ppermute(lax.slice_in_dim(block, block.shape[dim] - width, None, axis...  8.86 us
    all_to_all x1, waiting for transfers between devices, sum_at_owner(): parts = lax.all_to_all(in_blocks(value, dim, count), axis, 0, 0, tiled=True)  7.91 us
  transfers between devices with their start and end apart: 10, of which 7 were waited for; matrix products, arithmetic and copies ran while one was open for 2% of the time, Pallas kernels for 0%

profile of v4, /device:TPU:32, one launch (start us, length us, event | category | flops | bytes accessed | tf_op | source)
XLA Modules:
  0.0 210.6 jit_solution(3768668075007092555)
XLA Ops:
  0.6 0.0 copy-start
  0.6 1.3 copy.58
  2.0 3.8 %collective-permute-start = (f32[2,3,16384]{2,1,0:T(4,128)S(1)}, f32[2,3,16384]{2,1,0:T(4,128)S(1)}, u32[]{:S(2)}, u32[]{:S(2)}) collective-permute-start(f32[2,3,16384]{2,1,0:T(4,128)S(1)} %copy.58), channel_id=1, source_target_pairs={{0,8},{8,16},{16,24},{24,32},{32,40},{40,48},{48,56},{56,64},{64,7... | collective-permute-start | bytes 1179656 | tf_op jit(solution)/shard_map/ppermute | solution.py:22
  5.8 5.5 %collective-permute-start.1 = (f32[2,3,16384]{2,1,0:T(4,128)S(1)}, f32[2,3,16384]{2,1,0:T(4,128)}, u32[]{:S(2)}, u32[]{:S(2)}) collective-permute-start(f32[2,3,16384]{2,1,0:T(4,128)S(1)} %copy.58), channel_id=1, source_target_pairs={{8,0},{16,8},{24,16},{32,24},{40,32},{48,40},{56,48},{64,56},{72,6... | collective-permute-start | bytes 1179656 | tf_op jit(solution)/shard_map/ppermute | solution.py:25
  11.3 0.7 compare_and_fusion
  12.0 0.7 fusion.11
  12.6 1.5 sine_bitcast_fusion
  14.2 3.4 %collective-permute-done = f32[2,3,16384]{2,1,0:T(4,128)S(1)} collective-permute-done((f32[2,3,16384]{2,1,0:T(4,128)S(1)}, f32[2,3,16384]{2,1,0:T(4,128)S(1)}, u32[]{:S(2)}, u32[]{:S(2)}) %collective-permute-start) | collective-permute-done | bytes 393248 | tf_op jit(solution)/shard_map/ppermute | solution.py:22
  17.5 3.8 %collective-permute-done.1 = f32[2,3,16384]{2,1,0:T(4,128)} collective-permute-done((f32[2,3,16384]{2,1,0:T(4,128)S(1)}, f32[2,3,16384]{2,1,0:T(4,128)}, u32[]{:S(2)}, u32[]{:S(2)}) %collective-permute-start.1) | collective-permute-done | bytes 393248 | tf_op jit(solution)/shard_map/ppermute | solution.py:25
  21.4 1.4 pad_maximum_fusion
  22.8 1.2 gather_fusion
  24.0 0.3 broadcast_select_fusion.1
  24.3 0.6 reshape.132
  24.9 0.3 copy.62
  25.2 1.2 reshape.96.mt_ref
  26.4 23.1 %shard_map.95 = (f32[8,1024]{1,0:T(8,128)}, f32[4,3,128,128]{3,2,1,0:T(8,128)}) custom-call(f32[8]{0:T(128)} %bitcast.48, f32[3,128,512]{2,1,0:T(8,128)} %reshape.96.mt_ref, s32[8,1024]{1,0:T(8,128)} %bitcast.43, s32[8,1024]{1,0:T(8,128)} %bitcast.45, f32[8,1024]{1,0:T(8,128)} %get-tuple-element.23.cos_ref, f32[8,1024]{1,0:T(8,128)} %get-tuple-element.22.sin_ref, ...), custom_call_target="tpu_custom_call" | custom-call | tf_op jit(solution)/shard_map/pallas_call | solution.py:177
  49.5 1.5 reshape.133
  51.0 0.2 broadcast_in_dim.19
  51.2 1.6 scatter_fusion
  52.8 0.9 reshape.98
  53.8 2.0 copy.87
  55.7 4.5 %all-to-all-start = ((f32[8,6,3,2048]{3,2,1,0:T(4,128)}), f32[8,6,3,2048]{3,2,1,0:T(4,128)S(1)}, u32[]{:S(2)}, u32[]{:S(2)}) async-start(f32[8,6,3,2048]{3,2,1,0:T(4,128)} %bitcast.40), calls=%async_computation | async-start | bytes 3145728 | tf_op jit(solution)/shard_map/all_to_all | solution.py:43
  60.2 0.1 copy.81
  60.3 5.0 %collective-permute-start.4 = (f32[2,6,2048]{2,1,0:T(8,128)S(1)}, f32[2,6,2048]{2,1,0:T(8,128)S(1)}, u32[]{:S(2)}, u32[]{:S(2)}) collective-permute-start(f32[2,6,2048]{2,1,0:T(8,128)S(1)} %copy.81), channel_id=1, source_target_pairs={{0,8},{8,16},{16,24},{24,32},{32,40},{40,48},{48,56},{56,64},{64,7... | collective-permute-start | bytes 294920 | tf_op jit(solution)/shard_map/ppermute | solution.py:22
  65.4 6.2 %collective-permute-start.5 = (f32[2,6,2048]{2,1,0:T(8,128)S(1)}, f32[2,6,2048]{2,1,0:T(8,128)S(1)}, u32[]{:S(2)}, u32[]{:S(2)}) collective-permute-start(f32[2,6,2048]{2,1,0:T(8,128)S(1)} %copy.81), channel_id=1, source_target_pairs={{8,0},{16,8},{24,16},{32,24},{40,32},{48,40},{56,48},{64,56},{72,6... | collective-permute-start | bytes 294920 | tf_op jit(solution)/shard_map/ppermute | solution.py:25
  71.6 2.2 %collective-permute-done.4 = f32[2,6,2048]{2,1,0:T(8,128)S(1)} collective-permute-done((f32[2,6,2048]{2,1,0:T(8,128)S(1)}, f32[2,6,2048]{2,1,0:T(8,128)S(1)}, u32[]{:S(2)}, u32[]{:S(2)}) %collective-permute-start.4) | collective-permute-done | bytes 98336 | tf_op jit(solution)/shard_map/ppermute | solution.py:22
  73.8 0.1 copy_dynamic-update-slice_fusion
  73.8 7.9 %all-to-all-done = f32[8,6,3,2048]{3,2,1,0:T(4,128)S(1)} async-done(((f32[8,6,3,2048]{3,2,1,0:T(4,128)}), f32[8,6,3,2048]{3,2,1,0:T(4,128)S(1)}, u32[]{:S(2)}, u32[]{:S(2)}) %all-to-all-start) | async-done | bytes 1179680 | tf_op jit(solution)/shard_map/all_to_all | solution.py:43
  81.8 0.4 reduce_sum.27
  82.2 5.0 %collective-permute-start.2 = (f32[4,3,2048]{2,1,0:T(4,128)S(1)}, f32[4,3,2048]{2,1,0:T(4,128)S(1)}, u32[]{:S(2)}, u32[]{:S(2)}) collective-permute-start(f32[4,3,2048]{2,1,0:T(4,128)S(1)} %get-tuple-element.20), channel_id=1, source_target_pairs={{0,8},{8,16},{16,24},{24,32},{32,40},{40,48},{48,56},{56,64},{64,7... | collective-permute-start | bytes 294920 | tf_op jit(solution)/shard_map/ppermute | solution.py:32
  87.3 6.2 %collective-permute-start.3 = (f32[4,3,2048]{2,1,0:T(4,128)S(1)}, f32[4,3,2048]{2,1,0:T(4,128)S(1)}, u32[]{:S(2)}, u32[]{:S(2)}) collective-permute-start(f32[4,3,2048]{2,1,0:T(4,128)S(1)} %get-tuple-element.21), channel_id=1, source_target_pairs={{0,504},{8,0},{16,8},{24,16},{32,24},{40,32},{48,40},{56,48},{64,5... | collective-permute-start | bytes 294920 | tf_op jit(solution)/shard_map/ppermute | solution.py:32
  93.5 2.0 collective-permute-start.6
  95.5 9.2 %collective-permute-start.7 = (f32[2,3,2048]{2,1,0:T(4,128)S(1)}, f32[2,3,2048]{2,1,0:T(4,128)S(1)}, u32[]{:S(2)}, u32[]{:S(2)}) collective-permute-start(f32[2,3,2048]{2,1,0:T(4,128)S(1)} %get-tuple-element.19), channel_id=1, source_target_pairs={{0,496},{8,504},{16,0},{24,8},{32,16},{40,24},{48,32},{56,40},{64,... | collective-permute-start | bytes 147464 | tf_op jit(solution)/shard_map/ppermute | solution.py:32
  104.7 0.0 collective-permute-done.5
  104.7 0.3 collective-permute-done.6
  105.0 1.6 collective-permute-done.7
  106.6 0.1 fusion.2
  106.7 0.2 fusion.7
  106.9 0.3 fusion.5
  107.2 0.1 pad_maximum_fusion.1
  107.3 1.5 broadcast_in_dim.20
  108.8 3.8 %all-to-all-start.1 = ((f32[8,6,3,2048]{3,2,1,0:T(4,128)}), f32[8,6,3,2048]{3,2,1,0:T(4,128)S(1)}, u32[]{:S(2)}, u32[]{:S(2)}) async-start(f32[8,6,3,2048]{3,2,1,0:T(4,128)} %broadcast_in_dim.20), calls=%async_computation.1 | async-start | bytes 3145728 | tf_op jit(solution)/shard_map/all_to_all | solution.py:55
  112.6 0.7 fusion
  113.3 20.6 %all-to-all-done.1 = f32[8,6,3,2048]{3,2,1,0:T(4,128)S(1)} async-done(((f32[8,6,3,2048]{3,2,1,0:T(4,128)}), f32[8,6,3,2048]{3,2,1,0:T(4,128)S(1)}, u32[]{:S(2)}, u32[]{:S(2)}) %all-to-all-start.1) | async-done | bytes 1179680 | tf_op jit(solution)/shard_map/all_to_all | solution.py:55
  133.9 0.7 copy.88
  134.6 0.9 reshape.99
  135.5 2.1 gather_fusion.1
  137.6 1.5 broadcast_select_fusion
  139.1 1.5 reshape.134
  140.6 1.4 copy.70
  142.0 0.0 copy-start.3
  142.0 1.2 reshape.101.mt_ref
  143.2 10.3 %shard_map.96 = f32[8,1024]{1,0:T(8,128)} custom-call(f32[3,128,512]{2,1,0:T(8,128)} %reshape.101.mt_ref, s32[8,1024]{1,0:T(8,128)} %bitcast.44, s32[8,1024]{1,0:T(8,128)} %bitcast.46, f32[8,1024]{1,0:T(8,128)} %get-tuple-element.23.cos_ref, f32[8,1024]{1,0:T(8,128)} %get-tuple-element.22.sin_ref), custom_call_target="tpu_custom_call" | custom-call | tf_op jit(solution)/shard_map/pallas_call | solution.py:195
  153.5 1.4 fusion.8
  154.9 1.4 pad_maximum_fusion.6
  156.3 2.4 %psum.35 = f32[2]{0:T(128)S(1)} all-reduce(f32[2]{0:T(128)S(1)} %pad_maximum_fusion.6), channel_id=1, replica_groups=mesh['tm_0'=4,'tm_hi'=4,'tm_lo'=4,'wafer_0'=4,'wafer_1'=2] {'wafer_1'}, use_global_device_ids=true, to_apply=%region_4.6 | all-reduce | flops 2 | bytes 16 | tf_op jit(solution)/shard_map/psum | solution.py:63
  158.7 8.9 %psum.36 = f32[2]{0:T(128)S(1)} all-reduce(f32[2]{0:T(128)S(1)} %psum.35), channel_id=1, replica_groups=mesh['tm_0'=4,'tm_hi'=4,'tm_lo'=4,'wafer_0'=4,'wafer_1'=2] {'wafer_0'}, use_global_device_ids=true, to_apply=%region_5.7 | all-reduce | flops 2 | bytes 16 | tf_op jit(solution)/shard_map/psum | solution.py:63
  167.6 7.7 %psum.37 = f32[2]{0:T(128)S(1)} all-reduce(f32[2]{0:T(128)S(1)} %psum.36), channel_id=1, replica_groups=mesh['tm_0'=4,'tm_hi'=4,'tm_lo'=4,'wafer_0'=4,'wafer_1'=2] {'tm_0'}, use_global_device_ids=true, to_apply=%region_6.8 | all-reduce | flops 2 | bytes 16 | tf_op jit(solution)/shard_map/psum | solution.py:63
  175.3 13.0 %psum.38 = f32[2]{0:T(128)S(1)} all-reduce(f32[2]{0:T(128)S(1)} %psum.37), channel_id=1, replica_groups=mesh['tm_0'=4,'tm_hi'=4,'tm_lo'=4,'wafer_0'=4,'wafer_1'=2] {'tm_lo'}, use_global_device_ids=true, to_apply=%region_7.9 | all-reduce | flops 2 | bytes 16 | tf_op jit(solution)/shard_map/psum | solution.py:63
  188.4 17.6 %psum.39 = f32[2]{0:T(128)S(1)} all-reduce(f32[2]{0:T(128)S(1)} %psum.38), channel_id=1, replica_groups=mesh['tm_0'=4,'tm_hi'=4,'tm_lo'=4,'wafer_0'=4,'wafer_1'=2] {'tm_hi'}, use_global_device_ids=true, to_apply=%region_8.10 | all-reduce | flops 2 | bytes 16 | tf_op jit(solution)/shard_map/psum | solution.py:63
  205.9 0.6 fusion.14
  207.9 1.4 subtract_bitcast_fusion
  209.3 0.3 mul.109
  209.6 1.0 add.117
  (16 shorter events, 0.2 us)
Async XLA Ops:
  0.6 59.6 %copy-start = (f32[2,6,16384]{2,0,1:T(2,128)S(1)}, f32[2,6,16384]{2,0,1:T(2,128)}, u32[]{:S(2)}) copy-start(f32[2,6,16384]{2,0,1:T(2,128)} %param.17) | copy-start | bytes 2359300
  2.0 15.6 %collective-permute-start = (f32[2,3,16384]{2,1,0:T(4,128)S(1)}, f32[2,3,16384]{2,1,0:T(4,128)S(1)}, u32[]{:S(2)}, u32[]{:S(2)}) collective-permute-start(f32[2,3,16384]{2,1,0:T(4,128)S(1)} %copy.58), channel_id=1, source_target_pairs={{0,8},{8,16},{16,24},{24,32},{32,40},{40,48},{48,56},{56,64},{64,7... | collective-permute-start | bytes 1179656 | tf_op jit(solution)/shard_map/ppermute | solution.py:22
  5.8 15.6 %collective-permute-start.1 = (f32[2,3,16384]{2,1,0:T(4,128)S(1)}, f32[2,3,16384]{2,1,0:T(4,128)}, u32[]{:S(2)}, u32[]{:S(2)}) collective-permute-start(f32[2,3,16384]{2,1,0:T(4,128)S(1)} %copy.58), channel_id=1, source_target_pairs={{8,0},{16,8},{24,16},{32,24},{40,32},{48,40},{56,48},{64,56},{72,6... | collective-permute-start | bytes 1179656 | tf_op jit(solution)/shard_map/ppermute | solution.py:25
  55.7 26.0 %all-to-all-start = ((f32[8,6,3,2048]{3,2,1,0:T(4,128)}), f32[8,6,3,2048]{3,2,1,0:T(4,128)S(1)}, u32[]{:S(2)}, u32[]{:S(2)}) async-start(f32[8,6,3,2048]{3,2,1,0:T(4,128)} %bitcast.40), calls=%async_computation | async-start | bytes 3145728 | tf_op jit(solution)/shard_map/all_to_all | solution.py:43
  60.3 13.5 %collective-permute-start.4 = (f32[2,6,2048]{2,1,0:T(8,128)S(1)}, f32[2,6,2048]{2,1,0:T(8,128)S(1)}, u32[]{:S(2)}, u32[]{:S(2)}) collective-permute-start(f32[2,6,2048]{2,1,0:T(8,128)S(1)} %copy.81), channel_id=1, source_target_pairs={{0,8},{8,16},{16,24},{24,32},{32,40},{40,48},{48,56},{56,64},{64,7... | collective-permute-start | bytes 294920 | tf_op jit(solution)/shard_map/ppermute | solution.py:22
  65.4 39.3 %collective-permute-start.5 = (f32[2,6,2048]{2,1,0:T(8,128)S(1)}, f32[2,6,2048]{2,1,0:T(8,128)S(1)}, u32[]{:S(2)}, u32[]{:S(2)}) collective-permute-start(f32[2,6,2048]{2,1,0:T(8,128)S(1)} %copy.81), channel_id=1, source_target_pairs={{8,0},{16,8},{24,16},{32,24},{40,32},{48,40},{56,48},{64,56},{72,6... | collective-permute-start | bytes 294920 | tf_op jit(solution)/shard_map/ppermute | solution.py:25
  82.2 24.4 %collective-permute-start.2 = (f32[4,3,2048]{2,1,0:T(4,128)S(1)}, f32[4,3,2048]{2,1,0:T(4,128)S(1)}, u32[]{:S(2)}, u32[]{:S(2)}) collective-permute-start(f32[4,3,2048]{2,1,0:T(4,128)S(1)} %get-tuple-element.20), channel_id=1, source_target_pairs={{0,8},{8,16},{16,24},{24,32},{32,40},{40,48},{48,56},{56,64},{64,7... | collective-permute-start | bytes 294920 | tf_op jit(solution)/shard_map/ppermute | solution.py:32
  87.3 19.3 %collective-permute-start.3 = (f32[4,3,2048]{2,1,0:T(4,128)S(1)}, f32[4,3,2048]{2,1,0:T(4,128)S(1)}, u32[]{:S(2)}, u32[]{:S(2)}) collective-permute-start(f32[4,3,2048]{2,1,0:T(4,128)S(1)} %get-tuple-element.21), channel_id=1, source_target_pairs={{0,504},{8,0},{16,8},{24,16},{32,24},{40,32},{48,40},{56,48},{64,5... | collective-permute-start | bytes 294920 | tf_op jit(solution)/shard_map/ppermute | solution.py:32
  93.5 11.5 %collective-permute-start.6 = (f32[2,3,2048]{2,1,0:T(4,128)S(1)}, f32[2,3,2048]{2,1,0:T(4,128)S(1)}, u32[]{:S(2)}, u32[]{:S(2)}) collective-permute-start(f32[2,3,2048]{2,1,0:T(4,128)S(1)} %get-tuple-element.18), channel_id=1, source_target_pairs={{0,16},{8,24},{16,32},{24,40},{32,48},{40,56},{48,64},{56,72},{64,... | collective-permute-start | bytes 147464 | tf_op jit(solution)/shard_map/ppermute | solution.py:32
  95.5 11.1 %collective-permute-start.7 = (f32[2,3,2048]{2,1,0:T(4,128)S(1)}, f32[2,3,2048]{2,1,0:T(4,128)S(1)}, u32[]{:S(2)}, u32[]{:S(2)}) collective-permute-start(f32[2,3,2048]{2,1,0:T(4,128)S(1)} %get-tuple-element.19), channel_id=1, source_target_pairs={{0,496},{8,504},{16,0},{24,8},{32,16},{40,24},{48,32},{56,40},{64,... | collective-permute-start | bytes 147464 | tf_op jit(solution)/shard_map/ppermute | solution.py:32
  108.8 25.1 %all-to-all-start.1 = ((f32[8,6,3,2048]{3,2,1,0:T(4,128)}), f32[8,6,3,2048]{3,2,1,0:T(4,128)S(1)}, u32[]{:S(2)}, u32[]{:S(2)}) async-start(f32[8,6,3,2048]{3,2,1,0:T(4,128)} %broadcast_in_dim.20), calls=%async_computation.1 | async-start | bytes 3145728 | tf_op jit(solution)/shard_map/all_to_all | solution.py:55
  142.0 11.5 %copy-start.3 = (f32[1,8]{1,0:T(1,128)S(1)}, f32[1,8]{1,0:T(1,128)}, u32[]{:S(2)}) copy-start(f32[1,8]{1,0:T(1,128)} %param.11) | copy-start | bytes 100
  142.0 65.9 %copy-start.2 = (f32[8,1024]{1,0:T(8,128)S(1)}, f32[8,1024]{1,0:T(8,128)}, u32[]{:S(2)}) copy-start(f32[8,1024]{1,0:T(8,128)} %get-tuple-element.6) | copy-start | bytes 98308
  143.2 66.4 %copy-start.1 = (f32[2,3,16384]{2,0,1:T(2,128)S(1)}, f32[2,3,16384]{2,0,1:T(2,128)}, u32[]{:S(2)}) copy-start(f32[2,3,16384]{2,0,1:T(2,128)} %param.16) | copy-start | bytes 1179652

commit v5 on v4

--- a/solution.py
+++ b/solution.py
@@ -217,8 +217,13 @@
     share_width = pixels // wafers
     own_pixels = lax.axis_index(WAFER) * share_width
     precond_share = lax.dynamic_slice_in_dim(precond, own_pixels, share_width, 2)
-    precond_window = with_halo(precond_share, ((TM, 0),), tiles_dev)
-    window = with_halo(sky_map, ((TM, 0),), tiles_dev)
+    map_size = 3 * pixels
+    both = jnp.concatenate(
+        [sky_map.reshape(tiles_dev, map_size), precond_share.reshape(tiles_dev, -1)], axis=1
+    )
+    both_window = with_halo(both, ((TM, 0),), tiles_dev)
+    window = both_window[:, :map_size].reshape(3 * tiles_dev, 3, pixels)
+    precond_window = both_window[:, map_size:].reshape(3 * tiles_dev, 6, share_width)
     mt = transposed_window(window, local_ids)
     resid, binned = bin_call(weights, mt, slot, pix, cos_two, sin_two, timestream[0])
     partial_tiles = binned.reshape(binned.shape[0], 3, pixels)

time: 212 us -> 228 us (1.075)
  the two profiles are of different devices: /device:TPU:32 before, /device:TPU:8 now
where the time goes in v5:
time: 228 us; the launch traced here: 227 us
  blocking collectives  72.6 us (32%)
  starting transfers between devices  39.7 us (17%)
  waiting for transfers between devices  33.8 us (15%)
  Pallas kernels  33.4 us (15%)
  local copies, waits for them, and re-layouts  26.7 us (12%)
  other arithmetic  18.1 us (8%)
    psum x5, blocking collectives, by_axis(): return functools.reduce(lax.psum, axes, value)  47.6 us
    all_to_all x1, blocking collectives, sum_at_owner(): parts = lax.all_to_all(in_blocks(value, dim, count), axis, 0, 0, tiled=True)  25 us
    pallas_call x1, Pallas kernels, bin_call(): pl.pallas_call(bin_kernel, out_shape=(jax.ShapeDtypeStruct((dets, samp),...  23.1 us
    all_to_all x1, waiting for transfers between devices, copy_for_each(): return lax.all_to_all(copies, axis, split_axis=0, concat_axis=0, tiled=True)  19.5 us
    ppermute x4, starting transfers between devices, passed_along(): lax.ppermute(value, axis, [(i, (i + by) % count) for i in range(count)])  19.2 us
    ppermute x1, starting transfers between devices, with_halo(): lax.ppermute(lax.slice_in_dim(block, 0, width, axis=dim), axis, backward)  13.6 us
    pallas_call x1, Pallas kernels, scan_call(): pl.pallas_call(scan_kernel, out_shape=jax.ShapeDtypeStruct(slot.shape, jn...  10.3 us
    ppermute x1, waiting for transfers between devices, with_halo(): lax.ppermute(lax.slice_in_dim(block, block.shape[dim] - width, None, axis...  7.44 us
  transfers between devices with their start and end apart: 7, of which 4 were waited for; matrix products, arithmetic and copies ran while one was open for 2% of the time, Pallas kernels for 0%

profile of v5, /device:TPU:8, one launch (start us, length us, event | category | flops | bytes accessed | tf_op | source)
XLA Modules:
  0.0 226.8 jit_solution(15999541013023475415)
XLA Ops:
  0.6 0.0 copy-start
  0.6 0.0 copy-start.1
  0.7 1.1 copy-done
  1.8 1.2 pad_maximum_fusion.1
  3.0 13.6 %collective-permute-start.1 = (f32[2,61440]{1,0:T(2,128)S(1)}, f32[2,61440]{1,0:T(2,128)S(1)}, u32[]{:S(2)}, u32[]{:S(2)}) collective-permute-start(f32[2,61440]{1,0:T(2,128)S(1)} %pad_maximum_fusion.1), channel_id=1, source_target_pairs={{8,0},{16,8},{24,16},{32,24},{40,32},{48,40},{56,48},{64,56},{72,6... | collective-permute-start | bytes 1474568 | tf_op jit(solution)/shard_map/ppermute | solution.py:25
  16.6 1.9 collective-permute-start
  18.5 0.7 compare_and_fusion
  19.2 0.7 fusion.11
  19.9 1.5 sine_bitcast_fusion
  21.4 5.6 %collective-permute-done.1 = f32[2,61440]{1,0:T(2,128)S(1)} collective-permute-done((f32[2,61440]{1,0:T(2,128)S(1)}, f32[2,61440]{1,0:T(2,128)S(1)}, u32[]{:S(2)}, u32[]{:S(2)}) %collective-permute-start.1) | collective-permute-done | bytes 491552 | tf_op jit(solution)/shard_map/ppermute | solution.py:25
  27.1 7.4 %collective-permute-done = f32[2,61440]{1,0:T(2,128)S(1)} collective-permute-done((f32[2,61440]{1,0:T(2,128)S(1)}, f32[2,61440]{1,0:T(2,128)S(1)}, u32[]{:S(2)}, u32[]{:S(2)}) %collective-permute-start) | collective-permute-done | bytes 491552 | tf_op jit(solution)/shard_map/ppermute | solution.py:22
  34.5 0.8 copy-done.3
  35.3 0.6 pad_maximum_fusion
  35.9 0.1 slice.104
  36.0 2.0 reshape.109
  38.1 2.6 %gather_fusion = f32[4,3,16384]{2,1,0:T(4,128)S(1)} fusion(f32[6,3,16384]{2,1,0:T(4,128)} %reshape.109, s32[1024]{0:T(1024)S(1)} %pad_clamp_fusion), kind=kCustom, calls=%fused_computation.clone | custom fusion | bytes 1572880 | tf_op jit(solution)/shard_map/jit(_take)/gather | solution.py:163
  40.6 1.3 broadcast_select_fusion.1
  41.9 1.8 reshape.148
  43.7 0.3 copy.40
  44.0 1.2 reshape.111.mt_ref
  45.2 23.1 %shard_map.95 = (f32[8,1024]{1,0:T(8,128)}, f32[4,3,128,128]{3,2,1,0:T(8,128)}) custom-call(f32[8]{0:T(128)} %bitcast.56, f32[3,128,512]{2,1,0:T(8,128)} %reshape.111.mt_ref, s32[8,1024]{1,0:T(8,128)} %bitcast.51, s32[8,1024]{1,0:T(8,128)} %bitcast.53, f32[8,1024]{1,0:T(8,128)} %get-tuple-element.23.cos_ref, f32[8,1024]{1,0:T(8,128)} %get-tuple-element.22.sin_ref, ...), custom_call_target="tpu_custom_call" | custom-call | tf_op jit(solution)/shard_map/pallas_call | solution.py:177
  68.4 2.4 %reshape.149 = f32[4,3,16384]{2,1,0:T(4,128)} reshape(f32[4,3,128,128]{3,2,1,0:T(8,128)} %get-tuple-element.5) | data formatting | bytes 1572864 | tf_op jit(solution)/shard_map/reshape | solution.py:229
  70.7 0.2 broadcast_in_dim.19
  70.9 2.8 %scatter_fusion = f32[6,3,16384]{2,1,0:T(4,128)S(1)} fusion(f32[6,3,16384]{2,1,0:T(4,128)S(1)} %broadcast_in_dim.19, s32[4]{0:T(128)S(1)} %fusion.11, f32[4,3,16384]{2,1,0:T(4,128)} %reshape.149), kind=kCustom, calls=%fused_computation.2 | custom fusion | flops 196608 | bytes 2359312 | tf_op jit(solution)/shard_map/scatter-add | solution.py:230
  73.7 1.7 reshape.113
  75.4 2.1 copy.55
  77.5 25.0 %all_to_all.10 = f32[8,6,3,2048]{3,2,1,0:T(4,128)S(1)} all-to-all(f32[8,6,3,2048]{3,2,1,0:T(4,128)S(1)} %bitcast.42), channel_id=1, replica_groups=mesh['tm_0'=4,'tm_hi'=4,'tm_lo'=4,'wafer_0'=4,'wafer_1'=2] {'wafer_0','w..., dimensions={0} | all-to-all | bytes 2359296 | tf_op jit(solution)/shard_map/all_to_all | solution.py:43
  102.5 0.4 reduce_sum.27
  103.0 1.9 collective-permute-start.4
  104.9 8.1 %collective-permute-start.5 = (f32[2,3,2048]{2,1,0:T(4,128)S(1)}, f32[2,3,2048]{2,1,0:T(4,128)S(1)}, u32[]{:S(2)}, u32[]{:S(2)}) collective-permute-start(f32[2,3,2048]{2,1,0:T(4,128)S(1)} %get-tuple-element.19), channel_id=1, source_target_pairs={{0,496},{8,504},{16,0},{24,8},{32,16},{40,24},{48,32},{56,40},{64,... | collective-permute-start | bytes 147464 | tf_op jit(solution)/shard_map/ppermute | solution.py:32
  113.1 1.9 collective-permute-start.2
  115.0 7.2 %collective-permute-start.3 = (f32[4,3,2048]{2,1,0:T(4,128)S(1)}, f32[4,3,2048]{2,1,0:T(4,128)S(1)}, u32[]{:S(2)}, u32[]{:S(2)}) collective-permute-start(f32[4,3,2048]{2,1,0:T(4,128)S(1)} %get-tuple-element.21), channel_id=1, source_target_pairs={{0,504},{8,0},{16,8},{24,16},{32,24},{40,32},{48,40},{56,48},{64,5... | collective-permute-start | bytes 294920 | tf_op jit(solution)/shard_map/ppermute | solution.py:32
  122.2 1.0 pad_maximum_fusion.2
  123.3 0.2 reshape.114
  123.4 0.0 collective-permute-done.5
  123.5 1.3 collective-permute-done.3
  124.7 0.1 fusion.2
  124.8 0.2 fusion.7
  125.0 0.3 fusion.5
  125.3 0.1 pad_maximum_fusion.3
  125.4 1.5 broadcast_in_dim.20
  126.9 5.0 %all-to-all-start.1 = ((f32[8,6,3,2048]{3,2,1,0:T(4,128)}), f32[8,6,3,2048]{3,2,1,0:T(4,128)S(1)}, u32[]{:S(2)}, u32[]{:S(2)}) async-start(f32[8,6,3,2048]{3,2,1,0:T(4,128)} %broadcast_in_dim.20), calls=%async_computation.1 | async-start | bytes 3145728 | tf_op jit(solution)/shard_map/all_to_all | solution.py:55
  131.9 0.7 fusion
  132.6 19.5 %all-to-all-done.1 = f32[8,6,3,2048]{3,2,1,0:T(4,128)S(1)} async-done(((f32[8,6,3,2048]{3,2,1,0:T(4,128)}), f32[8,6,3,2048]{3,2,1,0:T(4,128)S(1)}, u32[]{:S(2)}, u32[]{:S(2)}) %all-to-all-start.1) | async-done | bytes 1179680 | tf_op jit(solution)/shard_map/all_to_all | solution.py:55
  152.0 0.7 copy.56
  152.7 0.9 reshape.115
  153.6 2.1 gather_fusion.1
  155.7 1.5 broadcast_select_fusion
  157.3 1.5 reshape.150
  158.7 1.4 copy.46
  160.2 0.0 copy-start.5
  160.2 1.2 reshape.117.mt_ref
  161.4 10.3 %shard_map.96 = f32[8,1024]{1,0:T(8,128)} custom-call(f32[3,128,512]{2,1,0:T(8,128)} %reshape.117.mt_ref, s32[8,1024]{1,0:T(8,128)} %bitcast.52, s32[8,1024]{1,0:T(8,128)} %bitcast.54, f32[8,1024]{1,0:T(8,128)} %get-tuple-element.23.cos_ref, f32[8,1024]{1,0:T(8,128)} %get-tuple-element.22.sin_ref), custom_call_target="tpu_custom_call" | custom-call | tf_op jit(solution)/shard_map/pallas_call | solution.py:195
  171.7 1.4 fusion.8
  173.1 1.3 pad_maximum_fusion.8
  174.4 2.4 %psum.35 = f32[2]{0:T(128)S(1)} all-reduce(f32[2]{0:T(128)S(1)} %pad_maximum_fusion.8), channel_id=1, replica_groups=mesh['tm_0'=4,'tm_hi'=4,'tm_lo'=4,'wafer_0'=4,'wafer_1'=2] {'wafer_1'}, use_global_device_ids=true, to_apply=%region_4.6 | all-reduce | flops 2 | bytes 16 | tf_op jit(solution)/shard_map/psum | solution.py:63
  176.9 9.1 %psum.36 = f32[2]{0:T(128)S(1)} all-reduce(f32[2]{0:T(128)S(1)} %psum.35), channel_id=1, replica_groups=mesh['tm_0'=4,'tm_hi'=4,'tm_lo'=4,'wafer_0'=4,'wafer_1'=2] {'wafer_0'}, use_global_device_ids=true, to_apply=%region_5.7 | all-reduce | flops 2 | bytes 16 | tf_op jit(solution)/shard_map/psum | solution.py:63
  186.0 7.7 %psum.37 = f32[2]{0:T(128)S(1)} all-reduce(f32[2]{0:T(128)S(1)} %psum.36), channel_id=1, replica_groups=mesh['tm_0'=4,'tm_hi'=4,'tm_lo'=4,'wafer_0'=4,'wafer_1'=2] {'tm_0'}, use_global_device_ids=true, to_apply=%region_6.8 | all-reduce | flops 2 | bytes 16 | tf_op jit(solution)/shard_map/psum | solution.py:63
  193.7 8.4 %psum.38 = f32[2]{0:T(128)S(1)} all-reduce(f32[2]{0:T(128)S(1)} %psum.37), channel_id=1, replica_groups=mesh['tm_0'=4,'tm_hi'=4,'tm_lo'=4,'wafer_0'=4,'wafer_1'=2] {'tm_lo'}, use_global_device_ids=true, to_apply=%region_7.9 | all-reduce | flops 2 | bytes 16 | tf_op jit(solution)/shard_map/psum | solution.py:63
  202.1 20.0 %psum.39 = f32[2]{0:T(128)S(1)} all-reduce(f32[2]{0:T(128)S(1)} %psum.38), channel_id=1, replica_groups=mesh['tm_0'=4,'tm_hi'=4,'tm_lo'=4,'wafer_0'=4,'wafer_1'=2] {'tm_hi'}, use_global_device_ids=true, to_apply=%region_8.10 | all-reduce | flops 2 | bytes 16 | tf_op jit(solution)/shard_map/psum | solution.py:63
  222.1 0.6 fusion.14
  224.0 1.4 subtract_bitcast_fusion
  225.5 0.3 mul.109
  225.8 1.0 add.117
  (15 shorter events, 0.2 us)
Async XLA Ops:
  0.6 1.1 copy-start
  0.6 34.6 %copy-start.1 = (f32[2,3,16384]{2,0,1:T(2,128)S(1)}, f32[2,3,16384]{2,0,1:T(2,128)}, u32[]{:S(2)}) copy-start(f32[2,3,16384]{2,0,1:T(2,128)} %param.16) | copy-start | bytes 1179652
  3.0 24.1 %collective-permute-start.1 = (f32[2,61440]{1,0:T(2,128)S(1)}, f32[2,61440]{1,0:T(2,128)S(1)}, u32[]{:S(2)}, u32[]{:S(2)}) collective-permute-start(f32[2,61440]{1,0:T(2,128)S(1)} %pad_maximum_fusion.1), channel_id=1, source_target_pairs={{8,0},{16,8},{24,16},{32,24},{40,32},{48,40},{56,48},{64,56},{72,6... | collective-permute-start | bytes 1474568 | tf_op jit(solution)/shard_map/ppermute | solution.py:25
  16.6 17.9 %collective-permute-start = (f32[2,61440]{1,0:T(2,128)S(1)}, f32[2,61440]{1,0:T(2,128)S(1)}, u32[]{:S(2)}, u32[]{:S(2)}) collective-permute-start(f32[2,61440]{1,0:T(2,128)S(1)} %pad_maximum_fusion.1), channel_id=1, source_target_pairs={{0,8},{8,16},{16,24},{24,32},{32,40},{40,48},{48,56},{56,64},{64,7... | collective-permute-start | bytes 1474568 | tf_op jit(solution)/shard_map/ppermute | solution.py:22
  34.5 0.8 copy-start.3
  103.0 20.4 %collective-permute-start.4 = (f32[2,3,2048]{2,1,0:T(4,128)S(1)}, f32[2,3,2048]{2,1,0:T(4,128)S(1)}, u32[]{:S(2)}, u32[]{:S(2)}) collective-permute-start(f32[2,3,2048]{2,1,0:T(4,128)S(1)} %get-tuple-element.18), channel_id=1, source_target_pairs={{0,16},{8,24},{16,32},{24,40},{32,48},{40,56},{48,64},{56,72},{64,... | collective-permute-start | bytes 147464 | tf_op jit(solution)/shard_map/ppermute | solution.py:32
  104.9 18.5 %collective-permute-start.5 = (f32[2,3,2048]{2,1,0:T(4,128)S(1)}, f32[2,3,2048]{2,1,0:T(4,128)S(1)}, u32[]{:S(2)}, u32[]{:S(2)}) collective-permute-start(f32[2,3,2048]{2,1,0:T(4,128)S(1)} %get-tuple-element.19), channel_id=1, source_target_pairs={{0,496},{8,504},{16,0},{24,8},{32,16},{40,24},{48,32},{56,40},{64,... | collective-permute-start | bytes 147464 | tf_op jit(solution)/shard_map/ppermute | solution.py:32
  113.1 10.4 %collective-permute-start.2 = (f32[4,3,2048]{2,1,0:T(4,128)S(1)}, f32[4,3,2048]{2,1,0:T(4,128)S(1)}, u32[]{:S(2)}, u32[]{:S(2)}) collective-permute-start(f32[4,3,2048]{2,1,0:T(4,128)S(1)} %get-tuple-element.20), channel_id=1, source_target_pairs={{0,8},{8,16},{16,24},{24,32},{32,40},{40,48},{48,56},{56,64},{64,7... | collective-permute-start | bytes 294920 | tf_op jit(solution)/shard_map/ppermute | solution.py:32
  115.0 9.7 %collective-permute-start.3 = (f32[4,3,2048]{2,1,0:T(4,128)S(1)}, f32[4,3,2048]{2,1,0:T(4,128)S(1)}, u32[]{:S(2)}, u32[]{:S(2)}) collective-permute-start(f32[4,3,2048]{2,1,0:T(4,128)S(1)} %get-tuple-element.21), channel_id=1, source_target_pairs={{0,504},{8,0},{16,8},{24,16},{32,24},{40,32},{48,40},{56,48},{64,5... | collective-permute-start | bytes 294920 | tf_op jit(solution)/shard_map/ppermute | solution.py:32
  126.9 25.1 %all-to-all-start.1 = ((f32[8,6,3,2048]{3,2,1,0:T(4,128)}), f32[8,6,3,2048]{3,2,1,0:T(4,128)S(1)}, u32[]{:S(2)}, u32[]{:S(2)}) async-start(f32[8,6,3,2048]{3,2,1,0:T(4,128)} %broadcast_in_dim.20), calls=%async_computation.1 | async-start | bytes 3145728 | tf_op jit(solution)/shard_map/all_to_all | solution.py:55
  160.2 11.5 %copy-start.5 = (f32[1,8]{1,0:T(1,128)S(1)}, f32[1,8]{1,0:T(1,128)}, u32[]{:S(2)}) copy-start(f32[1,8]{1,0:T(1,128)} %param.11) | copy-start | bytes 100
  160.2 63.9 %copy-start.4 = (f32[8,1024]{1,0:T(8,128)S(1)}, f32[8,1024]{1,0:T(8,128)}, u32[]{:S(2)}) copy-start(f32[8,1024]{1,0:T(8,128)} %get-tuple-element.6) | copy-start | bytes 98308
  161.4 64.4 %copy-start.2 = (f32[2,3,16384]{2,0,1:T(2,128)S(1)}, f32[2,3,16384]{2,0,1:T(2,128)}, u32[]{:S(2)}) copy-start(f32[2,3,16384]{2,0,1:T(2,128)} %param.16) | copy-start | bytes 1179652

commit v6 on v3

--- a/solution.py
+++ b/solution.py
@@ -94,11 +94,14 @@
     return ids == col
 
 
-def stacked_map(mt_ref, lhs_ref):
-    hi, lo = split2(mt_ref[...])
-    for comp in range(3):
-        lhs_ref[comp * SIDE:(comp + 1) * SIDE, :] = hi[comp]
-        lhs_ref[(3 + comp) * SIDE:(4 + comp) * SIDE, :] = lo[comp]
+def stacked_map(ids_ref, win_ref, lhs_ref):
+    for s in range(ids_ref.shape[0]):
+        tile_id = ids_ref[s]
+        for comp in range(3):
+            hi, lo = split2(win_ref[tile_id, comp].T)
+            cols = slice(s * SIDE, (s + 1) * SIDE)
+            lhs_ref[comp * SIDE:(comp + 1) * SIDE, cols] = hi
+            lhs_ref[(3 + comp) * SIDE:(4 + comp) * SIDE, cols] = lo
 
 
 def sampled(lhs_ref, at, mask):
@@ -110,11 +113,11 @@
     return values
 
 
-def bin_kernel(w_ref, mt_ref, slot_ref, pix_ref, cos_ref, sin_ref, ts_ref, resid_ref, g_ref,
+def bin_kernel(ids_ref, w_ref, win_ref, slot_ref, pix_ref, cos_ref, sin_ref, ts_ref, resid_ref, g_ref,
                lhs_ref, rhs_ref, acc_ref):
-    stacked_map(mt_ref, lhs_ref)
+    stacked_map(ids_ref, win_ref, lhs_ref)
     acc_ref[...] = jnp.zeros(acc_ref.shape, jnp.float32)
-    rows = mt_ref.shape[2]
+    rows = lhs_ref.shape[1]
     nt = (((1,), (1,)), ((), ()))
 
     def body(d, carry):
@@ -136,16 +139,17 @@
         return carry
 
     lax.fori_loop(0, slot_ref.shape[0], body, 0)
-    for s in range(g_ref.shape[0]):
+    g_ref[...] = jnp.zeros(g_ref.shape, jnp.float32)
+    for s in range(ids_ref.shape[0]):
         for comp in range(3):
             rows_s = slice(s * SIDE, (s + 1) * SIDE)
-            g_ref[s, comp] = (acc_ref[rows_s, comp * SIDE:(comp + 1) * SIDE]
+            g_ref[ids_ref[s], comp] = (acc_ref[rows_s, comp * SIDE:(comp + 1) * SIDE]
                               + acc_ref[rows_s, (3 + comp) * SIDE:(4 + comp) * SIDE])
 
 
-def scan_kernel(mt_ref, slot_ref, pix_ref, cos_ref, sin_ref, out_ref, lhs_ref):
-    stacked_map(mt_ref, lhs_ref)
-    rows = mt_ref.shape[2]
+def scan_kernel(ids_ref, win_ref, slot_ref, pix_ref, cos_ref, sin_ref, out_ref, lhs_ref):
+    stacked_map(ids_ref, win_ref, lhs_ref)
+    rows = lhs_ref.shape[1]
 
     def body(d, carry):
         slot = slot_ref[pl.ds(d, 1), :]
@@ -159,46 +163,45 @@
     lax.fori_loop(0, slot_ref.shape[0], body, 0)
 
 
-def transposed_window(window, local_ids):
-    hits = jnp.take(window, local_ids, axis=0)
-    count = hits.shape[0]
-    grid = hits.reshape(count, 3, SIDE, SIDE)
-    return jnp.transpose(grid, (1, 3, 0, 2)).reshape(3, SIDE, count * SIDE)
-
-
 VMEM = pltpu.MemorySpace.VMEM
 
 
-def bin_call(weights, mt, slot, pix, cos_two, sin_two, ts):
+def bin_call(local_ids, weights, win, slot, pix, cos_two, sin_two, ts):
     dets, samp = slot.shape
-    hits = mt.shape[2] // SIDE
+    hits = local_ids.shape[0]
     smem = pl.BlockSpec(memory_space=pltpu.SMEM)
     vmem = pl.BlockSpec(memory_space=VMEM)
     return pl.pallas_call(
         bin_kernel,
         out_shape=(
             jax.ShapeDtypeStruct((dets, samp), jnp.float32),
-            jax.ShapeDtypeStruct((hits, 3, SIDE, SIDE), jnp.float32),
+            jax.ShapeDtypeStruct(win.shape, jnp.float32),
         ),
-        in_specs=[smem] + [vmem] * 6,
+        in_specs=[smem, smem] + [vmem] * 6,
         out_specs=(vmem, vmem),
         scratch_shapes=[
             pltpu.VMEM((6 * SIDE, hits * SIDE), jnp.bfloat16),
             pltpu.VMEM((6 * SIDE, samp), jnp.bfloat16),
             pltpu.VMEM((hits * SIDE, 6 * SIDE), jnp.float32),
         ],
-    )(weights, mt, slot, pix, cos_two, sin_two, ts)
-
-
-def scan_call(mt, slot, pix, cos_two, sin_two):
+    )(local_ids, weights, win, slot, pix, cos_two, sin_two, ts)
+
+
+def scan_call(local_ids, win, slot, pix, cos_two, sin_two):
+    hits = local_ids.shape[0]
+    smem = pl.BlockSpec(memory_space=pltpu.SMEM)
     vmem = pl.BlockSpec(memory_space=VMEM)
     return pl.pallas_call(
         scan_kernel,
         out_shape=jax.ShapeDtypeStruct(slot.shape, jnp.float32),
-        in_specs=[vmem] * 5,
+        in_specs=[smem] + [vmem] * 5,
         out_specs=vmem,
-        scratch_shapes=[pltpu.VMEM((6 * SIDE, mt.shape[2]), jnp.bfloat16)],
-    )(mt, slot, pix, cos_two, sin_two)
+        scratch_shapes=[pltpu.VMEM((6 * SIDE, hits * SIDE), jnp.bfloat16)],
+    )(local_ids, win, slot, pix, cos_two, sin_two)
+
+
+def as_grid(tiles):
+    return tiles.reshape(tiles.shape[0], 3, SIDE, SIDE)
 
 
 def local(timestream, noise_weight, hit_slot, tile_pixel, pol_angle, hit_tiles, sky_map, precond):
@@ -213,11 +216,9 @@
     weights = noise_weight[0]
     slot = hit_slot[0]
     pix = tile_pixel[0]
-    window = with_halo(sky_map, ((TM, 0),), tiles_dev)
-    mt = transposed_window(window, local_ids)
-    resid, binned = bin_call(weights, mt, slot, pix, cos_two, sin_two, timestream[0])
-    partial_tiles = binned.reshape(binned.shape[0], 3, pixels)
-    near_tiles = jnp.zeros((3 * tiles_dev, 3, pixels), jnp.float32).at[local_ids].add(partial_tiles)
+    window = with_halo(as_grid(sky_map), ((TM, 0),), tiles_dev)
+    resid, binned = bin_call(local_ids, weights, window, slot, pix, cos_two, sin_two, timestream[0])
+    near_tiles = binned.reshape(binned.shape[0], 3, pixels)
     from_upper = passed_along(near_tiles[:tiles_dev], TM, -1)
     from_lower = passed_along(near_tiles[2 * tiles_dev :], TM, 1)
     owned_tiles = near_tiles[tiles_dev : 2 * tiles_dev] + from_upper + from_lower
@@ -229,9 +230,8 @@
     dir_share = precondition(grad_share, inverse_share)
     slope_part = jnp.sum(grad_share * dir_share)
     direction = collect(dir_share, WAFER, 2)
-    dir_window = with_halo(direction, ((TM, 0),), tiles_dev)
-    dir_mt = transposed_window(dir_window, local_ids)
-    rescanned = scan_call(dir_mt, slot, pix, cos_two, sin_two)
+    dir_window = with_halo(as_grid(direction), ((TM, 0),), tiles_dev)
+    rescanned = scan_call(local_ids, dir_window, slot, pix, cos_two, sin_two)
     curve_part = jnp.sum(weights[:, None] * rescanned * rescanned)
     totals = by_axis(jnp.stack([slope_part, curve_part]), ("wafer_1", "wafer_0", "tm_0", "tm_lo", "tm_hi"))
     step_size = totals[0] / totals[1]

time: 202 us -> 187 us (0.926)
  blocking collectives: 59 us -> 52.7 us
  local copies, waits for them, and re-layouts: 12.1 us -> 6.64 us
    ppermute x2, waiting for transfers between devices: 15.8 us -> 6.66 us  [passed_along(): lax.ppermute(value, axis, [(i, (i + by) % count) for i in range(count)])]
    ppermute x2, waiting for transfers between devices: 2.36 us -> 11.3 us  [with_halo(): lax.ppermute(lax.slice_in_dim(block, 0, width, axis=dim), axis, backward)]
    psum x5, blocking collectives: 47.7 us -> 41.4 us  [by_axis(): return functools.reduce(lax.psum, axes, value)]
    reshape x7 -> x2, local copies, waits for them, and re-layouts: 5.34 us -> 1.37 us  [as_grid(): return tiles.reshape(tiles.shape[0], 3, SIDE, SIDE)]
    gather x2 -> x0, local copies, waits for them, and re-layouts: 2.35 us -> none  [transposed_window(): hits = jnp.take(window, local_ids, axis=0)]
    ppermute x2, starting transfers between devices: 19.1 us -> 21.3 us  [with_halo(): lax.ppermute(lax.slice_in_dim(block, 0, width, axis=dim), axis, backward)]
where the time goes in v6:
time: 187 us; the launch traced here: 186 us
  blocking collectives  52.7 us (28%)
  waiting for transfers between devices  40.3 us (22%)
  starting transfers between devices  39.2 us (21%)
  Pallas kernels  34.1 us (18%)
  other arithmetic  10.9 us (6%)
  local copies, waits for them, and re-layouts  6.64 us (4%)
  between operations  2.1 us (1%)
    psum x5, blocking collectives, by_axis(): return functools.reduce(lax.psum, axes, value)  41.4 us
    pallas_call x1, Pallas kernels, bin_call(): pl.pallas_call(bin_kernel, out_shape=(jax.ShapeDtypeStruct((dets, samp),...  23.6 us
    ppermute x2, starting transfers between devices, with_halo(): lax.ppermute(lax.slice_in_dim(block, 0, width, axis=dim), axis, backward)  21.3 us
    ppermute x2, waiting for transfers between devices, with_halo(): lax.ppermute(lax.slice_in_dim(block, block.shape[dim] - width, None, axis...  14.9 us
    all_to_all x1, blocking collectives, copy_for_each(): return lax.all_to_all(copies, axis, split_axis=0, concat_axis=0, tiled=True)  11.3 us
    ppermute x2, waiting for transfers between devices, with_halo(): lax.ppermute(lax.slice_in_dim(block, 0, width, axis=dim), axis, backward)  11.3 us
    pallas_call x1, Pallas kernels, scan_call(): pl.pallas_call(scan_kernel, out_shape=jax.ShapeDtypeStruct(slot.shape, jn...  10.5 us
    ppermute x2, starting transfers between devices, passed_along(): lax.ppermute(value, axis, [(i, (i + by) % count) for i in range(count)])  9.16 us
  transfers between devices with their start and end apart: 7, of which 7 were waited for; matrix products, arithmetic and copies ran while one was open for 1% of the time, Pallas kernels for 0%

profile of v6, /device:TPU:8, one launch (start us, length us, event | category | flops | bytes accessed | tf_op | source)
XLA Modules:
  0.0 186.0 jit_solution(3316250463283514573)
XLA Ops:
  0.6 0.0 copy-start.4
  0.6 0.0 copy-start.1
  0.6 1.3 reshape.25
  2.0 13.6 %collective-permute-start.1 = (f32[2,3,128,128]{3,2,1,0:T(8,128)S(1)}, f32[2,3,128,128]{3,2,1,0:T(8,128)S(1)}, u32[]{:S(2)}, u32[]{:S(2)}) collective-permute-start(f32[2,3,128,128]{3,2,1,0:T(8,128)S(1)} %copy.49), channel_id=1, source_target_pairs={{8,0},{16,8},{24,16},{32,24},{40,32},{48,40},{56,48},{64,56},{72,6... | collective-permute-start | bytes 1179656 | tf_op jit(solution)/shard_map/ppermute | solution.py:25
  15.6 1.9 %collective-permute-start = (f32[2,3,128,128]{3,2,1,0:T(8,128)S(1)}, f32[2,3,128,128]{3,2,1,0:T(8,128)S(1)}, u32[]{:S(2)}, u32[]{:S(2)}) collective-permute-start(f32[2,3,128,128]{3,2,1,0:T(8,128)S(1)} %copy.49), channel_id=1, source_target_pairs={{0,8},{8,16},{16,24},{24,32},{32,40},{40,48},{48,56},{56,64},{64,7... | collective-permute-start | bytes 1179656 | tf_op jit(solution)/shard_map/ppermute | solution.py:22
  17.6 0.0 copy-done.4
  17.6 0.6 and_select_fusion.ids_ref
  18.2 0.0 copy-done.1
  18.2 0.8 sine_bitcast_fusion
  18.9 5.1 %collective-permute-done.1 = f32[2,3,128,128]{3,2,1,0:T(8,128)S(1)} collective-permute-done((f32[2,3,128,128]{3,2,1,0:T(8,128)S(1)}, f32[2,3,128,128]{3,2,1,0:T(8,128)S(1)}, u32[]{:S(2)}, u32[]{:S(2)}) %collective-permute-start.1) | collective-permute-done | bytes 393248 | tf_op jit(solution)/shard_map/ppermute | solution.py:25
  24.0 7.4 %collective-permute-done = f32[2,3,128,128]{3,2,1,0:T(8,128)S(1)} collective-permute-done((f32[2,3,128,128]{3,2,1,0:T(8,128)S(1)}, f32[2,3,128,128]{3,2,1,0:T(8,128)S(1)}, u32[]{:S(2)}, u32[]{:S(2)}) %collective-permute-start) | collective-permute-done | bytes 393248 | tf_op jit(solution)/shard_map/ppermute | solution.py:22
  31.4 1.1 pad_maximum_fusion.win_ref
  32.5 23.6 %shard_map.95 = (f32[8,1024]{1,0:T(8,128)}, f32[6,3,128,128]{3,2,1,0:T(8,128)}) custom-call(s32[4]{0:T(128)} %and_select_fusion.ids_ref, f32[8]{0:T(128)} %bitcast.50, f32[6,3,128,128]{3,2,1,0:T(8,128)} %pad_maximum_fusion.win_ref, s32[8,1024]{1,0:T(8,128)} %bitcast.45, s32[8,1024]{1,0:T(8,128)} %bitcast.47, f32[8,1024]{1,0:T(8,128)} %get-tuple-element.15.cos_ref, ...), custom_call_target="tpu_custom_call" | custom-call | tf_op jit(solution)/shard_map/pallas_call | solution.py:174
  56.1 1.3 fusion.7
  57.5 0.2 slice.57
  57.7 0.2 slice.59
  58.0 1.9 %collective-permute-start.3 = (f32[2,3,16384]{2,0,1:T(2,128)S(1)}, f32[2,3,16384]{2,0,1:T(2,128)S(1)}, u32[]{:S(2)}, u32[]{:S(2)}) collective-permute-start(f32[2,3,16384]{2,0,1:T(2,128)S(1)} %slice.59), channel_id=1, source_target_pairs={{0,8},{8,16},{16,24},{24,32},{32,40},{40,48},{48,56},{56,64},{64,7... | collective-permute-start | bytes 1179656 | tf_op jit(solution)/shard_map/ppermute | solution.py:32
  59.9 7.2 %collective-permute-start.2 = (f32[2,3,16384]{2,0,1:T(2,128)S(1)}, f32[2,3,16384]{2,0,1:T(2,128)S(1)}, u32[]{:S(2)}, u32[]{:S(2)}) collective-permute-start(f32[2,3,16384]{2,0,1:T(2,128)S(1)} %slice.57), channel_id=1, source_target_pairs={{0,504},{8,0},{16,8},{24,16},{32,24},{40,32},{48,40},{56,48},{64,5... | collective-permute-start | bytes 1179656 | tf_op jit(solution)/shard_map/ppermute | solution.py:32
  67.2 0.2 slice.55
  67.4 5.5 %collective-permute-done.3 = f32[2,3,16384]{2,0,1:T(2,128)S(1)} collective-permute-done((f32[2,3,16384]{2,0,1:T(2,128)S(1)}, f32[2,3,16384]{2,0,1:T(2,128)S(1)}, u32[]{:S(2)}, u32[]{:S(2)}) %collective-permute-start.3) | collective-permute-done | bytes 393248 | tf_op jit(solution)/shard_map/ppermute | solution.py:32
  72.9 1.2 collective-permute-done.2
  74.1 0.3 add_add_fusion
  74.4 0.3 reshape.26
  74.7 1.1 copy.55
  75.8 4.9 %all-to-all-start = ((f32[8,2,3,2048]{3,1,2,0:T(2,128)}), f32[8,2,3,2048]{3,1,2,0:T(2,128)S(1)}, u32[]{:S(2)}, u32[]{:S(2)}) async-start(f32[8,2,3,2048]{3,1,2,0:T(2,128)} %copy.55), calls=%async_computation | async-start | bytes 786432 | tf_op jit(solution)/shard_map/all_to_all | solution.py:43
  80.7 7.5 %all-to-all-done = f32[8,2,3,2048]{3,1,2,0:T(2,128)S(1)} async-done(((f32[8,2,3,2048]{3,1,2,0:T(2,128)}), f32[8,2,3,2048]{3,1,2,0:T(2,128)S(1)}, u32[]{:S(2)}, u32[]{:S(2)}) %all-to-all-start) | async-done | bytes 393248 | tf_op jit(solution)/shard_map/all_to_all | solution.py:43
  88.1 0.1 reduce_sum.27
  88.3 0.9 fusion.5
  89.1 0.7 multiply_reduce_fusion
  89.9 0.2 broadcast_in_dim.6
  90.0 11.3 %all_to_all.10 = f32[8,2,3,2048]{3,1,2,0:T(2,128)S(1)} all-to-all(f32[8,2,3,2048]{3,1,2,0:T(2,128)S(1)} %broadcast_in_dim.6), channel_id=1, replica_groups=mesh['tm_0'=4,'tm_hi'=4,'tm_lo'=4,'wafer_0'=4,'wafer_1'=2] {'wafer_0','w..., dimensions={0} | all-to-all | bytes 786432 | tf_op jit(solution)/shard_map/all_to_all | solution.py:55
  101.3 0.2 copy.63
  101.6 0.1 reshape_reshape.3
  101.6 7.7 %collective-permute-start.5 = (f32[2,3,128,128]{3,2,1,0:T(8,128)S(1)}, f32[2,3,128,128]{3,2,1,0:T(8,128)S(1)}, u32[]{:S(2)}, u32[]{:S(2)}) collective-permute-start(f32[2,3,128,128]{3,2,1,0:T(8,128)S(1)} %reshape_reshape.3), channel_id=1, source_target_pairs={{8,0},{16,8},{24,16},{32,24},{40,32},{48,40},{56,48},{64,56},{72,6... | collective-permute-start | bytes 1179656 | tf_op jit(solution)/shard_map/ppermute | solution.py:25
  109.4 1.9 %collective-permute-start.4 = (f32[2,3,128,128]{3,2,1,0:T(8,128)S(1)}, f32[2,3,128,128]{3,2,1,0:T(8,128)S(1)}, u32[]{:S(2)}, u32[]{:S(2)}) collective-permute-start(f32[2,3,128,128]{3,2,1,0:T(8,128)S(1)} %reshape_reshape.3), channel_id=1, source_target_pairs={{0,8},{8,16},{16,24},{24,32},{32,40},{40,48},{48,56},{56,64},{64,7... | collective-permute-start | bytes 1179656 | tf_op jit(solution)/shard_map/ppermute | solution.py:22
  111.3 6.2 %collective-permute-done.5 = f32[2,3,128,128]{3,2,1,0:T(8,128)S(1)} collective-permute-done((f32[2,3,128,128]{3,2,1,0:T(8,128)S(1)}, f32[2,3,128,128]{3,2,1,0:T(8,128)S(1)}, u32[]{:S(2)}, u32[]{:S(2)}) %collective-permute-start.5) | collective-permute-done | bytes 393248 | tf_op jit(solution)/shard_map/ppermute | solution.py:25
  117.5 7.4 %collective-permute-done.4 = f32[2,3,128,128]{3,2,1,0:T(8,128)S(1)} collective-permute-done((f32[2,3,128,128]{3,2,1,0:T(8,128)S(1)}, f32[2,3,128,128]{3,2,1,0:T(8,128)S(1)}, u32[]{:S(2)}, u32[]{:S(2)}) %collective-permute-start.4) | collective-permute-done | bytes 393248 | tf_op jit(solution)/shard_map/ppermute | solution.py:22
  125.0 1.1 pad_maximum_fusion.1.win_ref
  126.1 0.0 copy-start.3
  126.1 0.0 copy-start.2
  126.1 10.5 %shard_map.96 = f32[8,1024]{1,0:T(8,128)} custom-call(s32[4]{0:T(128)} %and_select_fusion.ids_ref, f32[6,3,128,128]{3,2,1,0:T(8,128)} %pad_maximum_fusion.1.win_ref, s32[8,1024]{1,0:T(8,128)} %bitcast.46, s32[8,1024]{1,0:T(8,128)} %bitcast.48, f32[8,1024]{1,0:T(8,128)} %get-tuple-element.15.cos_ref, f32[8,1024]{1,0:T(8,128)} %get-tuple-element.14.sin_ref), custom_call_target="tpu_custom_call" | custom-call | tf_op jit(solution)/shard_map/pallas_call | solution.py:194
  136.6 0.0 copy-done.3
  136.6 1.4 fusion
  138.0 1.3 pad_maximum_fusion.3
  139.4 2.4 %psum.35 = f32[2]{0:T(128)S(1)} all-reduce(f32[2]{0:T(128)S(1)} %pad_maximum_fusion.3), channel_id=1, replica_groups=mesh['tm_0'=4,'tm_hi'=4,'tm_lo'=4,'wafer_0'=4,'wafer_1'=2] {'wafer_1'}, use_global_device_ids=true, to_apply=%region_3.4 | all-reduce | flops 2 | bytes 16 | tf_op jit(solution)/shard_map/psum | solution.py:63
  141.8 9.2 %psum.36 = f32[2]{0:T(128)S(1)} all-reduce(f32[2]{0:T(128)S(1)} %psum.35), channel_id=1, replica_groups=mesh['tm_0'=4,'tm_hi'=4,'tm_lo'=4,'wafer_0'=4,'wafer_1'=2] {'wafer_0'}, use_global_device_ids=true, to_apply=%region_4.5 | all-reduce | flops 2 | bytes 16 | tf_op jit(solution)/shard_map/psum | solution.py:63
  151.0 7.7 %psum.37 = f32[2]{0:T(128)S(1)} all-reduce(f32[2]{0:T(128)S(1)} %psum.36), channel_id=1, replica_groups=mesh['tm_0'=4,'tm_hi'=4,'tm_lo'=4,'wafer_0'=4,'wafer_1'=2] {'tm_0'}, use_global_device_ids=true, to_apply=%region_5.6 | all-reduce | flops 2 | bytes 16 | tf_op jit(solution)/shard_map/psum | solution.py:63
  158.7 8.4 %psum.38 = f32[2]{0:T(128)S(1)} all-reduce(f32[2]{0:T(128)S(1)} %psum.37), channel_id=1, replica_groups=mesh['tm_0'=4,'tm_hi'=4,'tm_lo'=4,'wafer_0'=4,'wafer_1'=2] {'tm_lo'}, use_global_device_ids=true, to_apply=%region_6.7 | all-reduce | flops 2 | bytes 16 | tf_op jit(solution)/shard_map/psum | solution.py:63
  167.0 13.8 %psum.39 = f32[2]{0:T(128)S(1)} all-reduce(f32[2]{0:T(128)S(1)} %psum.38), channel_id=1, replica_groups=mesh['tm_0'=4,'tm_hi'=4,'tm_lo'=4,'wafer_0'=4,'wafer_1'=2] {'tm_hi'}, use_global_device_ids=true, to_apply=%region_7.8 | all-reduce | flops 2 | bytes 16 | tf_op jit(solution)/shard_map/psum | solution.py:63
  180.8 0.6 fusion.8
  182.6 0.0 copy-done.2
  182.6 1.4 subtract_bitcast_fusion
  184.0 0.0 copy-start
  184.0 0.2 broadcast_multiply_fusion
  184.3 0.3 mul.109
  184.6 0.4 copy-done
  185.0 0.9 add.75
  (5 shorter events, 0.1 us)
Async XLA Ops:
  0.6 17.0 %copy-start.4 = (s32[1,4]{1,0:T(1,128)S(1)}, s32[1,4]{1,0:T(1,128)}, u32[]{:S(2)}) copy-start(s32[1,4]{1,0:T(1,128)} %param.13) | copy-start | bytes 52
  0.6 17.5 %copy-start.1 = (f32[1,8,1024]{2,1,0:T(8,128)S(1)}, f32[1,8,1024]{2,1,0:T(8,128)}, u32[]{:S(2)}) copy-start(f32[1,8,1024]{2,1,0:T(8,128)} %param.12) | copy-start | bytes 98308
  2.0 22.0 %collective-permute-start.1 = (f32[2,3,128,128]{3,2,1,0:T(8,128)S(1)}, f32[2,3,128,128]{3,2,1,0:T(8,128)S(1)}, u32[]{:S(2)}, u32[]{:S(2)}) collective-permute-start(f32[2,3,128,128]{3,2,1,0:T(8,128)S(1)} %copy.49), channel_id=1, source_target_pairs={{8,0},{16,8},{24,16},{32,24},{40,32},{48,40},{56,48},{64,56},{72,6... | collective-permute-start | bytes 1179656 | tf_op jit(solution)/shard_map/ppermute | solution.py:25
  15.6 15.8 %collective-permute-start = (f32[2,3,128,128]{3,2,1,0:T(8,128)S(1)}, f32[2,3,128,128]{3,2,1,0:T(8,128)S(1)}, u32[]{:S(2)}, u32[]{:S(2)}) collective-permute-start(f32[2,3,128,128]{3,2,1,0:T(8,128)S(1)} %copy.49), channel_id=1, source_target_pairs={{0,8},{8,16},{16,24},{24,32},{32,40},{40,48},{48,56},{56,64},{64,7... | collective-permute-start | bytes 1179656 | tf_op jit(solution)/shard_map/ppermute | solution.py:22
  58.0 14.9 %collective-permute-start.3 = (f32[2,3,16384]{2,0,1:T(2,128)S(1)}, f32[2,3,16384]{2,0,1:T(2,128)S(1)}, u32[]{:S(2)}, u32[]{:S(2)}) collective-permute-start(f32[2,3,16384]{2,0,1:T(2,128)S(1)} %slice.59), channel_id=1, source_target_pairs={{0,8},{8,16},{16,24},{24,32},{32,40},{40,48},{48,56},{56,64},{64,7... | collective-permute-start | bytes 1179656 | tf_op jit(solution)/shard_map/ppermute | solution.py:32
  59.9 14.2 %collective-permute-start.2 = (f32[2,3,16384]{2,0,1:T(2,128)S(1)}, f32[2,3,16384]{2,0,1:T(2,128)S(1)}, u32[]{:S(2)}, u32[]{:S(2)}) collective-permute-start(f32[2,3,16384]{2,0,1:T(2,128)S(1)} %slice.57), channel_id=1, source_target_pairs={{0,504},{8,0},{16,8},{24,16},{32,24},{40,32},{48,40},{56,48},{64,5... | collective-permute-start | bytes 1179656 | tf_op jit(solution)/shard_map/ppermute | solution.py:32
  75.8 12.4 %all-to-all-start = ((f32[8,2,3,2048]{3,1,2,0:T(2,128)}), f32[8,2,3,2048]{3,1,2,0:T(2,128)S(1)}, u32[]{:S(2)}, u32[]{:S(2)}) async-start(f32[8,2,3,2048]{3,1,2,0:T(2,128)} %copy.55), calls=%async_computation | async-start | bytes 786432 | tf_op jit(solution)/shard_map/all_to_all | solution.py:43
  101.6 15.9 %collective-permute-start.5 = (f32[2,3,128,128]{3,2,1,0:T(8,128)S(1)}, f32[2,3,128,128]{3,2,1,0:T(8,128)S(1)}, u32[]{:S(2)}, u32[]{:S(2)}) collective-permute-start(f32[2,3,128,128]{3,2,1,0:T(8,128)S(1)} %reshape_reshape.3), channel_id=1, source_target_pairs={{8,0},{16,8},{24,16},{32,24},{40,32},{48,40},{56,48},{64,56},{72,6... | collective-permute-start | bytes 1179656 | tf_op jit(solution)/shard_map/ppermute | solution.py:25
  109.4 15.6 %collective-permute-start.4 = (f32[2,3,128,128]{3,2,1,0:T(8,128)S(1)}, f32[2,3,128,128]{3,2,1,0:T(8,128)S(1)}, u32[]{:S(2)}, u32[]{:S(2)}) collective-permute-start(f32[2,3,128,128]{3,2,1,0:T(8,128)S(1)} %reshape_reshape.3), channel_id=1, source_target_pairs={{0,8},{8,16},{16,24},{24,32},{32,40},{40,48},{48,56},{56,64},{64,7... | collective-permute-start | bytes 1179656 | tf_op jit(solution)/shard_map/ppermute | solution.py:22
  126.1 10.5 %copy-start.3 = (f32[1,8]{1,0:T(1,128)S(1)}, f32[1,8]{1,0:T(1,128)}, u32[]{:S(2)}) copy-start(f32[1,8]{1,0:T(1,128)} %param.9) | copy-start | bytes 100
  126.1 56.6 %copy-start.2 = (f32[8,1024]{1,0:T(8,128)S(1)}, f32[8,1024]{1,0:T(8,128)}, u32[]{:S(2)}) copy-start(f32[8,1024]{1,0:T(8,128)} %get-tuple-element.5) | copy-start | bytes 98308
  184.0 1.0 copy-start

commit v7 on v6

--- a/solution.py
+++ b/solution.py
@@ -147,20 +147,25 @@
                               + acc_ref[rows_s, (3 + comp) * SIDE:(4 + comp) * SIDE])
 
 
-def scan_kernel(ids_ref, win_ref, slot_ref, pix_ref, cos_ref, sin_ref, out_ref, lhs_ref):
+def scan_kernel(ids_ref, w_ref, slope_ref, win_ref, slot_ref, pix_ref, cos_ref, sin_ref, out_ref,
+                totals_ref, lhs_ref):
     stacked_map(ids_ref, win_ref, lhs_ref)
     rows = lhs_ref.shape[1]
 
-    def body(d, carry):
+    def body(d, curve):
         slot = slot_ref[pl.ds(d, 1), :]
         pix = pix_ref[pl.ds(d, 1), :]
         at = row_onehot(slot, pix, rows)
         mask = col_mask(pix)
         v0, v1, v2 = sampled(lhs_ref, at, mask)
-        out_ref[pl.ds(d, 1), :] = v0 + cos_ref[pl.ds(d, 1), :] * v1 + sin_ref[pl.ds(d, 1), :] * v2
-        return carry
-
-    lax.fori_loop(0, slot_ref.shape[0], body, 0)
+        value = v0 + cos_ref[pl.ds(d, 1), :] * v1 + sin_ref[pl.ds(d, 1), :] * v2
+        out_ref[pl.ds(d, 1), :] = value
+        return curve + w_ref[d] * value * value
+
+    curve = lax.fori_loop(0, slot_ref.shape[0], body, jnp.zeros(cos_ref.shape[1:], jnp.float32)[None])
+    curve_sum = jnp.sum(curve, axis=1, keepdims=True)
+    lane = lax.broadcasted_iota(jnp.int32, totals_ref.shape, 1)
+    totals_ref[...] = jnp.where(lane == 0, slope_ref[0], jnp.where(lane == 1, curve_sum, 0.0))
 
 
 VMEM = pltpu.MemorySpace.VMEM
@@ -187,17 +192,20 @@
     )(local_ids, weights, win, slot, pix, cos_two, sin_two, ts)
 
 
-def scan_call(local_ids, win, slot, pix, cos_two, sin_two):
+def scan_call(local_ids, weights, slope, win, slot, pix, cos_two, sin_two):
     hits = local_ids.shape[0]
     smem = pl.BlockSpec(memory_space=pltpu.SMEM)
     vmem = pl.BlockSpec(memory_space=VMEM)
     return pl.pallas_call(
         scan_kernel,
-        out_shape=jax.ShapeDtypeStruct(slot.shape, jnp.float32),
-        in_specs=[smem] + [vmem] * 5,
-        out_specs=vmem,
+        out_shape=(
+            jax.ShapeDtypeStruct(slot.shape, jnp.float32),
+            jax.ShapeDtypeStruct((1, SIDE), jnp.float32),
+        ),
+        in_specs=[smem] * 3 + [vmem] * 5,
+        out_specs=(vmem, vmem),
         scratch_shapes=[pltpu.VMEM((6 * SIDE, hits * SIDE), jnp.bfloat16)],
-    )(local_ids, win, slot, pix, cos_two, sin_two)
+    )(local_ids, weights, slope, win, slot, pix, cos_two, sin_two)
 
 
 def as_grid(tiles):
@@ -231,10 +239,11 @@
     slope_part = jnp.sum(grad_share * dir_share)
     direction = collect(dir_share, WAFER, 2)
     dir_window = with_halo(as_grid(direction), ((TM, 0),), tiles_dev)
-    rescanned = scan_call(local_ids, dir_window, slot, pix, cos_two, sin_two)
-    curve_part = jnp.sum(weights[:, None] * rescanned * rescanned)
-    totals = by_axis(jnp.stack([slope_part, curve_part]), ("wafer_1", "wafer_0", "tm_0", "tm_lo", "tm_hi"))
-    step_size = totals[0] / totals[1]
+    rescanned, parts = scan_call(
+        local_ids, weights, slope_part.reshape(1), dir_window, slot, pix, cos_two, sin_two
+    )
+    totals = by_axis(parts, ("wafer_1", "wafer_0", "tm_0", "tm_lo", "tm_hi"))
+    step_size = totals[0, 0] / totals[0, 1]
     new_map = sky_map + step_size * direction
     new_residual = (resid - step_size * rescanned)[None]
     return (new_map, new_residual)

time: 187 us -> 184 us (0.984)
  other arithmetic: 10.9 us -> 7.26 us
where the time goes in v7:
time: 184 us; the launch traced here: 183 us
  blocking collectives  52.9 us (29%)
  waiting for transfers between devices  40.3 us (22%)
  starting transfers between devices  39.2 us (21%)
  Pallas kernels  34.8 us (19%)
  other arithmetic  7.26 us (4%)
  local copies, waits for them, and re-layouts  6.62 us (4%)
  between operations  2.21 us (1%)
    psum x5, blocking collectives, by_axis(): return functools.reduce(lax.psum, axes, value)  41.6 us
    pallas_call x1, Pallas kernels, bin_call(): pl.pallas_call(bin_kernel, out_shape=(jax.ShapeDtypeStruct((dets, samp),...  23.6 us
    ppermute x2, starting transfers between devices, with_halo(): lax.ppermute(lax.slice_in_dim(block, 0, width, axis=dim), axis, backward)  21.3 us
    ppermute x2, waiting for transfers between devices, with_halo(): lax.ppermute(lax.slice_in_dim(block, block.shape[dim] - width, None, axis...  14.9 us
    all_to_all x1, blocking collectives, copy_for_each(): return lax.all_to_all(copies, axis, split_axis=0, concat_axis=0, tiled=True)  11.3 us
    ppermute x2, waiting for transfers between devices, with_halo(): lax.ppermute(lax.slice_in_dim(block, 0, width, axis=dim), axis, backward)  11.3 us
    pallas_call x1, Pallas kernels, scan_call(): pl.pallas_call(scan_kernel, out_shape=(jax.ShapeDtypeStruct(slot.shape, j...  11.1 us
    ppermute x2, starting transfers between devices, passed_along(): lax.ppermute(value, axis, [(i, (i + by) % count) for i in range(count)])  9.16 us
  transfers between devices with their start and end apart: 7, of which 7 were waited for; matrix products, arithmetic and copies ran while one was open for 1% of the time, Pallas kernels for 0%

profile of v7, /device:TPU:8, one launch (start us, length us, event | category | flops | bytes accessed | tf_op | source)
XLA Modules:
  0.0 183.2 jit_solution(8927068201125968359)
XLA Ops:
  0.6 0.0 copy-start.4
  0.6 0.0 copy-start.1
  0.6 1.3 reshape.27
  2.0 13.6 %collective-permute-start.1 = (f32[2,3,128,128]{3,2,1,0:T(8,128)S(1)}, f32[2,3,128,128]{3,2,1,0:T(8,128)S(1)}, u32[]{:S(2)}, u32[]{:S(2)}) collective-permute-start(f32[2,3,128,128]{3,2,1,0:T(8,128)S(1)} %copy.49), channel_id=1, source_target_pairs={{8,0},{16,8},{24,16},{32,24},{40,32},{48,40},{56,48},{64,56},{72,6... | collective-permute-start | bytes 1179656 | tf_op jit(solution)/shard_map/ppermute | solution.py:25
  15.6 1.9 %collective-permute-start = (f32[2,3,128,128]{3,2,1,0:T(8,128)S(1)}, f32[2,3,128,128]{3,2,1,0:T(8,128)S(1)}, u32[]{:S(2)}, u32[]{:S(2)}) collective-permute-start(f32[2,3,128,128]{3,2,1,0:T(8,128)S(1)} %copy.49), channel_id=1, source_target_pairs={{0,8},{8,16},{16,24},{24,32},{32,40},{40,48},{48,56},{56,64},{64,7... | collective-permute-start | bytes 1179656 | tf_op jit(solution)/shard_map/ppermute | solution.py:22
  17.6 0.0 copy-done.4
  17.6 0.6 and_select_fusion.ids_ref
  18.2 0.0 copy-done.1
  18.2 0.8 sine_bitcast_fusion
  18.9 5.1 %collective-permute-done.1 = f32[2,3,128,128]{3,2,1,0:T(8,128)S(1)} collective-permute-done((f32[2,3,128,128]{3,2,1,0:T(8,128)S(1)}, f32[2,3,128,128]{3,2,1,0:T(8,128)S(1)}, u32[]{:S(2)}, u32[]{:S(2)}) %collective-permute-start.1) | collective-permute-done | bytes 393248 | tf_op jit(solution)/shard_map/ppermute | solution.py:25
  24.0 7.4 %collective-permute-done = f32[2,3,128,128]{3,2,1,0:T(8,128)S(1)} collective-permute-done((f32[2,3,128,128]{3,2,1,0:T(8,128)S(1)}, f32[2,3,128,128]{3,2,1,0:T(8,128)S(1)}, u32[]{:S(2)}, u32[]{:S(2)}) %collective-permute-start) | collective-permute-done | bytes 393248 | tf_op jit(solution)/shard_map/ppermute | solution.py:22
  31.4 1.1 pad_maximum_fusion.win_ref
  32.5 23.6 %shard_map.95 = (f32[8,1024]{1,0:T(8,128)}, f32[6,3,128,128]{3,2,1,0:T(8,128)}) custom-call(s32[4]{0:T(128)} %and_select_fusion.ids_ref, f32[8]{0:T(128)} %bitcast.49, f32[6,3,128,128]{3,2,1,0:T(8,128)} %pad_maximum_fusion.win_ref, s32[8,1024]{1,0:T(8,128)} %bitcast.44, s32[8,1024]{1,0:T(8,128)} %bitcast.46, f32[8,1024]{1,0:T(8,128)} %get-tuple-element.19.cos_ref, ...), custom_call_target="tpu_custom_call" | custom-call | tf_op jit(solution)/shard_map/pallas_call | solution.py:179
  56.1 1.3 fusion.6
  57.5 0.2 slice.57
  57.8 0.2 slice.59
  58.0 1.9 %collective-permute-start.3 = (f32[2,3,16384]{2,0,1:T(2,128)S(1)}, f32[2,3,16384]{2,0,1:T(2,128)S(1)}, u32[]{:S(2)}, u32[]{:S(2)}) collective-permute-start(f32[2,3,16384]{2,0,1:T(2,128)S(1)} %slice.59), channel_id=1, source_target_pairs={{0,8},{8,16},{16,24},{24,32},{32,40},{40,48},{48,56},{56,64},{64,7... | collective-permute-start | bytes 1179656 | tf_op jit(solution)/shard_map/ppermute | solution.py:32
  59.9 7.2 %collective-permute-start.2 = (f32[2,3,16384]{2,0,1:T(2,128)S(1)}, f32[2,3,16384]{2,0,1:T(2,128)S(1)}, u32[]{:S(2)}, u32[]{:S(2)}) collective-permute-start(f32[2,3,16384]{2,0,1:T(2,128)S(1)} %slice.57), channel_id=1, source_target_pairs={{0,504},{8,0},{16,8},{24,16},{32,24},{40,32},{48,40},{56,48},{64,5... | collective-permute-start | bytes 1179656 | tf_op jit(solution)/shard_map/ppermute | solution.py:32
  67.2 0.2 slice.55
  67.4 5.5 %collective-permute-done.3 = f32[2,3,16384]{2,0,1:T(2,128)S(1)} collective-permute-done((f32[2,3,16384]{2,0,1:T(2,128)S(1)}, f32[2,3,16384]{2,0,1:T(2,128)S(1)}, u32[]{:S(2)}, u32[]{:S(2)}) %collective-permute-start.3) | collective-permute-done | bytes 393248 | tf_op jit(solution)/shard_map/ppermute | solution.py:32
  72.9 1.2 collective-permute-done.2
  74.1 0.3 add_add_fusion
  74.4 0.3 reshape.28
  74.7 1.1 copy.55
  75.8 4.9 %all-to-all-start = ((f32[8,2,3,2048]{3,1,2,0:T(2,128)}), f32[8,2,3,2048]{3,1,2,0:T(2,128)S(1)}, u32[]{:S(2)}, u32[]{:S(2)}) async-start(f32[8,2,3,2048]{3,1,2,0:T(2,128)} %copy.55), calls=%async_computation | async-start | bytes 786432 | tf_op jit(solution)/shard_map/all_to_all | solution.py:43
  80.7 7.5 %all-to-all-done = f32[8,2,3,2048]{3,1,2,0:T(2,128)S(1)} async-done(((f32[8,2,3,2048]{3,1,2,0:T(2,128)}), f32[8,2,3,2048]{3,1,2,0:T(2,128)S(1)}, u32[]{:S(2)}, u32[]{:S(2)}) %all-to-all-start) | async-done | bytes 393248 | tf_op jit(solution)/shard_map/all_to_all | solution.py:43
  88.2 0.1 reduce_sum.18
  88.3 0.9 fusion.4
  89.2 0.7 multiply_reduce_fusion
  89.8 0.2 broadcast_in_dim.6
  90.0 11.3 %all_to_all.10 = f32[8,2,3,2048]{3,1,2,0:T(2,128)S(1)} all-to-all(f32[8,2,3,2048]{3,1,2,0:T(2,128)S(1)} %broadcast_in_dim.6), channel_id=1, replica_groups=mesh['tm_0'=4,'tm_hi'=4,'tm_lo'=4,'wafer_0'=4,'wafer_1'=2] {'wafer_0','w..., dimensions={0} | all-to-all | bytes 786432 | tf_op jit(solution)/shard_map/all_to_all | solution.py:55
  101.3 0.2 copy.63
  101.5 0.1 reshape_reshape.3
  101.6 7.7 %collective-permute-start.5 = (f32[2,3,128,128]{3,2,1,0:T(8,128)S(1)}, f32[2,3,128,128]{3,2,1,0:T(8,128)S(1)}, u32[]{:S(2)}, u32[]{:S(2)}) collective-permute-start(f32[2,3,128,128]{3,2,1,0:T(8,128)S(1)} %reshape_reshape.3), channel_id=1, source_target_pairs={{8,0},{16,8},{24,16},{32,24},{40,32},{48,40},{56,48},{64,56},{72,6... | collective-permute-start | bytes 1179656 | tf_op jit(solution)/shard_map/ppermute | solution.py:25
  109.3 1.9 %collective-permute-start.4 = (f32[2,3,128,128]{3,2,1,0:T(8,128)S(1)}, f32[2,3,128,128]{3,2,1,0:T(8,128)S(1)}, u32[]{:S(2)}, u32[]{:S(2)}) collective-permute-start(f32[2,3,128,128]{3,2,1,0:T(8,128)S(1)} %reshape_reshape.3), channel_id=1, source_target_pairs={{0,8},{8,16},{16,24},{24,32},{32,40},{40,48},{48,56},{56,64},{64,7... | collective-permute-start | bytes 1179656 | tf_op jit(solution)/shard_map/ppermute | solution.py:22
  111.2 6.2 %collective-permute-done.5 = f32[2,3,128,128]{3,2,1,0:T(8,128)S(1)} collective-permute-done((f32[2,3,128,128]{3,2,1,0:T(8,128)S(1)}, f32[2,3,128,128]{3,2,1,0:T(8,128)S(1)}, u32[]{:S(2)}, u32[]{:S(2)}) %collective-permute-start.5) | collective-permute-done | bytes 393248 | tf_op jit(solution)/shard_map/ppermute | solution.py:25
  117.5 7.4 %collective-permute-done.4 = f32[2,3,128,128]{3,2,1,0:T(8,128)S(1)} collective-permute-done((f32[2,3,128,128]{3,2,1,0:T(8,128)S(1)}, f32[2,3,128,128]{3,2,1,0:T(8,128)S(1)}, u32[]{:S(2)}, u32[]{:S(2)}) %collective-permute-start.4) | collective-permute-done | bytes 393248 | tf_op jit(solution)/shard_map/ppermute | solution.py:22
  124.9 1.1 pad_maximum_fusion.1.win_ref
  126.0 11.1 %shard_map.96 = (f32[8,1024]{1,0:T(8,128)}, f32[1,128]{1,0:T(1,128)}) custom-call(s32[4]{0:T(128)} %and_select_fusion.ids_ref, f32[8]{0:T(128)} %bitcast.50, f32[1]{0:T(128)} %bitcast.8.slope_ref, f32[6,3,128,128]{3,2,1,0:T(8,128)} %pad_maximum_fusion.1.win_ref, s32[8,1024]{1,0:T(8,128)} %bitcast.45, s32[8,1024]{1,0:T(8,128)} %bitcast.47, ...), custom_call_target="tpu_custom_call" | custom-call | tf_op jit(solution)/shard_map/pallas_call | solution.py:199
  137.2 2.6 %psum.35 = f32[1,128]{1,0:T(1,128)S(1)} all-reduce(f32[1,128]{1,0:T(1,128)} %get-tuple-element.7), channel_id=1, replica_groups=mesh['tm_0'=4,'tm_hi'=4,'tm_lo'=4,'wafer_0'=4,'wafer_1'=2] {'wafer_1'}, use_global_device_ids=true, to_apply=%region_2.3 | all-reduce | flops 128 | bytes 1024 | tf_op jit(solution)/shard_map/psum | solution.py:63
  139.7 9.1 %psum.36 = f32[1,128]{1,0:T(1,128)S(1)} all-reduce(f32[1,128]{1,0:T(1,128)S(1)} %psum.35), channel_id=1, replica_groups=mesh['tm_0'=4,'tm_hi'=4,'tm_lo'=4,'wafer_0'=4,'wafer_1'=2] {'wafer_0'}, use_global_device_ids=true, to_apply=%region_3.4 | all-reduce | flops 128 | bytes 1024 | tf_op jit(solution)/shard_map/psum | solution.py:63
  148.9 7.7 %psum.37 = f32[1,128]{1,0:T(1,128)S(1)} all-reduce(f32[1,128]{1,0:T(1,128)S(1)} %psum.36), channel_id=1, replica_groups=mesh['tm_0'=4,'tm_hi'=4,'tm_lo'=4,'wafer_0'=4,'wafer_1'=2] {'tm_0'}, use_global_device_ids=true, to_apply=%region_4.5 | all-reduce | flops 128 | bytes 1024 | tf_op jit(solution)/shard_map/psum | solution.py:63
  156.6 8.4 %psum.38 = f32[1,128]{1,0:T(1,128)S(1)} all-reduce(f32[1,128]{1,0:T(1,128)S(1)} %psum.37), channel_id=1, replica_groups=mesh['tm_0'=4,'tm_hi'=4,'tm_lo'=4,'wafer_0'=4,'wafer_1'=2] {'tm_lo'}, use_global_device_ids=true, to_apply=%region_5.6 | all-reduce | flops 128 | bytes 1024 | tf_op jit(solution)/shard_map/psum | solution.py:63
  165.0 13.8 %psum.39 = f32[1,128]{1,0:T(1,128)S(1)} all-reduce(f32[1,128]{1,0:T(1,128)S(1)} %psum.38), channel_id=1, replica_groups=mesh['tm_0'=4,'tm_hi'=4,'tm_lo'=4,'wafer_0'=4,'wafer_1'=2] {'tm_hi'}, use_global_device_ids=true, to_apply=%region_6.7 | all-reduce | flops 128 | bytes 1024 | tf_op jit(solution)/shard_map/psum | solution.py:63
  178.7 0.6 fusion.7
  180.6 0.0 copy-start
  180.7 0.2 broadcast_multiply_fusion
  180.9 0.0 copy-start.2
  180.9 0.0 copy-start.3
  181.0 0.3 mul.95
  181.3 0.4 copy-done
  181.6 0.9 add.75
  182.6 0.0 copy-done.2
  182.6 0.0 copy-done.3
  182.6 0.6 subtract_bitcast_fusion
  (5 shorter events, 0.1 us)
Async XLA Ops:
  0.6 17.0 %copy-start.4 = (s32[1,4]{1,0:T(1,128)S(1)}, s32[1,4]{1,0:T(1,128)}, u32[]{:S(2)}) copy-start(s32[1,4]{1,0:T(1,128)} %param.13) | copy-start | bytes 52
  0.6 17.5 %copy-start.1 = (f32[1,8,1024]{2,1,0:T(8,128)S(1)}, f32[1,8,1024]{2,1,0:T(8,128)}, u32[]{:S(2)}) copy-start(f32[1,8,1024]{2,1,0:T(8,128)} %param.12) | copy-start | bytes 98308
  2.0 22.0 %collective-permute-start.1 = (f32[2,3,128,128]{3,2,1,0:T(8,128)S(1)}, f32[2,3,128,128]{3,2,1,0:T(8,128)S(1)}, u32[]{:S(2)}, u32[]{:S(2)}) collective-permute-start(f32[2,3,128,128]{3,2,1,0:T(8,128)S(1)} %copy.49), channel_id=1, source_target_pairs={{8,0},{16,8},{24,16},{32,24},{40,32},{48,40},{56,48},{64,56},{72,6... | collective-permute-start | bytes 1179656 | tf_op jit(solution)/shard_map/ppermute | solution.py:25
  15.6 15.8 %collective-permute-start = (f32[2,3,128,128]{3,2,1,0:T(8,128)S(1)}, f32[2,3,128,128]{3,2,1,0:T(8,128)S(1)}, u32[]{:S(2)}, u32[]{:S(2)}) collective-permute-start(f32[2,3,128,128]{3,2,1,0:T(8,128)S(1)} %copy.49), channel_id=1, source_target_pairs={{0,8},{8,16},{16,24},{24,32},{32,40},{40,48},{48,56},{56,64},{64,7... | collective-permute-start | bytes 1179656 | tf_op jit(solution)/shard_map/ppermute | solution.py:22
  58.0 14.9 %collective-permute-start.3 = (f32[2,3,16384]{2,0,1:T(2,128)S(1)}, f32[2,3,16384]{2,0,1:T(2,128)S(1)}, u32[]{:S(2)}, u32[]{:S(2)}) collective-permute-start(f32[2,3,16384]{2,0,1:T(2,128)S(1)} %slice.59), channel_id=1, source_target_pairs={{0,8},{8,16},{16,24},{24,32},{32,40},{40,48},{48,56},{56,64},{64,7... | collective-permute-start | bytes 1179656 | tf_op jit(solution)/shard_map/ppermute | solution.py:32
  59.9 14.2 %collective-permute-start.2 = (f32[2,3,16384]{2,0,1:T(2,128)S(1)}, f32[2,3,16384]{2,0,1:T(2,128)S(1)}, u32[]{:S(2)}, u32[]{:S(2)}) collective-permute-start(f32[2,3,16384]{2,0,1:T(2,128)S(1)} %slice.57), channel_id=1, source_target_pairs={{0,504},{8,0},{16,8},{24,16},{32,24},{40,32},{48,40},{56,48},{64,5... | collective-permute-start | bytes 1179656 | tf_op jit(solution)/shard_map/ppermute | solution.py:32
  75.8 12.4 %all-to-all-start = ((f32[8,2,3,2048]{3,1,2,0:T(2,128)}), f32[8,2,3,2048]{3,1,2,0:T(2,128)S(1)}, u32[]{:S(2)}, u32[]{:S(2)}) async-start(f32[8,2,3,2048]{3,1,2,0:T(2,128)} %copy.55), calls=%async_computation | async-start | bytes 786432 | tf_op jit(solution)/shard_map/all_to_all | solution.py:43
  101.6 15.9 %collective-permute-start.5 = (f32[2,3,128,128]{3,2,1,0:T(8,128)S(1)}, f32[2,3,128,128]{3,2,1,0:T(8,128)S(1)}, u32[]{:S(2)}, u32[]{:S(2)}) collective-permute-start(f32[2,3,128,128]{3,2,1,0:T(8,128)S(1)} %reshape_reshape.3), channel_id=1, source_target_pairs={{8,0},{16,8},{24,16},{32,24},{40,32},{48,40},{56,48},{64,56},{72,6... | collective-permute-start | bytes 1179656 | tf_op jit(solution)/shard_map/ppermute | solution.py:25
  109.3 15.6 %collective-permute-start.4 = (f32[2,3,128,128]{3,2,1,0:T(8,128)S(1)}, f32[2,3,128,128]{3,2,1,0:T(8,128)S(1)}, u32[]{:S(2)}, u32[]{:S(2)}) collective-permute-start(f32[2,3,128,128]{3,2,1,0:T(8,128)S(1)} %reshape_reshape.3), channel_id=1, source_target_pairs={{0,8},{8,16},{16,24},{24,32},{32,40},{40,48},{48,56},{56,64},{64,7... | collective-permute-start | bytes 1179656 | tf_op jit(solution)/shard_map/ppermute | solution.py:22
  180.6 1.0 copy-start
  180.9 1.7 copy-start.2
  180.9 1.7 copy-start.3

commit v8 on v7

--- a/solution.py
+++ b/solution.py
@@ -57,6 +57,10 @@
 
 def collect(value, axis, dim):
     return laid_out(copy_for_each(value, axis), dim)
+
+
+def summed_by_exchange(value, axis):
+    return jnp.sum(copy_for_each(value, axis), axis=0)
 
 
 def by_axis(value, axes):
@@ -242,7 +246,9 @@
     rescanned, parts = scan_call(
         local_ids, weights, slope_part.reshape(1), dir_window, slot, pix, cos_two, sin_two
     )
-    totals = by_axis(parts, ("wafer_1", "wafer_0", "tm_0", "tm_lo", "tm_hi"))
+    totals = summed_by_exchange(parts, WAFER)
+    totals = lax.psum(totals, "tm_0")
+    totals = summed_by_exchange(totals, ("tm_hi", "tm_lo"))
     step_size = totals[0, 0] / totals[0, 1]
     new_map = sky_map + step_size * direction
     new_residual = (resid - step_size * rescanned)[None]

time: 184 us -> 175 us (0.951)
  the two profiles are of different devices: /device:TPU:8 before, /device:TPU:1 now
where the time goes in v8:
time: 175 us; the launch traced here: 172 us
  starting transfers between devices  41.4 us (24%)
  blocking collectives  40.4 us (23%)
  waiting for transfers between devices  38.3 us (22%)
  Pallas kernels  34.7 us (20%)
  local copies, waits for them, and re-layouts  7.27 us (4%)
  other arithmetic  7.25 us (4%)
  between operations  2.21 us (1%)
    all_to_all x3, blocking collectives, copy_for_each(): return lax.all_to_all(copies, axis, split_axis=0, concat_axis=0, tiled=True)  34.4 us
    pallas_call x1, Pallas kernels, bin_call(): pl.pallas_call(bin_kernel, out_shape=(jax.ShapeDtypeStruct((dets, samp),...  23.6 us
    ppermute x2, starting transfers between devices, with_halo(): lax.ppermute(lax.slice_in_dim(block, 0, width, axis=dim), axis, backward)  21.6 us
    ppermute x2, waiting for transfers between devices, with_halo(): lax.ppermute(lax.slice_in_dim(block, block.shape[dim] - width, None, axis...  14.3 us
    pallas_call x1, Pallas kernels, scan_call(): pl.pallas_call(scan_kernel, out_shape=(jax.ShapeDtypeStruct(slot.shape, j...  11.1 us
    ppermute x2, waiting for transfers between devices, with_halo(): lax.ppermute(lax.slice_in_dim(block, 0, width, axis=dim), axis, backward)  10.2 us
    ppermute x2, starting transfers between devices, passed_along(): lax.ppermute(value, axis, [(i, (i + by) % count) for i in range(count)])  8.6 us
    all_to_all x1, waiting for transfers between devices, sum_at_owner(): parts = lax.all_to_all(in_blocks(value, dim, count), axis, 0, 0, tiled=True)  7.7 us
  transfers between devices with their start and end apart: 7, of which 7 were waited for; matrix products, arithmetic and copies ran while one was open for 1% of the time, Pallas kernels for 0%

profile of v8, /device:TPU:1, one launch (start us, length us, event | category | flops | bytes accessed | tf_op | source)
XLA Modules:
  0.0 171.6 jit_solution(15951059581524858475)
XLA Ops:
  0.6 0.0 copy-start.4
  0.6 0.0 copy-start.1
  0.6 1.3 reshape.31
  2.0 14.1 %collective-permute-start.1 = (f32[2,3,128,128]{3,2,1,0:T(8,128)S(1)}, f32[2,3,128,128]{3,2,1,0:T(8,128)S(1)}, u32[]{:S(2)}, u32[]{:S(2)}) collective-permute-start(f32[2,3,128,128]{3,2,1,0:T(8,128)S(1)} %copy.69), channel_id=1, source_target_pairs={{8,0},{16,8},{24,16},{32,24},{40,32},{48,40},{56,48},{64,56},{72,6... | collective-permute-start | bytes 1179656 | tf_op jit(solution)/shard_map/ppermute | solution.py:25
  16.2 1.9 %collective-permute-start = (f32[2,3,128,128]{3,2,1,0:T(8,128)S(1)}, f32[2,3,128,128]{3,2,1,0:T(8,128)S(1)}, u32[]{:S(2)}, u32[]{:S(2)}) collective-permute-start(f32[2,3,128,128]{3,2,1,0:T(8,128)S(1)} %copy.69), channel_id=1, source_target_pairs={{0,8},{8,16},{16,24},{24,32},{32,40},{40,48},{48,56},{56,64},{64,7... | collective-permute-start | bytes 1179656 | tf_op jit(solution)/shard_map/ppermute | solution.py:22
  18.1 0.0 copy-done.4
  18.1 0.5 and_select_fusion.ids_ref
  18.7 0.0 copy-done.1
  18.7 0.7 sine_bitcast_fusion
  19.4 4.5 %collective-permute-done.1 = f32[2,3,128,128]{3,2,1,0:T(8,128)S(1)} collective-permute-done((f32[2,3,128,128]{3,2,1,0:T(8,128)S(1)}, f32[2,3,128,128]{3,2,1,0:T(8,128)S(1)}, u32[]{:S(2)}, u32[]{:S(2)}) %collective-permute-start.1) | collective-permute-done | bytes 393248 | tf_op jit(solution)/shard_map/ppermute | solution.py:25
  24.0 7.2 %collective-permute-done = f32[2,3,128,128]{3,2,1,0:T(8,128)S(1)} collective-permute-done((f32[2,3,128,128]{3,2,1,0:T(8,128)S(1)}, f32[2,3,128,128]{3,2,1,0:T(8,128)S(1)}, u32[]{:S(2)}, u32[]{:S(2)}) %collective-permute-start) | collective-permute-done | bytes 393248 | tf_op jit(solution)/shard_map/ppermute | solution.py:22
  31.1 1.1 pad_maximum_fusion.win_ref
  32.2 23.6 %shard_map.95 = (f32[8,1024]{1,0:T(8,128)}, f32[6,3,128,128]{3,2,1,0:T(8,128)}) custom-call(s32[4]{0:T(128)} %and_select_fusion.ids_ref, f32[8]{0:T(128)} %bitcast.56, f32[6,3,128,128]{3,2,1,0:T(8,128)} %pad_maximum_fusion.win_ref, s32[8,1024]{1,0:T(8,128)} %bitcast.48, s32[8,1024]{1,0:T(8,128)} %bitcast.50, f32[8,1024]{1,0:T(8,128)} %get-tuple-element.19.cos_ref, ...), custom_call_target="tpu_custom_call" | custom-call | tf_op jit(solution)/shard_map/pallas_call | solution.py:183
  55.8 1.3 fusion.6
  57.2 0.2 slice.57
  57.4 0.2 slice.59
  57.7 1.9 %collective-permute-start.3 = (f32[2,3,16384]{2,0,1:T(2,128)S(1)}, f32[2,3,16384]{2,0,1:T(2,128)S(1)}, u32[]{:S(2)}, u32[]{:S(2)}) collective-permute-start(f32[2,3,16384]{2,0,1:T(2,128)S(1)} %slice.59), channel_id=1, source_target_pairs={{0,8},{8,16},{16,24},{24,32},{32,40},{40,48},{48,56},{56,64},{64,7... | collective-permute-start | bytes 1179656 | tf_op jit(solution)/shard_map/ppermute | solution.py:32
  59.6 6.7 %collective-permute-start.2 = (f32[2,3,16384]{2,0,1:T(2,128)S(1)}, f32[2,3,16384]{2,0,1:T(2,128)S(1)}, u32[]{:S(2)}, u32[]{:S(2)}) collective-permute-start(f32[2,3,16384]{2,0,1:T(2,128)S(1)} %slice.57), channel_id=1, source_target_pairs={{0,504},{8,0},{16,8},{24,16},{32,24},{40,32},{48,40},{56,48},{64,5... | collective-permute-start | bytes 1179656 | tf_op jit(solution)/shard_map/ppermute | solution.py:32
  66.3 0.2 slice.55
  66.6 5.2 %collective-permute-done.3 = f32[2,3,16384]{2,0,1:T(2,128)S(1)} collective-permute-done((f32[2,3,16384]{2,0,1:T(2,128)S(1)}, f32[2,3,16384]{2,0,1:T(2,128)S(1)}, u32[]{:S(2)}, u32[]{:S(2)}) %collective-permute-start.3) | collective-permute-done | bytes 393248 | tf_op jit(solution)/shard_map/ppermute | solution.py:32
  71.7 0.9 collective-permute-done.2
  72.6 0.3 add_add_fusion
  72.9 0.3 reshape.32
  73.3 1.1 copy.75
  74.3 7.4 %all-to-all-start = ((f32[8,2,3,2048]{3,1,2,0:T(2,128)}), f32[8,2,3,2048]{3,1,2,0:T(2,128)S(1)}, u32[]{:S(2)}, u32[]{:S(2)}) async-start(f32[8,2,3,2048]{3,1,2,0:T(2,128)} %copy.75), calls=%async_computation | async-start | bytes 786432 | tf_op jit(solution)/shard_map/all_to_all | solution.py:43
  81.7 7.7 %all-to-all-done = f32[8,2,3,2048]{3,1,2,0:T(2,128)S(1)} async-done(((f32[8,2,3,2048]{3,1,2,0:T(2,128)}), f32[8,2,3,2048]{3,1,2,0:T(2,128)S(1)}, u32[]{:S(2)}, u32[]{:S(2)}) %all-to-all-start) | async-done | bytes 393248 | tf_op jit(solution)/shard_map/all_to_all | solution.py:43
  89.4 0.1 reduce_sum.40
  89.6 0.9 fusion.4
  90.4 0.7 multiply_reduce_fusion
  91.1 0.2 broadcast_in_dim.12
  91.3 11.7 %all_to_all.20 = f32[8,2,3,2048]{3,1,2,0:T(2,128)S(1)} all-to-all(f32[8,2,3,2048]{3,1,2,0:T(2,128)S(1)} %broadcast_in_dim.12), channel_id=1, replica_groups=mesh['tm_0'=4,'tm_hi'=4,'tm_lo'=4,'wafer_0'=4,'wafer_1'=2] {'wafer_0','w..., dimensions={0} | all-to-all | bytes 786432 | tf_op jit(solution)/shard_map/all_to_all | solution.py:55
  102.9 0.2 copy.85
  103.1 0.1 reshape_reshape.3
  103.2 7.4 %collective-permute-start.5 = (f32[2,3,128,128]{3,2,1,0:T(8,128)S(1)}, f32[2,3,128,128]{3,2,1,0:T(8,128)S(1)}, u32[]{:S(2)}, u32[]{:S(2)}) collective-permute-start(f32[2,3,128,128]{3,2,1,0:T(8,128)S(1)} %reshape_reshape.3), channel_id=1, source_target_pairs={{8,0},{16,8},{24,16},{32,24},{40,32},{48,40},{56,48},{64,56},{72,6... | collective-permute-start | bytes 1179656 | tf_op jit(solution)/shard_map/ppermute | solution.py:25
  110.7 1.9 %collective-permute-start.4 = (f32[2,3,128,128]{3,2,1,0:T(8,128)S(1)}, f32[2,3,128,128]{3,2,1,0:T(8,128)S(1)}, u32[]{:S(2)}, u32[]{:S(2)}) collective-permute-start(f32[2,3,128,128]{3,2,1,0:T(8,128)S(1)} %reshape_reshape.3), channel_id=1, source_target_pairs={{0,8},{8,16},{16,24},{24,32},{32,40},{40,48},{48,56},{56,64},{64,7... | collective-permute-start | bytes 1179656 | tf_op jit(solution)/shard_map/ppermute | solution.py:22
  112.6 5.7 %collective-permute-done.5 = f32[2,3,128,128]{3,2,1,0:T(8,128)S(1)} collective-permute-done((f32[2,3,128,128]{3,2,1,0:T(8,128)S(1)}, f32[2,3,128,128]{3,2,1,0:T(8,128)S(1)}, u32[]{:S(2)}, u32[]{:S(2)}) %collective-permute-start.5) | collective-permute-done | bytes 393248 | tf_op jit(solution)/shard_map/ppermute | solution.py:25
  118.2 7.2 %collective-permute-done.4 = f32[2,3,128,128]{3,2,1,0:T(8,128)S(1)} collective-permute-done((f32[2,3,128,128]{3,2,1,0:T(8,128)S(1)}, f32[2,3,128,128]{3,2,1,0:T(8,128)S(1)}, u32[]{:S(2)}, u32[]{:S(2)}) %collective-permute-start.4) | collective-permute-done | bytes 393248 | tf_op jit(solution)/shard_map/ppermute | solution.py:22
  125.4 1.1 pad_maximum_fusion.1.win_ref
  126.5 11.1 %shard_map.96 = (f32[8,1024]{1,0:T(8,128)}, f32[1,128]{1,0:T(1,128)}) custom-call(s32[4]{0:T(128)} %and_select_fusion.ids_ref, f32[8]{0:T(128)} %bitcast.57, f32[1]{0:T(128)} %bitcast.8.slope_ref, f32[6,3,128,128]{3,2,1,0:T(8,128)} %pad_maximum_fusion.1.win_ref, s32[8,1024]{1,0:T(8,128)} %bitcast.49, s32[8,1024]{1,0:T(8,128)} %bitcast.51, ...), custom_call_target="tpu_custom_call" | custom-call | tf_op jit(solution)/shard_map/pallas_call | solution.py:203
  137.6 0.6 broadcast_in_dim.13
  138.3 8.9 %all_to_all.21 = f32[8,1,128]{2,1,0:T(1,128)S(1)} all-to-all(f32[8,1,128]{2,1,0:T(1,128)S(1)} %broadcast_in_dim.13), channel_id=1, replica_groups=mesh['tm_0'=4,'tm_hi'=4,'tm_lo'=4,'wafer_0'=4,'wafer_1'=2] {'wafer_0','w..., dimensions={0} | all-to-all | bytes 8192 | tf_op jit(solution)/shard_map/all_to_all | solution.py:55
  147.2 6.0 %psum.10 = f32[128]{0:T(128)S(1)} all-reduce(f32[128]{0:T(128)S(1)} %reduce_sum.42), channel_id=1, replica_groups=mesh['tm_0'=4,'tm_hi'=4,'tm_lo'=4,'wafer_0'=4,'wafer_1'=2] {'tm_0'}, use_global_device_ids=true, to_apply=%region_3.4 | all-reduce | flops 128 | bytes 1024 | tf_op jit(solution)/shard_map/psum | solution.py:250
  153.3 13.8 %all_to_all.22 = f32[16,1,128]{2,1,0:T(1,128)S(1)} all-to-all(f32[16,1,128]{2,1,0:T(1,128)S(1)} %broadcast_in_dim.14), channel_id=1, replica_groups=mesh['tm_0'=4,'tm_hi'=4,'tm_lo'=4,'wafer_0'=4,'wafer_1'=2] {'tm_hi','tm_..., dimensions={0} | all-to-all | bytes 16384 | tf_op jit(solution)/shard_map/all_to_all | solution.py:55
  167.1 0.6 fusion.7
  169.0 0.0 copy-start
  169.0 0.2 broadcast_multiply_fusion
  169.3 0.0 copy-start.2
  169.3 0.0 copy-start.3
  169.3 0.3 mul.95
  169.7 0.4 copy-done
  170.0 0.9 add.67
  171.0 0.0 copy-done.2
  171.0 0.0 copy-done.3
  171.0 0.6 subtract_bitcast_fusion
  (8 shorter events, 0.2 us)
Async XLA Ops:
  0.6 17.5 %copy-start.4 = (s32[1,4]{1,0:T(1,128)S(1)}, s32[1,4]{1,0:T(1,128)}, u32[]{:S(2)}) copy-start(s32[1,4]{1,0:T(1,128)} %param.13) | copy-start | bytes 52
  0.6 18.0 %copy-start.1 = (f32[1,8,1024]{2,1,0:T(8,128)S(1)}, f32[1,8,1024]{2,1,0:T(8,128)}, u32[]{:S(2)}) copy-start(f32[1,8,1024]{2,1,0:T(8,128)} %param.12) | copy-start | bytes 98308
  2.0 21.9 %collective-permute-start.1 = (f32[2,3,128,128]{3,2,1,0:T(8,128)S(1)}, f32[2,3,128,128]{3,2,1,0:T(8,128)S(1)}, u32[]{:S(2)}, u32[]{:S(2)}) collective-permute-start(f32[2,3,128,128]{3,2,1,0:T(8,128)S(1)} %copy.69), channel_id=1, source_target_pairs={{8,0},{16,8},{24,16},{32,24},{40,32},{48,40},{56,48},{64,56},{72,6... | collective-permute-start | bytes 1179656 | tf_op jit(solution)/shard_map/ppermute | solution.py:25
  16.2 14.9 %collective-permute-start = (f32[2,3,128,128]{3,2,1,0:T(8,128)S(1)}, f32[2,3,128,128]{3,2,1,0:T(8,128)S(1)}, u32[]{:S(2)}, u32[]{:S(2)}) collective-permute-start(f32[2,3,128,128]{3,2,1,0:T(8,128)S(1)} %copy.69), channel_id=1, source_target_pairs={{0,8},{8,16},{16,24},{24,32},{32,40},{40,48},{48,56},{56,64},{64,7... | collective-permute-start | bytes 1179656 | tf_op jit(solution)/shard_map/ppermute | solution.py:22
  57.7 14.1 %collective-permute-start.3 = (f32[2,3,16384]{2,0,1:T(2,128)S(1)}, f32[2,3,16384]{2,0,1:T(2,128)S(1)}, u32[]{:S(2)}, u32[]{:S(2)}) collective-permute-start(f32[2,3,16384]{2,0,1:T(2,128)S(1)} %slice.59), channel_id=1, source_target_pairs={{0,8},{8,16},{16,24},{24,32},{32,40},{40,48},{48,56},{56,64},{64,7... | collective-permute-start | bytes 1179656 | tf_op jit(solution)/shard_map/ppermute | solution.py:32
  59.6 13.1 %collective-permute-start.2 = (f32[2,3,16384]{2,0,1:T(2,128)S(1)}, f32[2,3,16384]{2,0,1:T(2,128)S(1)}, u32[]{:S(2)}, u32[]{:S(2)}) collective-permute-start(f32[2,3,16384]{2,0,1:T(2,128)S(1)} %slice.57), channel_id=1, source_target_pairs={{0,504},{8,0},{16,8},{24,16},{32,24},{40,32},{48,40},{56,48},{64,5... | collective-permute-start | bytes 1179656 | tf_op jit(solution)/shard_map/ppermute | solution.py:32
  74.3 15.1 %all-to-all-start = ((f32[8,2,3,2048]{3,1,2,0:T(2,128)}), f32[8,2,3,2048]{3,1,2,0:T(2,128)S(1)}, u32[]{:S(2)}, u32[]{:S(2)}) async-start(f32[8,2,3,2048]{3,1,2,0:T(2,128)} %copy.75), calls=%async_computation | async-start | bytes 786432 | tf_op jit(solution)/shard_map/all_to_all | solution.py:43
  103.2 15.0 %collective-permute-start.5 = (f32[2,3,128,128]{3,2,1,0:T(8,128)S(1)}, f32[2,3,128,128]{3,2,1,0:T(8,128)S(1)}, u32[]{:S(2)}, u32[]{:S(2)}) collective-permute-start(f32[2,3,128,128]{3,2,1,0:T(8,128)S(1)} %reshape_reshape.3), channel_id=1, source_target_pairs={{8,0},{16,8},{24,16},{32,24},{40,32},{48,40},{56,48},{64,56},{72,6... | collective-permute-start | bytes 1179656 | tf_op jit(solution)/shard_map/ppermute | solution.py:25
  110.7 14.7 %collective-permute-start.4 = (f32[2,3,128,128]{3,2,1,0:T(8,128)S(1)}, f32[2,3,128,128]{3,2,1,0:T(8,128)S(1)}, u32[]{:S(2)}, u32[]{:S(2)}) collective-permute-start(f32[2,3,128,128]{3,2,1,0:T(8,128)S(1)} %reshape_reshape.3), channel_id=1, source_target_pairs={{0,8},{8,16},{16,24},{24,32},{32,40},{40,48},{48,56},{56,64},{64,7... | collective-permute-start | bytes 1179656 | tf_op jit(solution)/shard_map/ppermute | solution.py:22
  169.0 1.0 copy-start
  169.3 1.7 copy-start.2
  169.3 1.7 copy-start.3

commit v9 on v8

--- a/solution.py
+++ b/solution.py
@@ -246,9 +246,7 @@
     rescanned, parts = scan_call(
         local_ids, weights, slope_part.reshape(1), dir_window, slot, pix, cos_two, sin_two
     )
-    totals = summed_by_exchange(parts, WAFER)
-    totals = lax.psum(totals, "tm_0")
-    totals = summed_by_exchange(totals, ("tm_hi", "tm_lo"))
+    totals = summed_by_exchange(summed_by_exchange(parts, WAFER), TM)
     step_size = totals[0, 0] / totals[0, 1]
     new_map = sky_map + step_size * direction
     new_residual = (resid - step_size * rescanned)[None]

time: 175 us -> 170 us (0.971); the launches traced: 172 us -> 169 us
  blocking collectives: 40.4 us -> 37.7 us
    psum x1 -> x0, blocking collectives: 5.99 us -> none  [local(): totals = lax.psum(totals, 'tm_0')]
    all_to_all x3, blocking collectives: 34.4 us -> 37.7 us  [copy_for_each(): return lax.all_to_all(copies, axis, split_axis=0, concat_axis=0, tiled=True)]
where the time goes in v9:
time: 170 us; the launch traced here: 169 us
  starting transfers between devices  41.4 us (24%)
  waiting for transfers between devices  38.3 us (23%)
  blocking collectives  37.7 us (22%)
  Pallas kernels  34.7 us (20%)
  other arithmetic  7.3 us (4%)
  local copies, waits for them, and re-layouts  7.25 us (4%)
  between operations  2.21 us (1%)
    all_to_all x3, blocking collectives, copy_for_each(): return lax.all_to_all(copies, axis, split_axis=0, concat_axis=0, tiled=True)  37.7 us
    pallas_call x1, Pallas kernels, bin_call(): pl.pallas_call(bin_kernel, out_shape=(jax.ShapeDtypeStruct((dets, samp),...  23.6 us
    ppermute x2, starting transfers between devices, with_halo(): lax.ppermute(lax.slice_in_dim(block, 0, width, axis=dim), axis, backward)  21.6 us
    ppermute x2, waiting for transfers between devices, with_halo(): lax.ppermute(lax.slice_in_dim(block, block.shape[dim] - width, None, axis...  14.3 us
    pallas_call x1, Pallas kernels, scan_call(): pl.pallas_call(scan_kernel, out_shape=(jax.ShapeDtypeStruct(slot.shape, j...  11.1 us
    ppermute x2, waiting for transfers between devices, with_halo(): lax.ppermute(lax.slice_in_dim(block, 0, width, axis=dim), axis, backward)  10.2 us
    ppermute x2, starting transfers between devices, passed_along(): lax.ppermute(value, axis, [(i, (i + by) % count) for i in range(count)])  8.6 us
    all_to_all x1, waiting for transfers between devices, sum_at_owner(): parts = lax.all_to_all(in_blocks(value, dim, count), axis, 0, 0, tiled=True)  7.7 us
  transfers between devices with their start and end apart: 7, of which 7 were waited for; matrix products, arithmetic and copies ran while one was open for 1% of the time, Pallas kernels for 0%

profile of v9, /device:TPU:1, one launch (start us, length us, event | category | flops | bytes accessed | tf_op | source)
XLA Modules:
  0.0 168.9 jit_solution(16946947648206294444)
XLA Ops:
  0.6 0.0 copy-start.4
  0.6 0.0 copy-start.1
  0.6 1.3 reshape.32
  2.0 14.1 %collective-permute-start.1 = (f32[2,3,128,128]{3,2,1,0:T(8,128)S(1)}, f32[2,3,128,128]{3,2,1,0:T(8,128)S(1)}, u32[]{:S(2)}, u32[]{:S(2)}) collective-permute-start(f32[2,3,128,128]{3,2,1,0:T(8,128)S(1)} %copy.69), channel_id=1, source_target_pairs={{8,0},{16,8},{24,16},{32,24},{40,32},{48,40},{56,48},{64,56},{72,6... | collective-permute-start | bytes 1179656 | tf_op jit(solution)/shard_map/ppermute | solution.py:25
  16.2 1.9 %collective-permute-start = (f32[2,3,128,128]{3,2,1,0:T(8,128)S(1)}, f32[2,3,128,128]{3,2,1,0:T(8,128)S(1)}, u32[]{:S(2)}, u32[]{:S(2)}) collective-permute-start(f32[2,3,128,128]{3,2,1,0:T(8,128)S(1)} %copy.69), channel_id=1, source_target_pairs={{0,8},{8,16},{16,24},{24,32},{32,40},{40,48},{48,56},{56,64},{64,7... | collective-permute-start | bytes 1179656 | tf_op jit(solution)/shard_map/ppermute | solution.py:22
  18.1 0.0 copy-done.4
  18.1 0.5 and_select_fusion.ids_ref
  18.7 0.0 copy-done.1
  18.7 0.8 sine_bitcast_fusion
  19.4 4.5 %collective-permute-done.1 = f32[2,3,128,128]{3,2,1,0:T(8,128)S(1)} collective-permute-done((f32[2,3,128,128]{3,2,1,0:T(8,128)S(1)}, f32[2,3,128,128]{3,2,1,0:T(8,128)S(1)}, u32[]{:S(2)}, u32[]{:S(2)}) %collective-permute-start.1) | collective-permute-done | bytes 393248 | tf_op jit(solution)/shard_map/ppermute | solution.py:25
  24.0 7.2 %collective-permute-done = f32[2,3,128,128]{3,2,1,0:T(8,128)S(1)} collective-permute-done((f32[2,3,128,128]{3,2,1,0:T(8,128)S(1)}, f32[2,3,128,128]{3,2,1,0:T(8,128)S(1)}, u32[]{:S(2)}, u32[]{:S(2)}) %collective-permute-start) | collective-permute-done | bytes 393248 | tf_op jit(solution)/shard_map/ppermute | solution.py:22
  31.1 1.1 pad_maximum_fusion.win_ref
  32.2 23.6 %shard_map.95 = (f32[8,1024]{1,0:T(8,128)}, f32[6,3,128,128]{3,2,1,0:T(8,128)}) custom-call(s32[4]{0:T(128)} %and_select_fusion.ids_ref, f32[8]{0:T(128)} %bitcast.56, f32[6,3,128,128]{3,2,1,0:T(8,128)} %pad_maximum_fusion.win_ref, s32[8,1024]{1,0:T(8,128)} %bitcast.48, s32[8,1024]{1,0:T(8,128)} %bitcast.50, f32[8,1024]{1,0:T(8,128)} %get-tuple-element.19.cos_ref, ...), custom_call_target="tpu_custom_call" | custom-call | tf_op jit(solution)/shard_map/pallas_call | solution.py:183
  55.8 1.3 fusion.6
  57.2 0.2 slice.57
  57.5 0.2 slice.59
  57.7 1.9 %collective-permute-start.3 = (f32[2,3,16384]{2,0,1:T(2,128)S(1)}, f32[2,3,16384]{2,0,1:T(2,128)S(1)}, u32[]{:S(2)}, u32[]{:S(2)}) collective-permute-start(f32[2,3,16384]{2,0,1:T(2,128)S(1)} %slice.59), channel_id=1, source_target_pairs={{0,8},{8,16},{16,24},{24,32},{32,40},{40,48},{48,56},{56,64},{64,7... | collective-permute-start | bytes 1179656 | tf_op jit(solution)/shard_map/ppermute | solution.py:32
  59.6 6.7 %collective-permute-start.2 = (f32[2,3,16384]{2,0,1:T(2,128)S(1)}, f32[2,3,16384]{2,0,1:T(2,128)S(1)}, u32[]{:S(2)}, u32[]{:S(2)}) collective-permute-start(f32[2,3,16384]{2,0,1:T(2,128)S(1)} %slice.57), channel_id=1, source_target_pairs={{0,504},{8,0},{16,8},{24,16},{32,24},{40,32},{48,40},{56,48},{64,5... | collective-permute-start | bytes 1179656 | tf_op jit(solution)/shard_map/ppermute | solution.py:32
  66.4 0.2 slice.55
  66.6 5.2 %collective-permute-done.3 = f32[2,3,16384]{2,0,1:T(2,128)S(1)} collective-permute-done((f32[2,3,16384]{2,0,1:T(2,128)S(1)}, f32[2,3,16384]{2,0,1:T(2,128)S(1)}, u32[]{:S(2)}, u32[]{:S(2)}) %collective-permute-start.3) | collective-permute-done | bytes 393248 | tf_op jit(solution)/shard_map/ppermute | solution.py:32
  71.8 0.9 collective-permute-done.2
  72.7 0.3 add_add_fusion
  73.0 0.3 reshape.33
  73.3 1.1 copy.75
  74.4 7.4 %all-to-all-start = ((f32[8,2,3,2048]{3,1,2,0:T(2,128)}), f32[8,2,3,2048]{3,1,2,0:T(2,128)S(1)}, u32[]{:S(2)}, u32[]{:S(2)}) async-start(f32[8,2,3,2048]{3,1,2,0:T(2,128)} %copy.75), calls=%async_computation | async-start | bytes 786432 | tf_op jit(solution)/shard_map/all_to_all | solution.py:43
  81.8 7.7 %all-to-all-done = f32[8,2,3,2048]{3,1,2,0:T(2,128)S(1)} async-done(((f32[8,2,3,2048]{3,1,2,0:T(2,128)}), f32[8,2,3,2048]{3,1,2,0:T(2,128)S(1)}, u32[]{:S(2)}, u32[]{:S(2)}) %all-to-all-start) | async-done | bytes 393248 | tf_op jit(solution)/shard_map/all_to_all | solution.py:43
  89.5 0.1 reduce_sum.38
  89.6 0.9 fusion.4
  90.5 0.7 multiply_reduce_fusion
  91.1 0.2 broadcast_in_dim.12
  91.3 11.7 %all_to_all.20 = f32[8,2,3,2048]{3,1,2,0:T(2,128)S(1)} all-to-all(f32[8,2,3,2048]{3,1,2,0:T(2,128)S(1)} %broadcast_in_dim.12), channel_id=1, replica_groups=mesh['tm_0'=4,'tm_hi'=4,'tm_lo'=4,'wafer_0'=4,'wafer_1'=2] {'wafer_0','w..., dimensions={0} | all-to-all | bytes 786432 | tf_op jit(solution)/shard_map/all_to_all | solution.py:55
  102.9 0.2 copy.85
  103.2 0.1 reshape_reshape.3
  103.2 7.4 %collective-permute-start.5 = (f32[2,3,128,128]{3,2,1,0:T(8,128)S(1)}, f32[2,3,128,128]{3,2,1,0:T(8,128)S(1)}, u32[]{:S(2)}, u32[]{:S(2)}) collective-permute-start(f32[2,3,128,128]{3,2,1,0:T(8,128)S(1)} %reshape_reshape.3), channel_id=1, source_target_pairs={{8,0},{16,8},{24,16},{32,24},{40,32},{48,40},{56,48},{64,56},{72,6... | collective-permute-start | bytes 1179656 | tf_op jit(solution)/shard_map/ppermute | solution.py:25
  110.7 1.9 %collective-permute-start.4 = (f32[2,3,128,128]{3,2,1,0:T(8,128)S(1)}, f32[2,3,128,128]{3,2,1,0:T(8,128)S(1)}, u32[]{:S(2)}, u32[]{:S(2)}) collective-permute-start(f32[2,3,128,128]{3,2,1,0:T(8,128)S(1)} %reshape_reshape.3), channel_id=1, source_target_pairs={{0,8},{8,16},{16,24},{24,32},{32,40},{40,48},{48,56},{56,64},{64,7... | collective-permute-start | bytes 1179656 | tf_op jit(solution)/shard_map/ppermute | solution.py:22
  112.6 5.7 %collective-permute-done.5 = f32[2,3,128,128]{3,2,1,0:T(8,128)S(1)} collective-permute-done((f32[2,3,128,128]{3,2,1,0:T(8,128)S(1)}, f32[2,3,128,128]{3,2,1,0:T(8,128)S(1)}, u32[]{:S(2)}, u32[]{:S(2)}) %collective-permute-start.5) | collective-permute-done | bytes 393248 | tf_op jit(solution)/shard_map/ppermute | solution.py:25
  118.3 7.2 %collective-permute-done.4 = f32[2,3,128,128]{3,2,1,0:T(8,128)S(1)} collective-permute-done((f32[2,3,128,128]{3,2,1,0:T(8,128)S(1)}, f32[2,3,128,128]{3,2,1,0:T(8,128)S(1)}, u32[]{:S(2)}, u32[]{:S(2)}) %collective-permute-start.4) | collective-permute-done | bytes 393248 | tf_op jit(solution)/shard_map/ppermute | solution.py:22
  125.4 1.1 pad_maximum_fusion.1.win_ref
  126.5 11.1 %shard_map.96 = (f32[8,1024]{1,0:T(8,128)}, f32[1,128]{1,0:T(1,128)}) custom-call(s32[4]{0:T(128)} %and_select_fusion.ids_ref, f32[8]{0:T(128)} %bitcast.57, f32[1]{0:T(128)} %bitcast.8.slope_ref, f32[6,3,128,128]{3,2,1,0:T(8,128)} %pad_maximum_fusion.1.win_ref, s32[8,1024]{1,0:T(8,128)} %bitcast.49, s32[8,1024]{1,0:T(8,128)} %bitcast.51, ...), custom_call_target="tpu_custom_call" | custom-call | tf_op jit(solution)/shard_map/pallas_call | solution.py:203
  137.7 0.6 broadcast_in_dim.13
  138.3 8.9 %all_to_all.21 = f32[8,1,128]{2,1,0:T(1,128)S(1)} all-to-all(f32[8,1,128]{2,1,0:T(1,128)S(1)} %broadcast_in_dim.13), channel_id=1, replica_groups=mesh['tm_0'=4,'tm_hi'=4,'tm_lo'=4,'wafer_0'=4,'wafer_1'=2] {'wafer_0','w..., dimensions={0} | all-to-all | bytes 8192 | tf_op jit(solution)/shard_map/all_to_all | solution.py:55
  147.3 17.1 %all_to_all.22 = f32[64,1,128]{2,1,0:T(1,128)S(1)} all-to-all(f32[64,1,128]{2,1,0:T(1,128)S(1)} %broadcast_in_dim.14), channel_id=1, replica_groups=mesh['tm_0'=4,'tm_hi'=4,'tm_lo'=4,'wafer_0'=4,'wafer_1'=2] {'tm_0','tm_h..., dimensions={0} | all-to-all | bytes 65536 | tf_op jit(solution)/shard_map/all_to_all | solution.py:55
  164.4 0.6 fusion.7
  166.3 0.0 copy-start
  166.4 0.2 broadcast_multiply_fusion
  166.6 0.0 copy-start.2
  166.6 0.0 copy-start.3
  166.7 0.3 mul.95
  167.0 0.4 copy-done
  167.3 0.9 add.65
  168.3 0.0 copy-done.2
  168.3 0.0 copy-done.3
  168.3 0.6 subtract_bitcast_fusion
  (8 shorter events, 0.2 us)
Async XLA Ops:
  0.6 17.5 %copy-start.4 = (s32[1,4]{1,0:T(1,128)S(1)}, s32[1,4]{1,0:T(1,128)}, u32[]{:S(2)}) copy-start(s32[1,4]{1,0:T(1,128)} %param.13) | copy-start | bytes 52
  0.6 18.0 %copy-start.1 = (f32[1,8,1024]{2,1,0:T(8,128)S(1)}, f32[1,8,1024]{2,1,0:T(8,128)}, u32[]{:S(2)}) copy-start(f32[1,8,1024]{2,1,0:T(8,128)} %param.12) | copy-start | bytes 98308
  2.0 21.9 %collective-permute-start.1 = (f32[2,3,128,128]{3,2,1,0:T(8,128)S(1)}, f32[2,3,128,128]{3,2,1,0:T(8,128)S(1)}, u32[]{:S(2)}, u32[]{:S(2)}) collective-permute-start(f32[2,3,128,128]{3,2,1,0:T(8,128)S(1)} %copy.69), channel_id=1, source_target_pairs={{8,0},{16,8},{24,16},{32,24},{40,32},{48,40},{56,48},{64,56},{72,6... | collective-permute-start | bytes 1179656 | tf_op jit(solution)/shard_map/ppermute | solution.py:25
  16.2 14.9 %collective-permute-start = (f32[2,3,128,128]{3,2,1,0:T(8,128)S(1)}, f32[2,3,128,128]{3,2,1,0:T(8,128)S(1)}, u32[]{:S(2)}, u32[]{:S(2)}) collective-permute-start(f32[2,3,128,128]{3,2,1,0:T(8,128)S(1)} %copy.69), channel_id=1, source_target_pairs={{0,8},{8,16},{16,24},{24,32},{32,40},{40,48},{48,56},{56,64},{64,7... | collective-permute-start | bytes 1179656 | tf_op jit(solution)/shard_map/ppermute | solution.py:22
  57.7 14.1 %collective-permute-start.3 = (f32[2,3,16384]{2,0,1:T(2,128)S(1)}, f32[2,3,16384]{2,0,1:T(2,128)S(1)}, u32[]{:S(2)}, u32[]{:S(2)}) collective-permute-start(f32[2,3,16384]{2,0,1:T(2,128)S(1)} %slice.59), channel_id=1, source_target_pairs={{0,8},{8,16},{16,24},{24,32},{32,40},{40,48},{48,56},{56,64},{64,7... | collective-permute-start | bytes 1179656 | tf_op jit(solution)/shard_map/ppermute | solution.py:32
  59.6 13.1 %collective-permute-start.2 = (f32[2,3,16384]{2,0,1:T(2,128)S(1)}, f32[2,3,16384]{2,0,1:T(2,128)S(1)}, u32[]{:S(2)}, u32[]{:S(2)}) collective-permute-start(f32[2,3,16384]{2,0,1:T(2,128)S(1)} %slice.57), channel_id=1, source_target_pairs={{0,504},{8,0},{16,8},{24,16},{32,24},{40,32},{48,40},{56,48},{64,5... | collective-permute-start | bytes 1179656 | tf_op jit(solution)/shard_map/ppermute | solution.py:32
  74.4 15.1 %all-to-all-start = ((f32[8,2,3,2048]{3,1,2,0:T(2,128)}), f32[8,2,3,2048]{3,1,2,0:T(2,128)S(1)}, u32[]{:S(2)}, u32[]{:S(2)}) async-start(f32[8,2,3,2048]{3,1,2,0:T(2,128)} %copy.75), calls=%async_computation | async-start | bytes 786432 | tf_op jit(solution)/shard_map/all_to_all | solution.py:43
  103.2 15.0 %collective-permute-start.5 = (f32[2,3,128,128]{3,2,1,0:T(8,128)S(1)}, f32[2,3,128,128]{3,2,1,0:T(8,128)S(1)}, u32[]{:S(2)}, u32[]{:S(2)}) collective-permute-start(f32[2,3,128,128]{3,2,1,0:T(8,128)S(1)} %reshape_reshape.3), channel_id=1, source_target_pairs={{8,0},{16,8},{24,16},{32,24},{40,32},{48,40},{56,48},{64,56},{72,6... | collective-permute-start | bytes 1179656 | tf_op jit(solution)/shard_map/ppermute | solution.py:25
  110.7 14.7 %collective-permute-start.4 = (f32[2,3,128,128]{3,2,1,0:T(8,128)S(1)}, f32[2,3,128,128]{3,2,1,0:T(8,128)S(1)}, u32[]{:S(2)}, u32[]{:S(2)}) collective-permute-start(f32[2,3,128,128]{3,2,1,0:T(8,128)S(1)} %reshape_reshape.3), channel_id=1, source_target_pairs={{0,8},{8,16},{16,24},{24,32},{32,40},{40,48},{48,56},{56,64},{64,7... | collective-permute-start | bytes 1179656 | tf_op jit(solution)/shard_map/ppermute | solution.py:22
  166.3 1.0 copy-start
  166.6 1.7 copy-start.2
  166.6 1.7 copy-start.3

commit v10 on v9

--- a/solution.py
+++ b/solution.py
@@ -231,10 +231,12 @@
     window = with_halo(as_grid(sky_map), ((TM, 0),), tiles_dev)
     resid, binned = bin_call(local_ids, weights, window, slot, pix, cos_two, sin_two, timestream[0])
     near_tiles = binned.reshape(binned.shape[0], 3, pixels)
-    from_upper = passed_along(near_tiles[:tiles_dev], TM, -1)
-    from_lower = passed_along(near_tiles[2 * tiles_dev :], TM, 1)
-    owned_tiles = near_tiles[tiles_dev : 2 * tiles_dev] + from_upper + from_lower
-    grad_share = sum_at_owner(owned_tiles, WAFER, 2)
+    wafers = lax.axis_size(WAFER)
+    near_blocks = in_blocks(near_tiles, 2, wafers)
+    from_upper = passed_along(near_blocks[:, :tiles_dev], TM, -1)
+    from_lower = passed_along(near_blocks[:, 2 * tiles_dev :], TM, 1)
+    owned_blocks = near_blocks[:, tiles_dev : 2 * tiles_dev] + from_upper + from_lower
+    grad_share = jnp.sum(lax.all_to_all(owned_blocks, WAFER, 0, 0, tiled=True), axis=0)
     share_width = grad_share.shape[2]
     inverse_share = lax.dynamic_slice_in_dim(
         precond, lax.axis_index(WAFER) * share_width, share_width, 2

time: 170 us -> 168 us (0.988)
  waiting for transfers between devices: 38.3 us -> 32.8 us
  blocking collectives: 37.7 us -> 41.5 us
    ppermute x2, waiting for transfers between devices: 10.2 us -> 1.8 us  [with_halo(): lax.ppermute(lax.slice_in_dim(block, 0, width, axis=dim), axis, backward)]
    ppermute x2, waiting for transfers between devices: 6.09 us -> 12.1 us  [passed_along(): lax.ppermute(value, axis, [(i, (i + by) % count) for i in range(count)])]
    all_to_all x3, blocking collectives: 37.7 us -> 41.5 us  [copy_for_each(): return lax.all_to_all(copies, axis, split_axis=0, concat_axis=0, tiled=True)]
    ppermute x2, starting transfers between devices: 21.6 us -> 18.4 us  [with_halo(): lax.ppermute(lax.slice_in_dim(block, 0, width, axis=dim), axis, backward)]
    ppermute x2, starting transfers between devices: 3.84 us -> 6.28 us  [with_halo(): lax.ppermute(lax.slice_in_dim(block, block.shape[dim] - width, None, axis...]
    ppermute x2, waiting for transfers between devices: 14.3 us -> 12 us  [with_halo(): lax.ppermute(lax.slice_in_dim(block, block.shape[dim] - width, None, axis...]
    another operation x0 -> x3, local copies, waits for them, and re-layouts: none -> 2.2 us  [the longest x2 2.16 us: in_blocks(): value.reshape(*shape[:dim], count, shape[dim] // count, *shape[dim + 1:])]
where the time goes in v10:
time: 168 us; the launch traced here: 167 us
  blocking collectives  41.5 us (25%)
  starting transfers between devices  41.1 us (24%)
  Pallas kernels  34.7 us (21%)
  waiting for transfers between devices  32.8 us (20%)
  other arithmetic  7.38 us (4%)
  local copies, waits for them, and re-layouts  7.28 us (4%)
  between operations  2.19 us (1%)
    all_to_all x3, blocking collectives, copy_for_each(): return lax.all_to_all(copies, axis, split_axis=0, concat_axis=0, tiled=True)  41.5 us
    pallas_call x1, Pallas kernels, bin_call(): pl.pallas_call(bin_kernel, out_shape=(jax.ShapeDtypeStruct((dets, samp),...  23.6 us
    ppermute x2, starting transfers between devices, with_halo(): lax.ppermute(lax.slice_in_dim(block, 0, width, axis=dim), axis, backward)  18.4 us
    ppermute x2, waiting for transfers between devices, passed_along(): lax.ppermute(value, axis, [(i, (i + by) % count) for i in range(count)])  12.1 us
    ppermute x2, waiting for transfers between devices, with_halo(): lax.ppermute(lax.slice_in_dim(block, block.shape[dim] - width, None, axis...  12 us
    pallas_call x1, Pallas kernels, scan_call(): pl.pallas_call(scan_kernel, out_shape=(jax.ShapeDtypeStruct(slot.shape, j...  11.1 us
    ppermute x2, starting transfers between devices, passed_along(): lax.ppermute(value, axis, [(i, (i + by) % count) for i in range(count)])  9.35 us
    all_to_all x1, starting transfers between devices, local(): lax.all_to_all(owned_blocks, WAFER, 0, 0, tiled=True)  7.13 us
  transfers between devices with their start and end apart: 7, of which 7 were waited for; matrix products, arithmetic and copies ran while one was open for 1% of the time, Pallas kernels for 0%

profile of v10, /device:TPU:1, one launch (start us, length us, event | category | flops | bytes accessed | tf_op | source)
XLA Modules:
  0.0 167.1 jit_solution(11916773955233864522)
XLA Ops:
  0.6 0.0 copy-start.4
  0.6 0.0 copy-start.1
  0.6 1.3 reshape.25
  2.0 4.4 %collective-permute-start = (f32[2,3,128,128]{3,2,1,0:T(8,128)S(1)}, f32[2,3,128,128]{3,2,1,0:T(8,128)S(1)}, u32[]{:S(2)}, u32[]{:S(2)}) collective-permute-start(f32[2,3,128,128]{3,2,1,0:T(8,128)S(1)} %copy.62), channel_id=1, source_target_pairs={{0,8},{8,16},{16,24},{24,32},{32,40},{40,48},{48,56},{56,64},{64,7... | collective-permute-start | bytes 1179656 | tf_op jit(solution)/shard_map/ppermute | solution.py:22
  6.4 11.7 %collective-permute-start.1 = (f32[2,3,128,128]{3,2,1,0:T(8,128)S(1)}, f32[2,3,128,128]{3,2,1,0:T(8,128)S(1)}, u32[]{:S(2)}, u32[]{:S(2)}) collective-permute-start(f32[2,3,128,128]{3,2,1,0:T(8,128)S(1)} %copy.62), channel_id=1, source_target_pairs={{8,0},{16,8},{24,16},{32,24},{40,32},{48,40},{56,48},{64,56},{72,6... | collective-permute-start | bytes 1179656 | tf_op jit(solution)/shard_map/ppermute | solution.py:25
  18.1 0.0 copy-done.4
  18.1 0.5 and_select_fusion.ids_ref
  18.6 0.0 copy-done.1
  18.6 0.7 sine_bitcast_fusion
  19.4 5.6 %collective-permute-done = f32[2,3,128,128]{3,2,1,0:T(8,128)S(1)} collective-permute-done((f32[2,3,128,128]{3,2,1,0:T(8,128)S(1)}, f32[2,3,128,128]{3,2,1,0:T(8,128)S(1)}, u32[]{:S(2)}, u32[]{:S(2)}) %collective-permute-start) | collective-permute-done | bytes 393248 | tf_op jit(solution)/shard_map/ppermute | solution.py:22
  25.0 0.9 collective-permute-done.1
  25.9 1.1 pad_maximum_fusion.win_ref
  27.0 23.6 %shard_map.95 = (f32[8,1024]{1,0:T(8,128)}, f32[6,3,128,128]{3,2,1,0:T(8,128)}) custom-call(s32[4]{0:T(128)} %and_select_fusion.ids_ref, f32[8]{0:T(128)} %bitcast.47, f32[6,3,128,128]{3,2,1,0:T(8,128)} %pad_maximum_fusion.win_ref, s32[8,1024]{1,0:T(8,128)} %bitcast.39, s32[8,1024]{1,0:T(8,128)} %bitcast.41, f32[8,1024]{1,0:T(8,128)} %get-tuple-element.24.cos_ref, ...), custom_call_target="tpu_custom_call" | custom-call | tf_op jit(solution)/shard_map/pallas_call | solution.py:183
  50.6 1.5 reshape_reshape.6
  52.1 0.7 copy.107
  52.8 0.4 fusion.7
  53.2 7.4 %collective-permute-start.2 = (f32[8,2,3,2048]{3,1,2,0:T(2,128)S(1)}, f32[8,2,3,2048]{3,1,2,0:T(2,128)S(1)}, u32[]{:S(2)}, u32[]{:S(2)}) collective-permute-start(f32[8,2,3,2048]{3,1,2,0:T(2,128)S(1)} %get-tuple-element.10), channel_id=1, source_target_pairs={{0,504},{8,0},{16,8},{24,16},{32,24},{40,32},{48,40},{56,48},{64,5... | collective-permute-start | bytes 1179656 | tf_op jit(solution)/shard_map/ppermute | solution.py:32
  60.6 1.9 %collective-permute-start.3 = (f32[8,2,3,2048]{3,1,2,0:T(2,128)S(1)}, f32[8,2,3,2048]{3,1,2,0:T(2,128)S(1)}, u32[]{:S(2)}, u32[]{:S(2)}) collective-permute-start(f32[8,2,3,2048]{3,1,2,0:T(2,128)S(1)} %get-tuple-element.11), channel_id=1, source_target_pairs={{0,8},{8,16},{16,24},{24,32},{32,40},{40,48},{48,56},{56,64},{64,7... | collective-permute-start | bytes 1179656 | tf_op jit(solution)/shard_map/ppermute | solution.py:32
  62.6 5.0 %collective-permute-done.2 = f32[8,2,3,2048]{3,1,2,0:T(2,128)S(1)} collective-permute-done((f32[8,2,3,2048]{3,1,2,0:T(2,128)S(1)}, f32[8,2,3,2048]{3,1,2,0:T(2,128)S(1)}, u32[]{:S(2)}, u32[]{:S(2)}) %collective-permute-start.2) | collective-permute-done | bytes 393248 | tf_op jit(solution)/shard_map/ppermute | solution.py:32
  67.6 7.2 %collective-permute-done.3 = f32[8,2,3,2048]{3,1,2,0:T(2,128)S(1)} collective-permute-done((f32[8,2,3,2048]{3,1,2,0:T(2,128)S(1)}, f32[8,2,3,2048]{3,1,2,0:T(2,128)S(1)}, u32[]{:S(2)}, u32[]{:S(2)}) %collective-permute-start.3) | collective-permute-done | bytes 393248 | tf_op jit(solution)/shard_map/ppermute | solution.py:32
  74.7 1.1 fusion
  75.9 7.1 %all-to-all-start = ((f32[8,2,3,2048]{3,1,2,0:T(2,128)}), f32[8,2,3,2048]{3,1,2,0:T(2,128)S(1)}, u32[]{:S(2)}, u32[]{:S(2)}) async-start(f32[8,2,3,2048]{3,1,2,0:T(2,128)} %fusion), calls=%async_computation | async-start | bytes 786432 | tf_op jit(solution)/shard_map/all_to_all | solution.py:239
  83.0 0.8 constant_dynamic-slice_fusion.4
  83.8 6.9 %all-to-all-done = f32[8,2,3,2048]{3,1,2,0:T(2,128)S(1)} async-done(((f32[8,2,3,2048]{3,1,2,0:T(2,128)}), f32[8,2,3,2048]{3,1,2,0:T(2,128)S(1)}, u32[]{:S(2)}, u32[]{:S(2)}) %all-to-all-start) | async-done | bytes 393248 | tf_op jit(solution)/shard_map/all_to_all | solution.py:239
  90.7 0.1 reduce_sum.38
  90.9 0.1 fusion.5
  91.0 0.7 pad_maximum_fusion.2
  91.7 0.2 broadcast_in_dim.12
  91.9 11.7 %all_to_all.20 = f32[8,2,3,2048]{3,1,2,0:T(2,128)S(1)} all-to-all(f32[8,2,3,2048]{3,1,2,0:T(2,128)S(1)} %broadcast_in_dim.12), channel_id=1, replica_groups=mesh['tm_0'=4,'tm_hi'=4,'tm_lo'=4,'wafer_0'=4,'wafer_1'=2] {'wafer_0','w..., dimensions={0} | all-to-all | bytes 786432 | tf_op jit(solution)/shard_map/all_to_all | solution.py:55
  103.5 0.2 copy.108
  103.8 0.1 reshape_reshape.7
  103.8 1.9 %collective-permute-start.4 = (f32[2,3,128,128]{3,2,1,0:T(8,128)S(1)}, f32[2,3,128,128]{3,2,1,0:T(8,128)S(1)}, u32[]{:S(2)}, u32[]{:S(2)}) collective-permute-start(f32[2,3,128,128]{3,2,1,0:T(8,128)S(1)} %reshape_reshape.7), channel_id=1, source_target_pairs={{0,8},{8,16},{16,24},{24,32},{32,40},{40,48},{48,56},{56,64},{64,7... | collective-permute-start | bytes 1179656 | tf_op jit(solution)/shard_map/ppermute | solution.py:22
  105.8 6.7 %collective-permute-start.5 = (f32[2,3,128,128]{3,2,1,0:T(8,128)S(1)}, f32[2,3,128,128]{3,2,1,0:T(8,128)S(1)}, u32[]{:S(2)}, u32[]{:S(2)}) collective-permute-start(f32[2,3,128,128]{3,2,1,0:T(8,128)S(1)} %reshape_reshape.7), channel_id=1, source_target_pairs={{8,0},{16,8},{24,16},{32,24},{40,32},{48,40},{56,48},{64,56},{72,6... | collective-permute-start | bytes 1179656 | tf_op jit(solution)/shard_map/ppermute | solution.py:25
  112.4 6.4 %collective-permute-done.4 = f32[2,3,128,128]{3,2,1,0:T(8,128)S(1)} collective-permute-done((f32[2,3,128,128]{3,2,1,0:T(8,128)S(1)}, f32[2,3,128,128]{3,2,1,0:T(8,128)S(1)}, u32[]{:S(2)}, u32[]{:S(2)}) %collective-permute-start.4) | collective-permute-done | bytes 393248 | tf_op jit(solution)/shard_map/ppermute | solution.py:22
  118.9 0.9 collective-permute-done.5
  119.8 1.1 pad_maximum_fusion.1.win_ref
  120.9 11.1 %shard_map.96 = (f32[8,1024]{1,0:T(8,128)}, f32[1,128]{1,0:T(1,128)}) custom-call(s32[4]{0:T(128)} %and_select_fusion.ids_ref, f32[8]{0:T(128)} %bitcast.48, f32[1]{0:T(128)} %bitcast.8.slope_ref, f32[6,3,128,128]{3,2,1,0:T(8,128)} %pad_maximum_fusion.1.win_ref, s32[8,1024]{1,0:T(8,128)} %bitcast.40, s32[8,1024]{1,0:T(8,128)} %bitcast.42, ...), custom_call_target="tpu_custom_call" | custom-call | tf_op jit(solution)/shard_map/pallas_call | solution.py:203
  132.0 0.6 broadcast_in_dim.13
  132.6 8.9 %all_to_all.21 = f32[8,1,128]{2,1,0:T(1,128)S(1)} all-to-all(f32[8,1,128]{2,1,0:T(1,128)S(1)} %broadcast_in_dim.13), channel_id=1, replica_groups=mesh['tm_0'=4,'tm_hi'=4,'tm_lo'=4,'wafer_0'=4,'wafer_1'=2] {'wafer_0','w..., dimensions={0} | all-to-all | bytes 8192 | tf_op jit(solution)/shard_map/all_to_all | solution.py:55
  141.6 20.9 %all_to_all.22 = f32[64,1,128]{2,1,0:T(1,128)S(1)} all-to-all(f32[64,1,128]{2,1,0:T(1,128)S(1)} %broadcast_in_dim.14), channel_id=1, replica_groups=mesh['tm_0'=4,'tm_hi'=4,'tm_lo'=4,'wafer_0'=4,'wafer_1'=2] {'tm_0','tm_h..., dimensions={0} | all-to-all | bytes 65536 | tf_op jit(solution)/shard_map/all_to_all | solution.py:55
  162.6 0.6 fusion.8
  164.5 0.0 copy-start
  164.5 0.2 broadcast_multiply_fusion
  164.8 0.0 copy-start.2
  164.8 0.0 copy-start.3
  164.8 0.3 mul.95
  165.1 0.4 copy-done
  165.5 0.9 add.65
  166.5 0.0 copy-done.2
  166.5 0.0 copy-done.3
  166.5 0.6 subtract_bitcast_fusion
  (7 shorter events, 0.2 us)
Async XLA Ops:
  0.6 17.5 %copy-start.4 = (s32[1,4]{1,0:T(1,128)S(1)}, s32[1,4]{1,0:T(1,128)}, u32[]{:S(2)}) copy-start(s32[1,4]{1,0:T(1,128)} %param.13) | copy-start | bytes 52
  0.6 18.0 %copy-start.1 = (f32[1,8,1024]{2,1,0:T(8,128)S(1)}, f32[1,8,1024]{2,1,0:T(8,128)}, u32[]{:S(2)}) copy-start(f32[1,8,1024]{2,1,0:T(8,128)} %param.12) | copy-start | bytes 98308
  2.0 22.9 %collective-permute-start = (f32[2,3,128,128]{3,2,1,0:T(8,128)S(1)}, f32[2,3,128,128]{3,2,1,0:T(8,128)S(1)}, u32[]{:S(2)}, u32[]{:S(2)}) collective-permute-start(f32[2,3,128,128]{3,2,1,0:T(8,128)S(1)} %copy.62), channel_id=1, source_target_pairs={{0,8},{8,16},{16,24},{24,32},{32,40},{40,48},{48,56},{56,64},{64,7... | collective-permute-start | bytes 1179656 | tf_op jit(solution)/shard_map/ppermute | solution.py:22
  6.4 19.5 %collective-permute-start.1 = (f32[2,3,128,128]{3,2,1,0:T(8,128)S(1)}, f32[2,3,128,128]{3,2,1,0:T(8,128)S(1)}, u32[]{:S(2)}, u32[]{:S(2)}) collective-permute-start(f32[2,3,128,128]{3,2,1,0:T(8,128)S(1)} %copy.62), channel_id=1, source_target_pairs={{8,0},{16,8},{24,16},{32,24},{40,32},{48,40},{56,48},{64,56},{72,6... | collective-permute-start | bytes 1179656 | tf_op jit(solution)/shard_map/ppermute | solution.py:25
  53.2 14.4 %collective-permute-start.2 = (f32[8,2,3,2048]{3,1,2,0:T(2,128)S(1)}, f32[8,2,3,2048]{3,1,2,0:T(2,128)S(1)}, u32[]{:S(2)}, u32[]{:S(2)}) collective-permute-start(f32[8,2,3,2048]{3,1,2,0:T(2,128)S(1)} %get-tuple-element.10), channel_id=1, source_target_pairs={{0,504},{8,0},{16,8},{24,16},{32,24},{40,32},{48,40},{56,48},{64,5... | collective-permute-start | bytes 1179656 | tf_op jit(solution)/shard_map/ppermute | solution.py:32
  60.6 14.1 %collective-permute-start.3 = (f32[8,2,3,2048]{3,1,2,0:T(2,128)S(1)}, f32[8,2,3,2048]{3,1,2,0:T(2,128)S(1)}, u32[]{:S(2)}, u32[]{:S(2)}) collective-permute-start(f32[8,2,3,2048]{3,1,2,0:T(2,128)S(1)} %get-tuple-element.11), channel_id=1, source_target_pairs={{0,8},{8,16},{16,24},{24,32},{32,40},{40,48},{48,56},{56,64},{64,7... | collective-permute-start | bytes 1179656 | tf_op jit(solution)/shard_map/ppermute | solution.py:32
  75.9 14.8 %all-to-all-start = ((f32[8,2,3,2048]{3,1,2,0:T(2,128)}), f32[8,2,3,2048]{3,1,2,0:T(2,128)S(1)}, u32[]{:S(2)}, u32[]{:S(2)}) async-start(f32[8,2,3,2048]{3,1,2,0:T(2,128)} %fusion), calls=%async_computation | async-start | bytes 786432 | tf_op jit(solution)/shard_map/all_to_all | solution.py:239
  103.8 15.0 %collective-permute-start.4 = (f32[2,3,128,128]{3,2,1,0:T(8,128)S(1)}, f32[2,3,128,128]{3,2,1,0:T(8,128)S(1)}, u32[]{:S(2)}, u32[]{:S(2)}) collective-permute-start(f32[2,3,128,128]{3,2,1,0:T(8,128)S(1)} %reshape_reshape.7), channel_id=1, source_target_pairs={{0,8},{8,16},{16,24},{24,32},{32,40},{40,48},{48,56},{56,64},{64,7... | collective-permute-start | bytes 1179656 | tf_op jit(solution)/shard_map/ppermute | solution.py:22
  105.8 14.0 %collective-permute-start.5 = (f32[2,3,128,128]{3,2,1,0:T(8,128)S(1)}, f32[2,3,128,128]{3,2,1,0:T(8,128)S(1)}, u32[]{:S(2)}, u32[]{:S(2)}) collective-permute-start(f32[2,3,128,128]{3,2,1,0:T(8,128)S(1)} %reshape_reshape.7), channel_id=1, source_target_pairs={{8,0},{16,8},{24,16},{32,24},{40,32},{48,40},{56,48},{64,56},{72,6... | collective-permute-start | bytes 1179656 | tf_op jit(solution)/shard_map/ppermute | solution.py:25
  164.5 1.0 copy-start
  164.8 1.7 copy-start.2
  164.8 1.7 copy-start.3

commit v11 on v10

--- a/solution.py
+++ b/solution.py
@@ -168,7 +168,7 @@
 
     curve = lax.fori_loop(0, slot_ref.shape[0], body, jnp.zeros(cos_ref.shape[1:], jnp.float32)[None])
     curve_sum = jnp.sum(curve, axis=1, keepdims=True)
-    lane = lax.broadcasted_iota(jnp.int32, totals_ref.shape, 1)
+    lane = lax.broadcasted_iota(jnp.int32, totals_ref.shape, 2)
     totals_ref[...] = jnp.where(lane == 0, slope_ref[0], jnp.where(lane == 1, curve_sum, 0.0))
 
 
@@ -196,7 +196,7 @@
     )(local_ids, weights, win, slot, pix, cos_two, sin_two, ts)
 
 
-def scan_call(local_ids, weights, slope, win, slot, pix, cos_two, sin_two):
+def scan_call(local_ids, weights, slope, win, slot, pix, cos_two, sin_two, copies):
     hits = local_ids.shape[0]
     smem = pl.BlockSpec(memory_space=pltpu.SMEM)
     vmem = pl.BlockSpec(memory_space=VMEM)
@@ -204,7 +204,7 @@
         scan_kernel,
         out_shape=(
             jax.ShapeDtypeStruct(slot.shape, jnp.float32),
-            jax.ShapeDtypeStruct((1, SIDE), jnp.float32),
+            jax.ShapeDtypeStruct((copies, 1, SIDE), jnp.float32),
         ),
         in_specs=[smem] * 3 + [vmem] * 5,
         out_specs=(vmem, vmem),
@@ -246,9 +246,11 @@
     direction = collect(dir_share, WAFER, 2)
     dir_window = with_halo(as_grid(direction), ((TM, 0),), tiles_dev)
     rescanned, parts = scan_call(
-        local_ids, weights, slope_part.reshape(1), dir_window, slot, pix, cos_two, sin_two
+        local_ids, weights, slope_part.reshape(1), dir_window, slot, pix, cos_two, sin_two,
+        lax.axis_size(WAFER),
     )
-    totals = summed_by_exchange(summed_by_exchange(parts, WAFER), TM)
+    wafer_sum = jnp.sum(lax.all_to_all(parts, WAFER, 0, 0, tiled=True), axis=0)
+    totals = summed_by_exchange(wafer_sum, TM)
     step_size = totals[0, 0] / totals[0, 1]
     new_map = sky_map + step_size * direction
     new_residual = (resid - step_size * rescanned)[None]

time: 168 us -> 168 us (level)
    all_to_all x0 -> x1, blocking collectives: none -> 9.73 us  [local(): wafer_sum = jnp.sum(lax.all_to_all(parts, WAFER, 0, 0, tiled=True), axis=0)]
    all_to_all x3 -> x2, blocking collectives: 41.5 us -> 32.6 us  [copy_for_each(): return lax.all_to_all(copies, axis, split_axis=0, concat_axis=0, tiled=True)]
where the time goes in v11:
time: 168 us; the launch traced here: 167 us
  blocking collectives  42.3 us (25%)
  starting transfers between devices  41.1 us (24%)
  Pallas kernels  34.8 us (21%)
  waiting for transfers between devices  32.8 us (20%)
  other arithmetic  7.42 us (4%)
  local copies, waits for them, and re-layouts  6.65 us (4%)
  between operations  2.19 us (1%)
    all_to_all x2, blocking collectives, copy_for_each(): return lax.all_to_all(copies, axis, split_axis=0, concat_axis=0, tiled=True)  32.6 us
    pallas_call x1, Pallas kernels, bin_call(): pl.pallas_call(bin_kernel, out_shape=(jax.ShapeDtypeStruct((dets, samp),...  23.6 us
    ppermute x2, starting transfers between devices, with_halo(): lax.ppermute(lax.slice_in_dim(block, 0, width, axis=dim), axis, backward)  18.4 us
    ppermute x2, waiting for transfers between devices, passed_along(): lax.ppermute(value, axis, [(i, (i + by) % count) for i in range(count)])  12.1 us
    ppermute x2, waiting for transfers between devices, with_halo(): lax.ppermute(lax.slice_in_dim(block, block.shape[dim] - width, None, axis...  12 us
    pallas_call x1, Pallas kernels, scan_call(): pl.pallas_call(scan_kernel, out_shape=(jax.ShapeDtypeStruct(slot.shape, j...  11.2 us
    all_to_all x1, blocking collectives, local(): wafer_sum = jnp.sum(lax.all_to_all(parts, WAFER, 0, 0, tiled=True), axis=0)  9.73 us
    ppermute x2, starting transfers between devices, passed_along(): lax.ppermute(value, axis, [(i, (i + by) % count) for i in range(count)])  9.35 us
  transfers between devices with their start and end apart: 7, of which 7 were waited for; matrix products, arithmetic and copies ran while one was open for 1% of the time, Pallas kernels for 0%

profile of v11, /device:TPU:1, one launch (start us, length us, event | category | flops | bytes accessed | tf_op | source)
XLA Modules:
  0.0 167.3 jit_solution(11501365237536102630)
XLA Ops:
  0.6 0.0 copy-start.4
  0.6 0.0 copy-start.1
  0.6 1.3 reshape.24
  2.0 4.4 %collective-permute-start = (f32[2,3,128,128]{3,2,1,0:T(8,128)S(1)}, f32[2,3,128,128]{3,2,1,0:T(8,128)S(1)}, u32[]{:S(2)}, u32[]{:S(2)}) collective-permute-start(f32[2,3,128,128]{3,2,1,0:T(8,128)S(1)} %copy.61), channel_id=1, source_target_pairs={{0,8},{8,16},{16,24},{24,32},{32,40},{40,48},{48,56},{56,64},{64,7... | collective-permute-start | bytes 1179656 | tf_op jit(solution)/shard_map/ppermute | solution.py:22
  6.4 11.7 %collective-permute-start.1 = (f32[2,3,128,128]{3,2,1,0:T(8,128)S(1)}, f32[2,3,128,128]{3,2,1,0:T(8,128)S(1)}, u32[]{:S(2)}, u32[]{:S(2)}) collective-permute-start(f32[2,3,128,128]{3,2,1,0:T(8,128)S(1)} %copy.61), channel_id=1, source_target_pairs={{8,0},{16,8},{24,16},{32,24},{40,32},{48,40},{56,48},{64,56},{72,6... | collective-permute-start | bytes 1179656 | tf_op jit(solution)/shard_map/ppermute | solution.py:25
  18.1 0.0 copy-done.4
  18.1 0.5 and_select_fusion.ids_ref
  18.6 0.0 copy-done.1
  18.6 0.7 sine_bitcast_fusion
  19.4 5.6 %collective-permute-done = f32[2,3,128,128]{3,2,1,0:T(8,128)S(1)} collective-permute-done((f32[2,3,128,128]{3,2,1,0:T(8,128)S(1)}, f32[2,3,128,128]{3,2,1,0:T(8,128)S(1)}, u32[]{:S(2)}, u32[]{:S(2)}) %collective-permute-start) | collective-permute-done | bytes 393248 | tf_op jit(solution)/shard_map/ppermute | solution.py:22
  25.0 0.9 collective-permute-done.1
  25.9 1.1 pad_maximum_fusion.win_ref
  27.0 23.6 %shard_map.95 = (f32[8,1024]{1,0:T(8,128)}, f32[6,3,128,128]{3,2,1,0:T(8,128)}) custom-call(s32[4]{0:T(128)} %and_select_fusion.ids_ref, f32[8]{0:T(128)} %bitcast.44, f32[6,3,128,128]{3,2,1,0:T(8,128)} %pad_maximum_fusion.win_ref, s32[8,1024]{1,0:T(8,128)} %bitcast.37, s32[8,1024]{1,0:T(8,128)} %bitcast.39, f32[8,1024]{1,0:T(8,128)} %get-tuple-element.24.cos_ref, ...), custom_call_target="tpu_custom_call" | custom-call | tf_op jit(solution)/shard_map/pallas_call | solution.py:183
  50.6 1.5 reshape_reshape.6
  52.1 0.7 copy.105
  52.8 0.4 fusion.7
  53.2 7.4 %collective-permute-start.2 = (f32[8,2,3,2048]{3,1,2,0:T(2,128)S(1)}, f32[8,2,3,2048]{3,1,2,0:T(2,128)S(1)}, u32[]{:S(2)}, u32[]{:S(2)}) collective-permute-start(f32[8,2,3,2048]{3,1,2,0:T(2,128)S(1)} %get-tuple-element.10), channel_id=1, source_target_pairs={{0,504},{8,0},{16,8},{24,16},{32,24},{40,32},{48,40},{56,48},{64,5... | collective-permute-start | bytes 1179656 | tf_op jit(solution)/shard_map/ppermute | solution.py:32
  60.6 1.9 %collective-permute-start.3 = (f32[8,2,3,2048]{3,1,2,0:T(2,128)S(1)}, f32[8,2,3,2048]{3,1,2,0:T(2,128)S(1)}, u32[]{:S(2)}, u32[]{:S(2)}) collective-permute-start(f32[8,2,3,2048]{3,1,2,0:T(2,128)S(1)} %get-tuple-element.11), channel_id=1, source_target_pairs={{0,8},{8,16},{16,24},{24,32},{32,40},{40,48},{48,56},{56,64},{64,7... | collective-permute-start | bytes 1179656 | tf_op jit(solution)/shard_map/ppermute | solution.py:32
  62.6 5.0 %collective-permute-done.2 = f32[8,2,3,2048]{3,1,2,0:T(2,128)S(1)} collective-permute-done((f32[8,2,3,2048]{3,1,2,0:T(2,128)S(1)}, f32[8,2,3,2048]{3,1,2,0:T(2,128)S(1)}, u32[]{:S(2)}, u32[]{:S(2)}) %collective-permute-start.2) | collective-permute-done | bytes 393248 | tf_op jit(solution)/shard_map/ppermute | solution.py:32
  67.6 7.2 %collective-permute-done.3 = f32[8,2,3,2048]{3,1,2,0:T(2,128)S(1)} collective-permute-done((f32[8,2,3,2048]{3,1,2,0:T(2,128)S(1)}, f32[8,2,3,2048]{3,1,2,0:T(2,128)S(1)}, u32[]{:S(2)}, u32[]{:S(2)}) %collective-permute-start.3) | collective-permute-done | bytes 393248 | tf_op jit(solution)/shard_map/ppermute | solution.py:32
  74.7 1.1 fusion
  75.9 7.1 %all-to-all-start = ((f32[8,2,3,2048]{3,1,2,0:T(2,128)}), f32[8,2,3,2048]{3,1,2,0:T(2,128)S(1)}, u32[]{:S(2)}, u32[]{:S(2)}) async-start(f32[8,2,3,2048]{3,1,2,0:T(2,128)} %fusion), calls=%async_computation | async-start | bytes 786432 | tf_op jit(solution)/shard_map/all_to_all | solution.py:239
  83.0 0.8 constant_dynamic-slice_fusion.4
  83.8 6.9 %all-to-all-done = f32[8,2,3,2048]{3,1,2,0:T(2,128)S(1)} async-done(((f32[8,2,3,2048]{3,1,2,0:T(2,128)}), f32[8,2,3,2048]{3,1,2,0:T(2,128)S(1)}, u32[]{:S(2)}, u32[]{:S(2)}) %all-to-all-start) | async-done | bytes 393248 | tf_op jit(solution)/shard_map/all_to_all | solution.py:239
  90.7 0.1 reduce_sum.38
  90.9 0.1 fusion.5
  91.0 0.7 pad_maximum_fusion.2
  91.7 0.2 broadcast_in_dim.9
  91.9 11.7 %all_to_all.20 = f32[8,2,3,2048]{3,1,2,0:T(2,128)S(1)} all-to-all(f32[8,2,3,2048]{3,1,2,0:T(2,128)S(1)} %broadcast_in_dim.9), channel_id=1, replica_groups=mesh['tm_0'=4,'tm_hi'=4,'tm_lo'=4,'wafer_0'=4,'wafer_1'=2] {'wafer_0','w..., dimensions={0} | all-to-all | bytes 786432 | tf_op jit(solution)/shard_map/all_to_all | solution.py:55
  103.6 0.2 copy.106
  103.8 0.1 reshape_reshape.7
  103.9 1.9 %collective-permute-start.4 = (f32[2,3,128,128]{3,2,1,0:T(8,128)S(1)}, f32[2,3,128,128]{3,2,1,0:T(8,128)S(1)}, u32[]{:S(2)}, u32[]{:S(2)}) collective-permute-start(f32[2,3,128,128]{3,2,1,0:T(8,128)S(1)} %reshape_reshape.7), channel_id=1, source_target_pairs={{0,8},{8,16},{16,24},{24,32},{32,40},{40,48},{48,56},{56,64},{64,7... | collective-permute-start | bytes 1179656 | tf_op jit(solution)/shard_map/ppermute | solution.py:22
  105.8 6.7 %collective-permute-start.5 = (f32[2,3,128,128]{3,2,1,0:T(8,128)S(1)}, f32[2,3,128,128]{3,2,1,0:T(8,128)S(1)}, u32[]{:S(2)}, u32[]{:S(2)}) collective-permute-start(f32[2,3,128,128]{3,2,1,0:T(8,128)S(1)} %reshape_reshape.7), channel_id=1, source_target_pairs={{8,0},{16,8},{24,16},{32,24},{40,32},{48,40},{56,48},{64,56},{72,6... | collective-permute-start | bytes 1179656 | tf_op jit(solution)/shard_map/ppermute | solution.py:25
  112.5 6.4 %collective-permute-done.4 = f32[2,3,128,128]{3,2,1,0:T(8,128)S(1)} collective-permute-done((f32[2,3,128,128]{3,2,1,0:T(8,128)S(1)}, f32[2,3,128,128]{3,2,1,0:T(8,128)S(1)}, u32[]{:S(2)}, u32[]{:S(2)}) %collective-permute-start.4) | collective-permute-done | bytes 393248 | tf_op jit(solution)/shard_map/ppermute | solution.py:22
  118.9 0.9 collective-permute-done.5
  119.8 1.1 pad_maximum_fusion.1.win_ref
  120.9 11.2 %shard_map.96 = (f32[8,1024]{1,0:T(8,128)}, f32[8,1,128]{2,1,0:T(1,128)}) custom-call(s32[4]{0:T(128)} %and_select_fusion.ids_ref, f32[8]{0:T(128)} %bitcast.45, f32[1]{0:T(128)} %bitcast.8.slope_ref, f32[6,3,128,128]{3,2,1,0:T(8,128)} %pad_maximum_fusion.1.win_ref, s32[8,1024]{1,0:T(8,128)} %bitcast.38, s32[8,1024]{1,0:T(8,128)} %bitcast.40, ...), custom_call_target="tpu_custom_call" | custom-call | tf_op jit(solution)/shard_map/pallas_call | solution.py:203
  132.1 9.7 %all_to_all.21 = f32[8,1,128]{2,1,0:T(1,128)S(1)} all-to-all(f32[8,1,128]{2,1,0:T(1,128)} %get-tuple-element.7), channel_id=1, replica_groups=mesh['tm_0'=4,'tm_hi'=4,'tm_lo'=4,'wafer_0'=4,'wafer_1'=2] {'wafer_0','w..., dimensions={0} | all-to-all | bytes 8192 | tf_op jit(solution)/shard_map/all_to_all | solution.py:252
  141.9 20.9 %all_to_all.22 = f32[64,1,128]{2,1,0:T(1,128)S(1)} all-to-all(f32[64,1,128]{2,1,0:T(1,128)S(1)} %broadcast_in_dim.10), channel_id=1, replica_groups=mesh['tm_0'=4,'tm_hi'=4,'tm_lo'=4,'wafer_0'=4,'wafer_1'=2] {'tm_0','tm_h..., dimensions={0} | all-to-all | bytes 65536 | tf_op jit(solution)/shard_map/all_to_all | solution.py:55
  162.8 0.6 fusion.8
  164.7 0.0 copy-start
  164.8 0.2 broadcast_multiply_fusion
  165.0 0.0 copy-start.2
  165.0 0.0 copy-start.3
  165.1 0.3 mul.95
  165.4 0.4 copy-done
  165.7 0.9 add.65
  166.7 0.0 copy-done.2
  166.7 0.0 copy-done.3
  166.7 0.6 subtract_bitcast_fusion
  (7 shorter events, 0.2 us)
Async XLA Ops:
  0.6 17.5 %copy-start.4 = (s32[1,4]{1,0:T(1,128)S(1)}, s32[1,4]{1,0:T(1,128)}, u32[]{:S(2)}) copy-start(s32[1,4]{1,0:T(1,128)} %param.13) | copy-start | bytes 52
  0.6 18.0 %copy-start.1 = (f32[1,8,1024]{2,1,0:T(8,128)S(1)}, f32[1,8,1024]{2,1,0:T(8,128)}, u32[]{:S(2)}) copy-start(f32[1,8,1024]{2,1,0:T(8,128)} %param.12) | copy-start | bytes 98308
  2.0 22.9 %collective-permute-start = (f32[2,3,128,128]{3,2,1,0:T(8,128)S(1)}, f32[2,3,128,128]{3,2,1,0:T(8,128)S(1)}, u32[]{:S(2)}, u32[]{:S(2)}) collective-permute-start(f32[2,3,128,128]{3,2,1,0:T(8,128)S(1)} %copy.61), channel_id=1, source_target_pairs={{0,8},{8,16},{16,24},{24,32},{32,40},{40,48},{48,56},{56,64},{64,7... | collective-permute-start | bytes 1179656 | tf_op jit(solution)/shard_map/ppermute | solution.py:22
  6.4 19.5 %collective-permute-start.1 = (f32[2,3,128,128]{3,2,1,0:T(8,128)S(1)}, f32[2,3,128,128]{3,2,1,0:T(8,128)S(1)}, u32[]{:S(2)}, u32[]{:S(2)}) collective-permute-start(f32[2,3,128,128]{3,2,1,0:T(8,128)S(1)} %copy.61), channel_id=1, source_target_pairs={{8,0},{16,8},{24,16},{32,24},{40,32},{48,40},{56,48},{64,56},{72,6... | collective-permute-start | bytes 1179656 | tf_op jit(solution)/shard_map/ppermute | solution.py:25
  53.2 14.4 %collective-permute-start.2 = (f32[8,2,3,2048]{3,1,2,0:T(2,128)S(1)}, f32[8,2,3,2048]{3,1,2,0:T(2,128)S(1)}, u32[]{:S(2)}, u32[]{:S(2)}) collective-permute-start(f32[8,2,3,2048]{3,1,2,0:T(2,128)S(1)} %get-tuple-element.10), channel_id=1, source_target_pairs={{0,504},{8,0},{16,8},{24,16},{32,24},{40,32},{48,40},{56,48},{64,5... | collective-permute-start | bytes 1179656 | tf_op jit(solution)/shard_map/ppermute | solution.py:32
  60.6 14.1 %collective-permute-start.3 = (f32[8,2,3,2048]{3,1,2,0:T(2,128)S(1)}, f32[8,2,3,2048]{3,1,2,0:T(2,128)S(1)}, u32[]{:S(2)}, u32[]{:S(2)}) collective-permute-start(f32[8,2,3,2048]{3,1,2,0:T(2,128)S(1)} %get-tuple-element.11), channel_id=1, source_target_pairs={{0,8},{8,16},{16,24},{24,32},{32,40},{40,48},{48,56},{56,64},{64,7... | collective-permute-start | bytes 1179656 | tf_op jit(solution)/shard_map/ppermute | solution.py:32
  75.9 14.8 %all-to-all-start = ((f32[8,2,3,2048]{3,1,2,0:T(2,128)}), f32[8,2,3,2048]{3,1,2,0:T(2,128)S(1)}, u32[]{:S(2)}, u32[]{:S(2)}) async-start(f32[8,2,3,2048]{3,1,2,0:T(2,128)} %fusion), calls=%async_computation | async-start | bytes 786432 | tf_op jit(solution)/shard_map/all_to_all | solution.py:239
  103.9 15.0 %collective-permute-start.4 = (f32[2,3,128,128]{3,2,1,0:T(8,128)S(1)}, f32[2,3,128,128]{3,2,1,0:T(8,128)S(1)}, u32[]{:S(2)}, u32[]{:S(2)}) collective-permute-start(f32[2,3,128,128]{3,2,1,0:T(8,128)S(1)} %reshape_reshape.7), channel_id=1, source_target_pairs={{0,8},{8,16},{16,24},{24,32},{32,40},{40,48},{48,56},{56,64},{64,7... | collective-permute-start | bytes 1179656 | tf_op jit(solution)/shard_map/ppermute | solution.py:22
  105.8 14.0 %collective-permute-start.5 = (f32[2,3,128,128]{3,2,1,0:T(8,128)S(1)}, f32[2,3,128,128]{3,2,1,0:T(8,128)S(1)}, u32[]{:S(2)}, u32[]{:S(2)}) collective-permute-start(f32[2,3,128,128]{3,2,1,0:T(8,128)S(1)} %reshape_reshape.7), channel_id=1, source_target_pairs={{8,0},{16,8},{24,16},{32,24},{40,32},{48,40},{56,48},{64,56},{72,6... | collective-permute-start | bytes 1179656 | tf_op jit(solution)/shard_map/ppermute | solution.py:25
  164.7 1.0 copy-start
  165.0 1.7 copy-start.2
  165.0 1.7 copy-start.3
